TPU v7x, 256 devices: a whole 4x4x8 slice. The times are simulated.
256 devices in a mesh: row: 8 (over x_lo, y), col: 32 (over z, x_hi, core).
Axes of the slice: x: 4 (x_hi: 2, x_lo: 2; x = x_hi * 2 + x_lo), y: 4, z: 8, core: 2. Of those that a mesh axis runs over, the one named last changes fastest.
Arguments:
- frames: bfloat16 [1024, 8192], P('col', 'row'), may hold values from -6 to 6
- cotangent: bfloat16 [1024, 8192], P('col', 'row'), may hold values from -6 to 6
- gate_weight: bfloat16 [8192, 14336], P('row', 'col'), may hold values from -0.0625 to 0.0625
- up_weight: bfloat16 [8192, 14336], P('row', 'col'), may hold values from -0.0625 to 0.0625
- down_weight: bfloat16 [14336, 8192], P('col', 'row'), may hold values from -0.046875 to 0.046875
- utt_ids: int32 [1024], replicated, may hold values from 0 to 15, never falling along the last dimension, each value on 1 to 128 neighbouring positions
- valid_len: int32 [16], replicated, may hold values from 1 to 128
- time_start: int32 [16], replicated, may hold values from 0 to 127
- time_width: int32 [16], replicated, may hold values from 0 to 32
- freq_start: int32 [16], replicated, may hold values from 0 to 8191
- freq_width: int32 [16], replicated, may hold values from 0 to 2048
Outputs:
- output: bfloat16 [1024, 8192], P('col', 'row')
- grad_frames: bfloat16 [1024, 8192], P('col', 'row')
- grad_gate: bfloat16 [8192, 14336], P('row', 'col')
- grad_up: bfloat16 [8192, 14336], P('row', 'col')
- grad_down: bfloat16 [14336, 8192], P('col', 'row')
Inputs may be any that keep to these rules, and one draw needn't show every extreme that they name: `utt_ids`: token ids never fall along the tokens; each utterance holds 1 to 128 tokens.
All inputs are finite; a program needn't handle non-finite values.
Results may differ from a plain program's by a relative error of at most 0.025.
Values may be sent and summed in bfloat16 or wider, within the bound.
No kernel may reach another device: no remote copies, remote signals or barrier semaphores. Data moves between devices by JAX's collectives and lax.ppermute only.
A program may use at most 64 MiB of HBM per device.

v0:
```python
import jax
import jax.numpy as jnp
from jax import lax
from jax.sharding import PartitionSpec as P


def span_masks(
    utt_ids,
    local_ids,
    tok_index,
    feat_index,
    valid_len,
    time_start,
    time_width,
    freq_start,
    freq_width,
):
    utt_index = jnp.arange(valid_len.shape[0], dtype=jnp.int32)
    starts = jnp.sum((utt_ids[None, :] < utt_index[:, None]).astype(jnp.int32), axis=1)
    member = (local_ids[:, None] == utt_index[None, :]).astype(jnp.int32)

    def lookup(table):
        return jnp.sum(member * table[None, :], axis=1)

    position = tok_index - lookup(starts)
    valid_rows = position < lookup(valid_len)
    time_low = lookup(time_start)
    in_time = (position >= time_low) & (position < time_low + lookup(time_width))
    freq_low = lookup(freq_start)[:, None]
    freq_high = freq_low + lookup(freq_width)[:, None]
    in_freq = (feat_index[None, :] >= freq_low) & (feat_index[None, :] < freq_high)
    keep_mask = (valid_rows & jnp.logical_not(in_time))[:, None] & jnp.logical_not(in_freq)
    return (keep_mask, valid_rows)


def shards(
    frames,
    cotangent,
    gate_weight,
    up_weight,
    down_weight,
    utt_ids,
    valid_len,
    time_start,
    time_width,
    freq_start,
    freq_width,
):
    tok_rows, feat_cols = frames.shape
    hidden_cols = gate_weight.shape[1]
    first_tok = lax.axis_index("col") * tok_rows
    first_feat = lax.axis_index("row") * feat_cols
    tok_index = first_tok + jnp.arange(tok_rows, dtype=jnp.int32)
    feat_index = first_feat + jnp.arange(feat_cols, dtype=jnp.int32)
    local_ids = lax.dynamic_slice_in_dim(utt_ids, first_tok, tok_rows)
    keep_mask, valid_rows = span_masks(
        utt_ids,
        local_ids,
        tok_index,
        feat_index,
        valid_len,
        time_start,
        time_width,
        freq_start,
        freq_width,
    )
    masked = jnp.where(keep_mask, frames, jnp.zeros_like(frames))
    cot_valid = jnp.where(valid_rows[:, None], cotangent, jnp.zeros_like(cotangent))
    contract_last = (((1,), (1,)), ((), ()))
    contract_first = (((0,), (0,)), ((), ()))
    tokens_all = lax.all_gather(masked, "col", axis=0, tiled=True)
    block = tokens_all
    gate_up = lax.psum_scatter(
        jnp.concatenate(
            [
                jnp.dot(block, gate_weight, preferred_element_type=jnp.float32),
                jnp.dot(block, up_weight, preferred_element_type=jnp.float32),
            ],
            axis=1,
        ).astype(jnp.bfloat16),
        "row",
        scatter_dimension=0,
        tiled=True,
    ).astype(jnp.float32)
    gate = gate_up[:, :hidden_cols]
    up = gate_up[:, hidden_cols:]
    sigmoid_gate = jax.nn.sigmoid(gate)
    hidden = (gate * sigmoid_gate * up).astype(jnp.bfloat16)
    hidden_all = lax.all_gather(hidden, "row", axis=0, tiled=True)
    block = hidden_all
    output = lax.psum_scatter(
        jnp.dot(block, down_weight, preferred_element_type=jnp.float32).astype(jnp.bfloat16),
        "col",
        scatter_dimension=0,
        tiled=True,
    )
    cot_all = lax.all_gather(cot_valid, "col", axis=0, tiled=True)
    block = cot_all
    grad_hidden = lax.psum_scatter(
        lax.dot_general(
            block, down_weight, contract_last, preferred_element_type=jnp.float32
        ).astype(jnp.bfloat16),
        "row",
        scatter_dimension=0,
        tiled=True,
    ).astype(jnp.float32)
    dgate = (grad_hidden * up * sigmoid_gate * (1.0 + gate * (1.0 - sigmoid_gate))).astype(
        jnp.bfloat16
    )
    dup = (grad_hidden * gate * sigmoid_gate).astype(jnp.bfloat16)
    dgate_all, dup_all = (
        lax.all_gather(dgate, "row", axis=0, tiled=True),
        lax.all_gather(dup, "row", axis=0, tiled=True),
    )
    grad_down = lax.dot_general(
        hidden_all, cot_all, contract_first, preferred_element_type=jnp.float32
    ).astype(jnp.bfloat16)
    grad_gate = lax.dot_general(
        tokens_all, dgate_all, contract_first, preferred_element_type=jnp.float32
    ).astype(jnp.bfloat16)
    grad_up = lax.dot_general(
        tokens_all, dup_all, contract_first, preferred_element_type=jnp.float32
    ).astype(jnp.bfloat16)
    grad_masked = lax.psum_scatter(
        (
            lax.dot_general(
                dgate_all, gate_weight, contract_last, preferred_element_type=jnp.float32
            )
            + lax.dot_general(dup_all, up_weight, contract_last, preferred_element_type=jnp.float32)
        ).astype(jnp.bfloat16),
        "col",
        scatter_dimension=0,
        tiled=True,
    ).astype(jnp.float32)
    grad_frames = jnp.where(keep_mask, grad_masked, jnp.zeros_like(grad_masked)).astype(
        jnp.bfloat16
    )
    return (output, grad_frames, grad_gate, grad_up, grad_down)


def solution(mesh):
    placed = (
        P("col", "row"),
        P("col", "row"),
        P("row", "col"),
        P("row", "col"),
        P("col", "row"),
        P(),
        P(),
        P(),
        P(),
        P(),
        P(),
    )
    return jax.shard_map(
        shards,
        mesh=mesh,
        in_specs=placed,
        out_specs=(
            P("col", "row"),
            P("col", "row"),
            P("row", "col"),
            P("row", "col"),
            P("col", "row"),
        ),
        check_vma=False,
    )
```

profile of v0, /device:TPU:1, one launch (start us, length us, event | category | flops | bytes accessed | tf_op | source)
XLA Modules:
  0.0 565.4 jit_solution(14889428391263606232)
XLA Ops:
  7.2 0.0 copy-start
  7.2 0.0 all-gather.5.cloned.1.call-start
  7.2 0.9 convert_reduce_fusion
  8.1 0.8 dynamic_slice.3
  8.9 0.8 select_reduce_fusion.4
  9.7 1.5 broadcast_select_fusion
  11.3 0.0 all-gather.5.cloned.1.call-update
  11.3 0.0 all-gather.3.cloned.1.call-start
  11.4 1.6 broadcast_select_fusion.1
  12.9 0.0 all-gather.3.cloned.1.call-update
  13.0 0.0 reduce-scatter.15.cloned.1.call-start
  13.0 82.5 %all-gather.5.cloned.1.call-done = bf16[1024,1024]{1,0:T(8,128)(2,1)} async-done(((bf16[32,1024]{1,0:T(8,128)(2,1)}), bf16[1024,1024]{1,0:T(8,128)(2,1)}) %all-gather.5.cloned.1.call-update) | async-done | bytes 2097168 | tf_op jit(solution)/shard_map/all_gather | solution.py:97
  95.5 3.0 convolution_convert_fusion.4
  98.4 0.0 copy-start.2
  98.4 1.3 copy.18
  99.8 0.0 reduce-scatter.15.cloned.1.call-update
  99.8 0.0 reduce-scatter.13.cloned.1.call-start
  99.8 75.4 %all-gather.3.cloned.1.call-done = bf16[1024,1024]{1,0:T(8,128)(2,1)} async-done(((bf16[32,1024]{1,0:T(8,128)(2,1)}), bf16[1024,1024]{1,0:T(8,128)(2,1)}) %all-gather.3.cloned.1.call-update) | async-done | bytes 2097168 | tf_op jit(solution)/shard_map/all_gather | solution.py:71
  175.2 0.0 copy-done.2
  175.2 2.9 convolution_convert_fusion.5
  178.1 0.0 copy-done
  178.1 1.2 convolution_convert_fusion.6
  179.3 0.1 pad_maximum_fusion
  179.5 2.5 copy.16
  182.0 0.0 reduce-scatter.13.cloned.1.call-update
  182.0 0.0 reduce-scatter.11.cloned.1.call-start
  182.0 28.8 %reduce-scatter.15.cloned.1.call-done = bf16[128,448]{1,0:T(8,128)(2,1)} async-done(((bf16[1024,448]{1,0:T(8,128)(2,1)}), bf16[128,448]{1,0:T(8,128)(2,1)}) %reduce-scatter.15.cloned.1.call-update) | async-done | bytes 114704
  210.9 1.0 copy.19
  211.9 44.5 %reduce-scatter.13.cloned.1.call-done = bf16[128,896]{1,0:T(8,128)(2,1)} async-done(((bf16[1024,896]{1,0:T(8,128)(2,1)}), bf16[128,896]{1,0:T(8,128)(2,1)}) %reduce-scatter.13.cloned.1.call-update) | async-done | bytes 229392
  256.5 1.1 copy.17
  257.6 0.2 fusion.4
  257.8 23.0 %all_gather.19 = bf16[1024,448]{0,1:T(8,128)(2,1)S(1)} all-gather(bf16[128,448]{0,1:T(8,128)(2,1)S(1)} %get-tuple-element.11), channel_id=1, replica_groups=mesh['row'=8,'col'=32] {'row'}, dimensions={0}, use_global_device_ids=true | all-gather | bytes 1032192 | tf_op jit(solution)/shard_map/all_gather | solution.py:113
  280.7 23.3 %all_gather.18 = bf16[1024,448]{0,1:T(8,128)(2,1)S(1)} all-gather(bf16[128,448]{0,1:T(8,128)(2,1)S(1)} %get-tuple-element.12), channel_id=1, replica_groups=mesh['row'=8,'col'=32] {'row'}, dimensions={0}, use_global_device_ids=true | all-gather | bytes 1032192 | tf_op jit(solution)/shard_map/all_gather | solution.py:112
  304.0 1.3 fusion.6
  305.4 2.7 add_convert_fusion
  308.1 0.0 reduce-scatter.11.cloned.1.call-update
  308.1 0.0 reduce-scatter.9.cloned.1.call-start
  308.2 23.0 %all_gather.16 = bf16[1024,448]{0,1:T(8,128)(2,1)S(1)} all-gather(bf16[128,448]{0,1:T(8,128)(2,1)S(1)} %get-tuple-element.13), channel_id=1, replica_groups=mesh['row'=8,'col'=32] {'row'}, dimensions={0}, use_global_device_ids=true | all-gather | bytes 1032192 | tf_op jit(solution)/shard_map/all_gather | solution.py:89
  331.1 0.9 copy-done.1
  332.1 3.8 convolution_convert_fusion
  335.9 0.0 reduce-scatter.9.cloned.1.call-update
  335.9 4.1 convolution_convert_fusion.3
  340.0 0.0 copy-done.5
  340.0 2.1 convolution_convert_fusion.2
  342.1 2.1 convolution_convert_fusion.1
  344.1 92.1 %reduce-scatter.11.cloned.1.call-done = bf16[32,1024]{1,0:T(8,128)(2,1)} async-done(((bf16[1024,1024]{1,0:T(8,128)(2,1)}), bf16[32,1024]{1,0:T(8,128)(2,1)}) %reduce-scatter.11.cloned.1.call-update) | async-done | bytes 65552 | tf_op jit(solution)/shard_map/reduce_scatter | solution.py:124
  436.2 1.6 select_convert_fusion
  437.8 120.8 %reduce-scatter.9.cloned.1.call-done = bf16[32,1024]{1,0:T(8,128)(2,1)} async-done(((bf16[1024,1024]{1,0:T(8,128)(2,1)}), bf16[32,1024]{1,0:T(8,128)(2,1)}) %reduce-scatter.9.cloned.1.call-update) | async-done | bytes 65552 | tf_op jit(solution)/shard_map/reduce_scatter | solution.py:91
  (10 shorter events, 0.1 us)
Async XLA Ops:
  7.2 170.9 %copy-start = (bf16[1024,448]{0,1:T(8,128)(2,1)S(1)}, bf16[1024,448]{0,1:T(8,128)(2,1)}, u32[]{:S(2)}) copy-start(bf16[1024,448]{0,1:T(8,128)(2,1)} %param.13) | copy-start | bytes 2752516
  7.2 88.3 %all-gather.5.cloned.1.call-start = ((), (), s32[]{:S(2)}) async-start(), calls=%async_computation.6 | async-start | bytes 2162688 | tf_op jit(solution)/shard_map/all_gather | solution.py:97
  11.3 163.9 %all-gather.3.cloned.1.call-start = ((), (), s32[]{:S(2)}) async-start(), calls=%async_computation.4 | async-start | bytes 2162688 | tf_op jit(solution)/shard_map/all_gather | solution.py:71
  13.0 197.9 %reduce-scatter.15.cloned.1.call-start = ((), (), s32[]{:S(2)}) async-start(), calls=%async_computation.9 | async-start | bytes 1179648
  98.4 76.8 %copy-start.2 = (bf16[1024,448]{0,1:T(8,128)(2,1)S(1)}, bf16[1024,448]{0,1:T(8,128)(2,1)}, u32[]{:S(2)}) copy-start(bf16[1024,448]{0,1:T(8,128)(2,1)} %param.14) | copy-start | bytes 2752516
  99.8 156.7 %reduce-scatter.13.cloned.1.call-start = ((), (), s32[]{:S(2)}) async-start(), calls=%async_computation.8 | async-start | bytes 2064384
  175.2 2.9 copy-start.4
  182.0 254.2 %reduce-scatter.11.cloned.1.call-start = ((), (), s32[]{:S(2)}) async-start(), calls=%async_computation.7 | async-start | bytes 2162688 | tf_op jit(solution)/shard_map/reduce_scatter | solution.py:124
  304.0 1.3 copy-start.3
  308.1 250.4 %reduce-scatter.9.cloned.1.call-start = ((), (), s32[]{:S(2)}) async-start(), calls=%async_computation.5 | async-start | bytes 2162688 | tf_op jit(solution)/shard_map/reduce_scatter | solution.py:91
  331.1 0.9 copy-start.1
  335.9 4.1 copy-start.5
Sparse Core Ops, SparseCore 0:
  11.4 84.0 all-gather.4
  98.8 76.3 all-gather.2
  177.7 33.1 reduce-scatter.14
  213.3 43.0 reduce-scatter.12
  308.2 127.9 reduce-scatter.10
  440.8 117.7 reduce-scatter.8
where the time goes:
time: 570 us; the launch traced here: 565 us
  waiting for transfers between devices  444 us (78%)
  blocking collectives  69.2 us (12%)
  matrix products  23.1 us (4%)
  between operations  14.3 us (3%)
  local copies, waits for them, and re-layouts  7.68 us (1%)
  other arithmetic  6.75 us (1%)
    reduce_scatter x1, waiting for transfers between devices, shards(): lax.psum_scatter(jnp.dot(block, down_weight, preferred_element_type=jnp.f...  121 us
    reduce_scatter x1, waiting for transfers between devices, shards(): lax.psum_scatter((lax.dot_general(dgate_all, gate_weight, contract_last,...  92.1 us
    all_gather x1, waiting for transfers between devices, shards(): cot_all = lax.all_gather(cot_valid, 'col', axis=0, tiled=True)  82.5 us
    all_gather x1, waiting for transfers between devices, shards(): tokens_all = lax.all_gather(masked, 'col', axis=0, tiled=True)  75.4 us
    unnamed x8, waiting for transfers between devices  73.5 us
    all_gather x1, blocking collectives, shards(): lax.all_gather(dgate, 'row', axis=0, tiled=True)  23.3 us
    all_gather x1, blocking collectives, shards(): lax.all_gather(dup, 'row', axis=0, tiled=True)  23 us
    all_gather x1, blocking collectives, shards(): hidden_all = lax.all_gather(hidden, 'row', axis=0, tiled=True)  23 us
  transfers between devices with their start and end apart: 6, of which 6 were waited for; matrix products, arithmetic and copies ran while one was open for 5% of the time, Pallas kernels for 0%

commit v1 on v0

--- a/solution.py
+++ b/solution.py
@@ -68,13 +68,19 @@
     cot_valid = jnp.where(valid_rows[:, None], cotangent, jnp.zeros_like(cotangent))
     contract_last = (((1,), (1,)), ((), ()))
     contract_first = (((0,), (0,)), ((), ()))
-    tokens_all = lax.all_gather(masked, "col", axis=0, tiled=True)
-    block = tokens_all
-    gate_up = lax.psum_scatter(
+    both_all = lax.all_gather(
+        jnp.concatenate([masked, cot_valid], axis=1), "col", axis=0, tiled=True
+    )
+    tokens_all = both_all[:, :feat_cols]
+    cot_all = both_all[:, feat_cols:]
+    sums = lax.psum_scatter(
         jnp.concatenate(
             [
-                jnp.dot(block, gate_weight, preferred_element_type=jnp.float32),
-                jnp.dot(block, up_weight, preferred_element_type=jnp.float32),
+                jnp.dot(tokens_all, gate_weight, preferred_element_type=jnp.float32),
+                jnp.dot(tokens_all, up_weight, preferred_element_type=jnp.float32),
+                lax.dot_general(
+                    cot_all, down_weight, contract_last, preferred_element_type=jnp.float32
+                ),
             ],
             axis=1,
         ).astype(jnp.bfloat16),
@@ -82,36 +88,21 @@
         scatter_dimension=0,
         tiled=True,
     ).astype(jnp.float32)
-    gate = gate_up[:, :hidden_cols]
-    up = gate_up[:, hidden_cols:]
+    gate = sums[:, :hidden_cols]
+    up = sums[:, hidden_cols : 2 * hidden_cols]
+    grad_hidden = sums[:, 2 * hidden_cols :]
     sigmoid_gate = jax.nn.sigmoid(gate)
     hidden = (gate * sigmoid_gate * up).astype(jnp.bfloat16)
-    hidden_all = lax.all_gather(hidden, "row", axis=0, tiled=True)
-    block = hidden_all
-    output = lax.psum_scatter(
-        jnp.dot(block, down_weight, preferred_element_type=jnp.float32).astype(jnp.bfloat16),
-        "col",
-        scatter_dimension=0,
-        tiled=True,
-    )
-    cot_all = lax.all_gather(cot_valid, "col", axis=0, tiled=True)
-    block = cot_all
-    grad_hidden = lax.psum_scatter(
-        lax.dot_general(
-            block, down_weight, contract_last, preferred_element_type=jnp.float32
-        ).astype(jnp.bfloat16),
-        "row",
-        scatter_dimension=0,
-        tiled=True,
-    ).astype(jnp.float32)
     dgate = (grad_hidden * up * sigmoid_gate * (1.0 + gate * (1.0 - sigmoid_gate))).astype(
         jnp.bfloat16
     )
     dup = (grad_hidden * gate * sigmoid_gate).astype(jnp.bfloat16)
-    dgate_all, dup_all = (
-        lax.all_gather(dgate, "row", axis=0, tiled=True),
-        lax.all_gather(dup, "row", axis=0, tiled=True),
+    acts_all = lax.all_gather(
+        jnp.concatenate([hidden, dgate, dup], axis=1), "row", axis=0, tiled=True
     )
+    hidden_all = acts_all[:, :hidden_cols]
+    dgate_all = acts_all[:, hidden_cols : 2 * hidden_cols]
+    dup_all = acts_all[:, 2 * hidden_cols :]
     grad_down = lax.dot_general(
         hidden_all, cot_all, contract_first, preferred_element_type=jnp.float32
     ).astype(jnp.bfloat16)
@@ -121,17 +112,29 @@
     grad_up = lax.dot_general(
         tokens_all, dup_all, contract_first, preferred_element_type=jnp.float32
     ).astype(jnp.bfloat16)
-    grad_masked = lax.psum_scatter(
-        (
-            lax.dot_general(
-                dgate_all, gate_weight, contract_last, preferred_element_type=jnp.float32
-            )
-            + lax.dot_general(dup_all, up_weight, contract_last, preferred_element_type=jnp.float32)
-        ).astype(jnp.bfloat16),
+    out_sums = lax.psum_scatter(
+        jnp.concatenate(
+            [
+                jnp.dot(hidden_all, down_weight, preferred_element_type=jnp.float32).astype(
+                    jnp.bfloat16
+                ),
+                (
+                    lax.dot_general(
+                        dgate_all, gate_weight, contract_last, preferred_element_type=jnp.float32
+                    )
+                    + lax.dot_general(
+                        dup_all, up_weight, contract_last, preferred_element_type=jnp.float32
+                    )
+                ).astype(jnp.bfloat16),
+            ],
+            axis=1,
+        ),
         "col",
         scatter_dimension=0,
         tiled=True,
-    ).astype(jnp.float32)
+    )
+    output = out_sums[:, :feat_cols]
+    grad_masked = out_sums[:, feat_cols:].astype(jnp.float32)
     grad_frames = jnp.where(keep_mask, grad_masked, jnp.zeros_like(grad_masked)).astype(
         jnp.bfloat16
     )

time: 570 us -> 368 us (0.65)
  waiting for transfers between devices: 444 us -> 304 us
  blocking collectives: 69.2 us -> 0 us
  local copies, waits for them, and re-layouts: 7.68 us -> 17.7 us
    reduce_scatter x2 -> x0, waiting for transfers between devices: 213 us -> none  [the longest x1 121 us: shards(): lax.psum_scatter(jnp.dot(block, down_weight, preferred_element_type=jnp.f...]
    unnamed x8 -> x6, waiting for transfers between devices: 73.5 us -> 161 us
    all_gather x3 -> x0, blocking collectives: 69.2 us -> none  [the longest x1 23.3 us: shards(): lax.all_gather(dgate, 'row', axis=0, tiled=True)]
    all_gather x2, waiting for transfers between devices: 158 us -> 143 us  [the longest x1 90.9 us: shards(): lax.all_gather(jnp.concatenate([masked, cot_valid], axis=1), 'col', axis=...]
    unnamed x16 -> x23, local copies, waits for them, and re-layouts: 6.92 us -> 15.2 us
  transfers between devices with their start and end apart: 6 -> 4, of which waited for: 6 -> 4; matrix products, arithmetic and copies ran while one was open for 5% -> 2% of each run, Pallas kernels for 0% -> 0%
where the time goes in v1:
time: 368 us; the launch traced here: 363 us
  waiting for transfers between devices  304 us (83%)
  matrix products  18.8 us (5%)
  local copies, waits for them, and re-layouts  17.7 us (5%)
  between operations  14 us (4%)
  other arithmetic  8.17 us (2%)
    unnamed x6, waiting for transfers between devices  161 us
    all_gather x1, waiting for transfers between devices, shards(): lax.all_gather(jnp.concatenate([masked, cot_valid], axis=1), 'col', axis=...  90.9 us
    all_gather x1, waiting for transfers between devices, shards(): lax.all_gather(jnp.concatenate([hidden, dgate, dup], axis=1), 'row', axis...  52 us
    unnamed x23, local copies, waits for them, and re-layouts  15.2 us
  transfers between devices with their start and end apart: 4, of which 4 were waited for; matrix products, arithmetic and copies ran while one was open for 2% of the time, Pallas kernels for 0%

profile of v1, /device:TPU:1, one launch (start us, length us, event | category | flops | bytes accessed | tf_op | source)
XLA Modules:
  0.0 362.6 jit_solution(1127609087687936519)
XLA Ops:
  7.2 0.0 copy-start
  7.2 0.0 all-gather.3.cloned.1.call-start
  7.2 0.9 convert_reduce_fusion
  8.2 0.8 dynamic_slice.3
  8.9 1.0 copy.26
  10.0 1.0 copy.27
  11.0 0.8 select_reduce_fusion.2
  11.8 0.3 broadcast_select_fusion
  12.1 0.1 copy.29
  12.2 0.1 copy.28
  12.4 0.7 pad_maximum_fusion.3
  13.0 0.0 all-gather.3.cloned.1.call-update
  13.1 0.0 reduce-scatter.7.cloned.1.call-start
  13.1 90.9 %all-gather.3.cloned.1.call-done = bf16[1024,2048]{1,0:T(8,128)(2,1)} async-done(((bf16[32,2048]{1,0:T(8,128)(2,1)}), bf16[1024,2048]{1,0:T(8,128)(2,1)}) %all-gather.3.cloned.1.call-update) | async-done | bytes 4194320 | tf_op jit(solution)/shard_map/all_gather | solution.py:71
  104.0 0.0 copy-done.1
  104.0 2.9 convolution_convert_fusion.3
  106.9 0.0 copy-start.6
  106.9 1.2 fusion.4
  108.1 1.2 convolution_convert_fusion.4
  109.3 1.8 pad_maximum_fusion.1
  111.1 4.5 %copy.32 = bf16[1024,1344]{1,0:T(8,128)(2,1)} copy(bf16[1024,1344]{0,1:T(8,128)(2,1)} %pad_maximum_fusion.1) | data formatting | bytes 5505024
  115.6 0.0 reduce-scatter.7.cloned.1.call-update
  115.7 0.0 all-gather.5.cloned.1.call-start
  115.7 39.9 %reduce-scatter.7.cloned.1.call-done = bf16[128,1344]{1,0:T(8,128)(2,1)} async-done(((bf16[1024,1344]{1,0:T(8,128)(2,1)}), bf16[128,1344]{1,0:T(8,128)(2,1)}) %reduce-scatter.7.cloned.1.call-update) | async-done | bytes 344080
  155.6 1.2 copy.33
  156.8 0.1 multiply_convert_fusion.2
  157.0 0.8 pad_maximum_fusion.2
  157.8 0.0 all-gather.5.cloned.1.call-update
  157.8 0.0 copy-start.7
  157.8 0.2 reduce-scatter.9.cloned.1.call-start
  158.0 52.0 %all-gather.5.cloned.1.call-done = bf16[1024,1344]{0,1:T(8,128)(2,1)} async-done(((bf16[128,1344]{0,1:T(8,128)(2,1)}), bf16[1024,1344]{0,1:T(8,128)(2,1)}) %all-gather.5.cloned.1.call-update) | async-done | bytes 2752528 | tf_op jit(solution)/shard_map/all_gather | solution.py:100
  210.1 2.6 convolution_convert_fusion
  212.7 0.0 copy-done.7
  212.7 0.0 copy-done.2
  212.7 1.4 fusion.17
  214.1 1.4 add_convert_fusion
  215.5 2.4 pad_maximum_fusion
  217.9 6.5 %copy.34 = bf16[1024,2048]{1,0:T(8,128)(2,1)} copy(bf16[1024,2048]{0,1:T(8,128)(2,1)} %pad_maximum_fusion) | data formatting | bytes 8388608
  224.5 0.0 reduce-scatter.9.cloned.1.call-update
  224.5 4.1 %fusion.7 = bf16[448,1024]{1,0:T(8,128)(2,1)} fusion(bf16[1024,2048]{1,0:T(8,128)(2,1)} %all-gather.3.cloned.1.call-done, bf16[1024,1344]{0,1:T(8,128)(2,1)} %all-gather.5.cloned.1.call-done), kind=kOutput, calls=%fused_computation.9 | convolution fusion | flops 939982848 | bytes 3932160 | tf_op jit(solution)/shard_map/dot_general | solution.py:106
  228.6 0.0 copy-done.3
  228.6 2.1 convolution_convert_fusion.2
  230.6 2.0 convolution_convert_fusion.1
  232.7 120.7 %reduce-scatter.9.cloned.1.call-done = bf16[32,2048]{1,0:T(8,128)(2,1)} async-done(((bf16[1024,2048]{1,0:T(8,128)(2,1)}), bf16[32,2048]{1,0:T(8,128)(2,1)}) %reduce-scatter.9.cloned.1.call-update) | async-done | bytes 131088
  353.4 1.5 fusion.23
  354.9 0.2 copy.37
  355.1 0.2 select_convert_fusion
  355.3 0.8 copy.31
  (13 shorter events, 0.1 us)
Async XLA Ops:
  7.2 99.7 %copy-start = (bf16[448,1024]{1,0:T(8,128)(2,1)S(1)}, bf16[448,1024]{1,0:T(8,128)(2,1)}, u32[]{:S(2)}) copy-start(bf16[448,1024]{1,0:T(8,128)(2,1)} %param.15) | copy-start | bytes 2752516
  7.2 96.8 %copy-start.1 = (bf16[1024,448]{0,1:T(8,128)(2,1)S(1)}, bf16[1024,448]{0,1:T(8,128)(2,1)}, u32[]{:S(2)}) copy-start(bf16[1024,448]{0,1:T(8,128)(2,1)} %param.14) | copy-start | bytes 2752516
  7.2 96.8 %all-gather.3.cloned.1.call-start = ((), (), s32[]{:S(2)}) async-start(), calls=%async_computation.2 | async-start | bytes 4325376 | tf_op jit(solution)/shard_map/all_gather | solution.py:71
  13.1 142.5 %reduce-scatter.7.cloned.1.call-start = ((), (), s32[]{:S(2)}) async-start(), calls=%async_computation.4 | async-start | bytes 3244032
  104.0 2.9 copy-start.4
  106.9 1.2 copy-start.6
  115.7 94.4 %all-gather.5.cloned.1.call-start = ((), (), s32[]{:S(2)}) async-start(), calls=%async_computation.3 | async-start | bytes 3096576 | tf_op jit(solution)/shard_map/all_gather | solution.py:100
  157.8 54.9 %copy-start.7 = (bf16[1024,448]{0,1:T(8,128)(2,1)S(1)}, bf16[1024,448]{0,1:T(8,128)(2,1)}, u32[]{:S(2)}) copy-start(bf16[1024,448]{0,1:T(8,128)(2,1)} %param.13) | copy-start | bytes 2752516
  157.8 195.6 %reduce-scatter.9.cloned.1.call-start = ((), (), s32[]{:S(2)}) async-start(), calls=%async_computation.5 | async-start | bytes 4325376
  210.1 2.6 copy-start.2
  224.5 4.1 %copy-start.3 = (bf16[1024,1344]{0,1:T(8,128)(2,1)S(1)}, bf16[1024,1344]{0,1:T(8,128)(2,1)}, u32[]{:S(2)}) copy-start(bf16[1024,1344]{0,1:T(8,128)(2,1)} %all-gather.5.cloned.1.call-done) | copy-start | bytes 8257540
  224.5 4.1 %copy-start.5 = (bf16[1024,2048]{1,0:T(8,128)(2,1)S(1)}, bf16[1024,2048]{1,0:T(8,128)(2,1)}, u32[]{:S(2)}) copy-start(bf16[1024,2048]{1,0:T(8,128)(2,1)} %all-gather.3.cloned.1.call-done) | copy-start | bytes 12582916
Sparse Core Ops, SparseCore 0:
  13.2 90.7 all-gather.2
  115.8 39.7 reduce-scatter.6
  157.9 52.1 all-gather.4
  224.6 128.7 reduce-scatter.8

commit v2 on v1

--- a/solution.py
+++ b/solution.py
@@ -31,6 +31,18 @@
     in_freq = (feat_index[None, :] >= freq_low) & (feat_index[None, :] < freq_high)
     keep_mask = (valid_rows & jnp.logical_not(in_time))[:, None] & jnp.logical_not(in_freq)
     return (keep_mask, valid_rows)
+
+
+def gather_by_exchange(part, axis, count):
+    spread = jnp.broadcast_to(part[None], (count,) + part.shape)
+    got = lax.all_to_all(spread, axis, 0, 0)
+    return got.reshape((count * part.shape[0],) + part.shape[1:])
+
+
+def sum_by_exchange(partial, axis, count):
+    split = partial.reshape((count, partial.shape[0] // count) + partial.shape[1:])
+    got = lax.all_to_all(split, axis, 0, 0)
+    return jnp.sum(got.astype(jnp.float32), axis=0)
 
 
 def shards(
@@ -73,7 +85,7 @@
     )
     tokens_all = both_all[:, :feat_cols]
     cot_all = both_all[:, feat_cols:]
-    sums = lax.psum_scatter(
+    sums = sum_by_exchange(
         jnp.concatenate(
             [
                 jnp.dot(tokens_all, gate_weight, preferred_element_type=jnp.float32),
@@ -85,9 +97,8 @@
             axis=1,
         ).astype(jnp.bfloat16),
         "row",
-        scatter_dimension=0,
-        tiled=True,
-    ).astype(jnp.float32)
+        lax.psum(1, "row"),
+    )
     gate = sums[:, :hidden_cols]
     up = sums[:, hidden_cols : 2 * hidden_cols]
     grad_hidden = sums[:, 2 * hidden_cols :]
@@ -97,8 +108,8 @@
         jnp.bfloat16
     )
     dup = (grad_hidden * gate * sigmoid_gate).astype(jnp.bfloat16)
-    acts_all = lax.all_gather(
-        jnp.concatenate([hidden, dgate, dup], axis=1), "row", axis=0, tiled=True
+    acts_all = gather_by_exchange(
+        jnp.concatenate([hidden, dgate, dup], axis=1), "row", lax.psum(1, "row")
     )
     hidden_all = acts_all[:, :hidden_cols]
     dgate_all = acts_all[:, hidden_cols : 2 * hidden_cols]
@@ -112,7 +123,7 @@
     grad_up = lax.dot_general(
         tokens_all, dup_all, contract_first, preferred_element_type=jnp.float32
     ).astype(jnp.bfloat16)
-    out_sums = lax.psum_scatter(
+    out_sums = sum_by_exchange(
         jnp.concatenate(
             [
                 jnp.dot(hidden_all, down_weight, preferred_element_type=jnp.float32).astype(
@@ -130,11 +141,10 @@
             axis=1,
         ),
         "col",
-        scatter_dimension=0,
-        tiled=True,
+        lax.psum(1, "col"),
     )
-    output = out_sums[:, :feat_cols]
-    grad_masked = out_sums[:, feat_cols:].astype(jnp.float32)
+    output = out_sums[:, :feat_cols].astype(jnp.bfloat16)
+    grad_masked = out_sums[:, feat_cols:]
     grad_frames = jnp.where(keep_mask, grad_masked, jnp.zeros_like(grad_masked)).astype(
         jnp.bfloat16
     )

time: 368 us -> 309 us (0.84); the launches traced: 363 us -> 308 us
  waiting for transfers between devices: 304 us -> 177 us
  blocking collectives: 0 us -> 72.4 us
  local copies, waits for them, and re-layouts: 17.7 us -> 8.57 us
  starting transfers between devices: 0.34 us -> 8.61 us
    unnamed x6 -> x1, waiting for transfers between devices: 161 us -> 0.02 us
    all_to_all x0 -> x1, waiting for transfers between devices: none -> 85.9 us  [sum_by_exchange(): got = lax.all_to_all(split, axis, 0, 0)]
    all_to_all x0 -> x2, blocking collectives: none -> 72.4 us  [the longest x1 37 us: sum_by_exchange(): got = lax.all_to_all(split, axis, 0, 0)]
    all_gather x1 -> x0, waiting for transfers between devices: 52 us -> none  [shards(): lax.all_gather(jnp.concatenate([hidden, dgate, dup], axis=1), 'row', axis...]
    unnamed x23 -> x14, local copies, waits for them, and re-layouts: 15.2 us -> 0.04 us
    all_to_all x0 -> x1, starting transfers between devices: none -> 8.57 us  [sum_by_exchange(): got = lax.all_to_all(split, axis, 0, 0)]
    concatenate x0 -> x4, local copies, waits for them, and re-layouts: none -> 7.01 us  [the longest x1 6.52 us: shards(): jnp.concatenate([jnp.dot(hidden_all, down_weight, preferred_element_type=...]
  transfers between devices with their start and end apart: 4 -> 2, of which waited for: 4 -> 2; matrix products, arithmetic and copies ran while one was open for 2% -> 3% of each run, Pallas kernels for 0% -> 0%
where the time goes in v2:
time: 309 us; the launch traced here: 308 us
  waiting for transfers between devices  177 us (57%)
  blocking collectives  72.4 us (23%)
  matrix products  17.5 us (6%)
  between operations  14.3 us (5%)
  other arithmetic  10.1 us (3%)
  starting transfers between devices  8.61 us (3%)
  local copies, waits for them, and re-layouts  8.57 us (3%)
    all_gather x1, waiting for transfers between devices, shards(): lax.all_gather(jnp.concatenate([masked, cot_valid], axis=1), 'col', axis=...  90.9 us
    all_to_all x1, waiting for transfers between devices, sum_by_exchange(): got = lax.all_to_all(split, axis, 0, 0)  85.9 us
    all_to_all x1, blocking collectives, sum_by_exchange(): got = lax.all_to_all(split, axis, 0, 0)  37 us
    all_to_all x1, blocking collectives, gather_by_exchange(): got = lax.all_to_all(spread, axis, 0, 0)  35.4 us
    all_to_all x1, starting transfers between devices, sum_by_exchange(): got = lax.all_to_all(split, axis, 0, 0)  8.57 us
    concatenate x1, local copies, waits for them, and re-layouts, shards(): jnp.concatenate([jnp.dot(hidden_all, down_weight, preferred_element_type=...  6.52 us
  transfers between devices with their start and end apart: 2, of which 2 were waited for; matrix products, arithmetic and copies ran while one was open for 3% of the time, Pallas kernels for 0%

profile of v2, /device:TPU:1, one launch (start us, length us, event | category | flops | bytes accessed | tf_op | source)
XLA Modules:
  0.0 308.3 jit_solution(14216487822354247606)
XLA Ops:
  7.2 0.0 copy-start
  7.2 0.0 all-gather.2.cloned.1.call-start
  7.2 0.9 convert_reduce_fusion.2
  8.1 0.8 dynamic_slice.3
  8.9 0.8 select_reduce_fusion.2
  9.7 1.0 broadcast_select_fusion
  10.7 0.7 pad_maximum_fusion.3
  11.4 0.0 all-gather.2.cloned.1.call-update
  11.4 90.9 %all-gather.2.cloned.1.call-done = bf16[1024,2048]{1,0:T(8,128)(2,1)} async-done(((bf16[32,2048]{1,0:T(8,128)(2,1)}), bf16[1024,2048]{1,0:T(8,128)(2,1)}) %all-gather.2.cloned.1.call-update) | async-done | bytes 4194320 | tf_op jit(solution)/shard_map/all_gather | solution.py:83
  102.3 0.0 copy-start.4
  102.3 3.1 %fusion.17 = bf16[56,8,8,128]{3,2,1,0:T(8,128)(2,1)S(1)} fusion(bf16[1024,448]{0,1:T(8,128)(2,1)} %param.14, bf16[1024,2048]{1,0:T(8,128)(2,1)} %all-gather.2.cloned.1.call-done), kind=kOutput, calls=%fused_computation.22 | convolution fusion | flops 939982848 | bytes 3932160 | tf_op jit(solution)/shard_map/dot_general | solution.py:92
  105.5 0.2 copy.47
  105.6 0.0 copy-done
  105.6 0.0 copy-done.4
  105.6 0.0 copy-start.6
  105.7 1.2 fusion.20
  106.8 0.2 copy.46
  107.0 0.0 copy-done.6
  107.0 1.2 fusion.14
  108.2 0.2 copy.48
  108.4 0.2 pad_maximum_fusion.1
  108.5 37.0 %all_to_all.15 = bf16[8,128,1344]{1,2,0:T(8,128)(2,1)S(1)} all-to-all(bf16[8,128,1344]{1,2,0:T(8,128)(2,1)S(1)} %pad_maximum_fusion.1), channel_id=1, replica_groups=mesh['row'=8,'col'=32] {'row'}, dimensions={0} | all-to-all | bytes 5505024 | tf_op jit(solution)/shard_map/all_to_all | solution.py:44
  145.5 0.4 convert_reduce_fusion.1
  145.9 0.1 multiply_convert_fusion.2
  146.1 0.4 broadcast_in_dim.10
  146.4 35.4 %all_to_all.16 = bf16[8,128,1344]{1,2,0:T(8,128)(2,1)S(1)} all-to-all(bf16[8,128,1344]{1,2,0:T(8,128)(2,1)S(1)} %broadcast_in_dim.10), channel_id=1, replica_groups=mesh['row'=8,'col'=32] {'row'}, dimensions={0} | all-to-all | bytes 5505024 | tf_op jit(solution)/shard_map/all_to_all | solution.py:38
  181.8 0.4 copy_bitcast_fusion
  182.2 0.0 copy-start.1
  182.3 1.3 convolution_convert_fusion
  183.6 0.0 copy-start.3
  183.6 1.3 fusion.26
  184.9 0.0 copy-done.1
  184.9 0.0 copy-done.3
  184.9 1.3 add_convert_fusion
  186.3 2.4 pad_maximum_fusion
  188.7 6.5 %copy.33 = bf16[1024,2048]{1,0:T(8,128)(2,1)} copy(bf16[1024,2048]{0,1:T(8,128)(2,1)} %pad_maximum_fusion) | data formatting | bytes 8388608 | tf_op jit(solution)/shard_map/concatenate | solution.py:127
  195.2 8.6 %all-to-all-start.2 = ((bf16[32,32,2048]{2,1,0:T(8,128)(2,1)}), bf16[32,32,2048]{2,1,0:T(8,128)(2,1)}, u32[]{:S(2)}, u32[]{:S(2)}) async-start(bf16[32,32,2048]{2,1,0:T(8,128)(2,1)} %bitcast.27), calls=%async_computation.2 | async-start | bytes 8388608 | tf_op jit(solution)/shard_map/all_to_all | solution.py:44
  203.8 0.0 copy-start.2
  203.8 0.0 copy-start.5
  203.8 4.1 %fusion.7 = bf16[448,1024]{1,0:T(8,128)(2,1)} fusion(bf16[1024,2048]{1,0:T(8,128)(2,1)} %all-gather.2.cloned.1.call-done, bf16[1024,1344]{0,1:T(8,128)(2,1)} %copy-done.1), kind=kOutput, calls=%fused_computation.12 | convolution fusion | flops 939982848 | bytes 3932160 | tf_op jit(solution)/shard_map/dot_general | solution.py:117
  207.9 0.0 copy-done.2
  207.9 0.0 copy-done.5
  207.9 2.1 convolution_convert_fusion.2
  209.9 2.1 convolution_convert_fusion.1
  212.0 85.9 %all-to-all-done.2 = bf16[32,32,2048]{2,1,0:T(8,128)(2,1)} async-done(((bf16[32,32,2048]{2,1,0:T(8,128)(2,1)}), bf16[32,32,2048]{2,1,0:T(8,128)(2,1)}, u32[]{:S(2)}, u32[]{:S(2)}) %all-to-all-start.2) | async-done | bytes 4194336 | tf_op jit(solution)/shard_map/all_to_all | solution.py:44
  297.9 2.8 convert_reduce_fusion
  300.7 0.7 fusion.30
  (4 shorter events, 0.0 us)
Async XLA Ops:
  7.2 98.5 %copy-start = (bf16[448,1024]{1,0:T(8,128)(2,1)S(1)}, bf16[448,1024]{1,0:T(8,128)(2,1)}, u32[]{:S(2)}) copy-start(bf16[448,1024]{1,0:T(8,128)(2,1)} %param.15) | copy-start | bytes 2752516
  7.2 95.2 %all-gather.2.cloned.1.call-start = ((), (), s32[]{:S(2)}) async-start(), calls=%async_computation.3 | async-start | bytes 4325376 | tf_op jit(solution)/shard_map/all_gather | solution.py:83
  102.3 3.3 %copy-start.4 = (bf16[1024,2048]{1,0:T(8,128)(2,1)S(1)}, bf16[1024,2048]{1,0:T(8,128)(2,1)}, u32[]{:S(2)}) copy-start(bf16[1024,2048]{1,0:T(8,128)(2,1)} %all-gather.2.cloned.1.call-done) | copy-start | bytes 12582916
  105.6 1.4 copy-start.6
  182.2 2.7 copy-start.1
  183.6 1.3 copy-start.3
  195.2 102.7 %all-to-all-start.2 = ((bf16[32,32,2048]{2,1,0:T(8,128)(2,1)}), bf16[32,32,2048]{2,1,0:T(8,128)(2,1)}, u32[]{:S(2)}, u32[]{:S(2)}) async-start(bf16[32,32,2048]{2,1,0:T(8,128)(2,1)} %bitcast.27), calls=%async_computation.2 | async-start | bytes 8388608 | tf_op jit(solution)/shard_map/all_to_all | solution.py:44
  203.8 4.1 %copy-start.2 = (bf16[1024,1344]{0,1:T(8,128)(2,1)S(1)}, bf16[1024,1344]{0,1:T(8,128)(2,1)}, u32[]{:S(2)}) copy-start(bf16[1024,1344]{0,1:T(8,128)(2,1)} %copy-done.1) | copy-start | bytes 8257540
  203.8 4.1 %copy-start.5 = (bf16[1024,2048]{1,0:T(8,128)(2,1)S(1)}, bf16[1024,2048]{1,0:T(8,128)(2,1)}, u32[]{:S(2)}) copy-start(bf16[1024,2048]{1,0:T(8,128)(2,1)} %all-gather.2.cloned.1.call-done) | copy-start | bytes 12582916
Sparse Core Ops, SparseCore 0:
  11.5 90.7 all-gather.1

commit v3 on v2

--- a/solution.py
+++ b/solution.py
@@ -1,7 +1,11 @@
 import jax
 import jax.numpy as jnp
 from jax import lax
-from jax.sharding import PartitionSpec as P
+from jax.sharding import Mesh, PartitionSpec as P
+
+COL = ("cz", "cx", "cc")
+CHIPS = ("cz", "cx")
+CORE = "cc"
 
 
 def span_masks(
@@ -60,7 +64,7 @@
 ):
     tok_rows, feat_cols = frames.shape
     hidden_cols = gate_weight.shape[1]
-    first_tok = lax.axis_index("col") * tok_rows
+    first_tok = lax.axis_index(COL) * tok_rows
     first_feat = lax.axis_index("row") * feat_cols
     tok_index = first_tok + jnp.arange(tok_rows, dtype=jnp.int32)
     feat_index = first_feat + jnp.arange(feat_cols, dtype=jnp.int32)
@@ -80,8 +84,9 @@
     cot_valid = jnp.where(valid_rows[:, None], cotangent, jnp.zeros_like(cotangent))
     contract_last = (((1,), (1,)), ((), ()))
     contract_first = (((0,), (0,)), ((), ()))
-    both_all = lax.all_gather(
-        jnp.concatenate([masked, cot_valid], axis=1), "col", axis=0, tiled=True
+    both = jnp.concatenate([masked, cot_valid], axis=1)
+    both_all = gather_by_exchange(
+        gather_by_exchange(both, CHIPS, lax.psum(1, CHIPS)), CORE, lax.psum(1, CORE)
     )
     tokens_all = both_all[:, :feat_cols]
     cot_all = both_all[:, feat_cols:]
@@ -124,7 +129,8 @@
         tokens_all, dup_all, contract_first, preferred_element_type=jnp.float32
     ).astype(jnp.bfloat16)
     out_sums = sum_by_exchange(
-        jnp.concatenate(
+        sum_by_exchange(
+            jnp.concatenate(
             [
                 jnp.dot(hidden_all, down_weight, preferred_element_type=jnp.float32).astype(
                     jnp.bfloat16
@@ -140,8 +146,11 @@
             ],
             axis=1,
         ),
-        "col",
-        lax.psum(1, "col"),
+            CORE,
+            lax.psum(1, CORE),
+        ).astype(jnp.bfloat16),
+        CHIPS,
+        lax.psum(1, CHIPS),
     )
     output = out_sums[:, :feat_cols].astype(jnp.bfloat16)
     grad_masked = out_sums[:, feat_cols:]
@@ -152,12 +161,14 @@
 
 
 def solution(mesh):
+    n_row, n_col = mesh.devices.shape
+    split = Mesh(mesh.devices.reshape(n_row, n_col // 4, 2, 2), ("row",) + COL)
     placed = (
-        P("col", "row"),
-        P("col", "row"),
-        P("row", "col"),
-        P("row", "col"),
-        P("col", "row"),
+        P(COL, "row"),
+        P(COL, "row"),
+        P("row", COL),
+        P("row", COL),
+        P(COL, "row"),
         P(),
         P(),
         P(),
@@ -167,14 +178,14 @@
     )
     return jax.shard_map(
         shards,
-        mesh=mesh,
+        mesh=split,
         in_specs=placed,
         out_specs=(
-            P("col", "row"),
-            P("col", "row"),
-            P("row", "col"),
-            P("row", "col"),
-            P("col", "row"),
+            P(COL, "row"),
+            P(COL, "row"),
+            P("row", COL),
+            P("row", COL),
+            P(COL, "row"),
         ),
         check_vma=False,
     )

time: 309 us -> 233 us (0.75)
  waiting for transfers between devices: 177 us -> 42.5 us
  blocking collectives: 72.4 us -> 154 us
  between operations: 14.3 us -> 0.92 us
  starting transfers between devices: 8.61 us -> 3.72 us
    all_gather x1 -> x0, waiting for transfers between devices: 90.9 us -> none  [shards(): lax.all_gather(jnp.concatenate([masked, cot_valid], axis=1), 'col', axis=...]
    all_to_all x1 -> x3, blocking collectives: 35.4 us -> 107 us  [gather_by_exchange(): got = lax.all_to_all(spread, axis, 0, 0)]
    all_to_all x1, waiting for transfers between devices: 85.9 us -> 42.5 us  [sum_by_exchange(): got = lax.all_to_all(split, axis, 0, 0)]
    all_to_all x1 -> x2, blocking collectives: 37 us -> 47.9 us  [sum_by_exchange(): got = lax.all_to_all(split, axis, 0, 0)]
    concatenate x1 -> x0, local copies, waits for them, and re-layouts: 6.52 us -> none  [shards(): jnp.concatenate([jnp.dot(hidden_all, down_weight, preferred_element_type=...]
    all_to_all x1, starting transfers between devices: 8.57 us -> 3.72 us  [sum_by_exchange(): got = lax.all_to_all(split, axis, 0, 0)]
  transfers between devices with their start and end apart: 2 -> 1, of which waited for: 2 -> 1; matrix products, arithmetic and copies ran while one was open for 3% -> 4% of each run, Pallas kernels for 0% -> 0%
where the time goes in v3:
time: 233 us; the launch traced here: 232 us
  blocking collectives  154 us (66%)
  waiting for transfers between devices  42.5 us (18%)
  matrix products  15.6 us (7%)
  other arithmetic  9.37 us (4%)
  local copies, waits for them, and re-layouts  5.68 us (2%)
  starting transfers between devices  3.72 us (2%)
    all_to_all x3, blocking collectives, gather_by_exchange(): got = lax.all_to_all(spread, axis, 0, 0)  107 us
    all_to_all x2, blocking collectives, sum_by_exchange(): got = lax.all_to_all(split, axis, 0, 0)  47.9 us
    all_to_all x1, waiting for transfers between devices, sum_by_exchange(): got = lax.all_to_all(split, axis, 0, 0)  42.5 us
    reduce_sum x3, other arithmetic, sum_by_exchange(): return jnp.sum(got.astype(jnp.float32), axis=0)  5.11 us
  transfers between devices with their start and end apart: 1, of which 1 were waited for; matrix products, arithmetic and copies ran while one was open for 4% of the time, Pallas kernels for 0%

profile of v3, /device:TPU:1, one launch (start us, length us, event | category | flops | bytes accessed | tf_op | source)
XLA Modules:
  0.0 232.2 jit_solution(12516291840933219930)
XLA Ops:
  0.6 0.0 copy-start
  0.7 0.9 convert_reduce_fusion.2
  1.5 0.8 dynamic_slice.3
  2.3 0.8 select_reduce_fusion.2
  3.2 1.0 broadcast_select_fusion
  4.2 0.2 broadcast_in_dim.16
  4.4 62.3 %all_to_all.30 = bf16[16,32,2048]{2,1,0:T(8,128)(2,1)S(1)} all-to-all(bf16[16,32,2048]{2,1,0:T(8,128)(2,1)S(1)} %broadcast_in_dim.16), channel_id=1, replica_groups=mesh['row'=8,'cz'=8,'cx'=2,'cc'=2] {'cz','cx'}, dimensions={0} | all-to-all | bytes 4194304 | tf_op jit(solution)/shard_map/all_to_all | solution.py:42
  66.7 0.5 broadcast_in_dim.18
  67.2 0.0 copy-start.5
  67.2 9.5 %all_to_all.31 = bf16[2,512,2048]{2,1,0:T(8,128)(2,1)S(1)} all-to-all(bf16[2,512,2048]{2,1,0:T(8,128)(2,1)S(1)} %broadcast_in_dim.18), channel_id=1, replica_groups=mesh['row'=8,'cz'=8,'cx'=2,'cc'=2] {'cc'}, dimensions={0} | all-to-all | bytes 8388608 | tf_op jit(solution)/shard_map/all_to_all | solution.py:42
  76.7 0.0 copy-done.5
  76.7 1.1 fusion.17
  77.9 0.2 copy.55
  78.0 0.0 copy-done
  78.0 0.0 copy-start.6
  78.0 1.2 fusion.20
  79.2 0.2 copy.54
  79.4 0.0 copy-done.3
  79.4 0.0 copy-done.6
  79.4 1.2 fusion.14
  80.6 0.2 copy.56
  80.8 0.2 pad_maximum_fusion.1
  80.9 37.1 %all_to_all.32 = bf16[8,128,1344]{1,2,0:T(8,128)(2,1)S(1)} all-to-all(bf16[8,128,1344]{1,2,0:T(8,128)(2,1)S(1)} %pad_maximum_fusion.1), channel_id=1, replica_groups=mesh['row'=8,'cz'=8,'cx'=2,'cc'=2] {'row'}, dimensions={0} | all-to-all | bytes 5505024 | tf_op jit(solution)/shard_map/all_to_all | solution.py:48
  118.0 0.4 convert_reduce_fusion
  118.4 0.1 multiply_convert_fusion.2
  118.6 0.4 broadcast_in_dim.19
  119.0 34.9 %all_to_all.33 = bf16[8,128,1344]{1,2,0:T(8,128)(2,1)S(1)} all-to-all(bf16[8,128,1344]{1,2,0:T(8,128)(2,1)S(1)} %broadcast_in_dim.19), channel_id=1, replica_groups=mesh['row'=8,'cz'=8,'cx'=2,'cc'=2] {'row'}, dimensions={0} | all-to-all | bytes 5505024 | tf_op jit(solution)/shard_map/all_to_all | solution.py:42
  153.9 0.4 copy_bitcast_fusion.1
  154.3 0.0 copy-start.1
  154.3 1.3 convolution_convert_fusion
  155.6 1.3 fusion.26
  156.9 0.0 copy-done.1
  156.9 1.3 add_convert_fusion
  158.3 0.4 pad_maximum_fusion
  158.7 0.3 copy.53
  159.0 10.8 %all_to_all.34 = bf16[2,512,2048]{1,2,0:T(8,128)(2,1)} all-to-all(bf16[2,512,2048]{1,2,0:T(8,128)(2,1)S(1)} %bitcast.34), channel_id=1, replica_groups=mesh['row'=8,'cz'=8,'cx'=2,'cc'=2] {'cc'}, dimensions={0} | all-to-all | bytes 8388608 | tf_op jit(solution)/shard_map/all_to_all | solution.py:48
  169.8 4.4 %reduce_sum.101 = bf16[512,2048]{0,1:T(8,128)(2,1)S(1)} reduce(bf16[2,512,2048]{1,2,0:T(8,128)(2,1)} %all_to_all.34, bf16[]{:T(256)} %constant.37.clone.1), dimensions={0}, to_apply=%region_8.9 | reduce | flops 1048576 | bytes 6291458 | tf_op jit(solution)/shard_map/reduce_sum | solution.py:49
  174.2 2.5 %copy.37 = bf16[512,2048]{1,0:T(8,128)(2,1)} copy(bf16[512,2048]{0,1:T(8,128)(2,1)S(1)} %reduce_sum.101) | data formatting | bytes 4194304 | tf_op jit(solution)/shard_map/reduce_sum | solution.py:49
  176.7 3.7 %all-to-all-start.5 = ((bf16[16,32,2048]{2,1,0:T(8,128)(2,1)}), bf16[16,32,2048]{2,1,0:T(8,128)(2,1)S(1)}, u32[]{:S(2)}, u32[]{:S(2)}) async-start(bf16[16,32,2048]{2,1,0:T(8,128)(2,1)} %bitcast.36), calls=%async_computation.5 | async-start | bytes 4194304 | tf_op jit(solution)/shard_map/all_to_all | solution.py:48
  180.5 0.0 copy-start.2
  180.5 0.0 copy-start.4
  180.5 4.1 %fusion.7 = bf16[448,1024]{1,0:T(8,128)(2,1)} fusion(bf16[1024,2048]{1,0:T(8,128)(2,1)} %bitcast.40, bf16[1024,1344]{0,1:T(8,128)(2,1)} %copy-done.1), kind=kOutput, calls=%fused_computation.13 | convolution fusion | flops 939982848 | bytes 3932160 | tf_op jit(solution)/shard_map/dot_general | solution.py:122
  184.5 0.0 copy-done.2
  184.6 2.1 convolution_convert_fusion.2
  186.6 2.0 convolution_convert_fusion.1
  188.7 42.5 %all-to-all-done.5 = bf16[16,32,2048]{2,1,0:T(8,128)(2,1)S(1)} async-done(((bf16[16,32,2048]{2,1,0:T(8,128)(2,1)}), bf16[16,32,2048]{2,1,0:T(8,128)(2,1)S(1)}, u32[]{:S(2)}, u32[]{:S(2)}) %all-to-all-start.5) | async-done | bytes 2097184 | tf_op jit(solution)/shard_map/all_to_all | solution.py:48
  231.1 0.3 convert_reduce_fusion.1
  231.4 0.7 fusion.30
  (7 shorter events, 0.1 us)
Async XLA Ops:
  0.6 77.4 %copy-start = (bf16[448,1024]{1,0:T(8,128)(2,1)S(1)}, bf16[448,1024]{1,0:T(8,128)(2,1)}, u32[]{:S(2)}) copy-start(bf16[448,1024]{1,0:T(8,128)(2,1)} %param.15) | copy-start | bytes 2752516
  67.2 9.5 %copy-start.5 = (bf16[1024,448]{0,1:T(8,128)(2,1)S(1)}, bf16[1024,448]{0,1:T(8,128)(2,1)}, u32[]{:S(2)}) copy-start(bf16[1024,448]{0,1:T(8,128)(2,1)} %param.14) | copy-start | bytes 2752516
  76.7 2.7 %copy-start.3 = (bf16[2,512,2048]{2,1,0:T(8,128)(2,1)}, bf16[2,512,2048]{2,1,0:T(8,128)(2,1)S(1)}, u32[]{:S(2)}) copy-start(bf16[2,512,2048]{2,1,0:T(8,128)(2,1)S(1)} %all_to_all.31) | copy-start | bytes 12582916
  78.0 1.4 copy-start.6
  154.3 2.6 %copy-start.1 = (bf16[1024,1344]{0,1:T(8,128)(2,1)}, bf16[1024,1344]{0,1:T(8,128)(2,1)S(1)}, u32[]{:S(2)}) copy-start(bf16[1024,1344]{0,1:T(8,128)(2,1)S(1)} %copy_bitcast_fusion.1) | copy-start | bytes 8257540
  176.7 54.4 %all-to-all-start.5 = ((bf16[16,32,2048]{2,1,0:T(8,128)(2,1)}), bf16[16,32,2048]{2,1,0:T(8,128)(2,1)S(1)}, u32[]{:S(2)}, u32[]{:S(2)}) async-start(bf16[16,32,2048]{2,1,0:T(8,128)(2,1)} %bitcast.36), calls=%async_computation.5 | async-start | bytes 4194304 | tf_op jit(solution)/shard_map/all_to_all | solution.py:48
  180.5 4.1 %copy-start.2 = (bf16[1024,1344]{0,1:T(8,128)(2,1)S(1)}, bf16[1024,1344]{0,1:T(8,128)(2,1)}, u32[]{:S(2)}) copy-start(bf16[1024,1344]{0,1:T(8,128)(2,1)} %copy-done.1) | copy-start | bytes 8257540
  180.5 4.1 %copy-start.4 = (bf16[2,512,2048]{2,1,0:T(8,128)(2,1)S(1)}, bf16[2,512,2048]{2,1,0:T(8,128)(2,1)}, u32[]{:S(2)}) copy-start(bf16[2,512,2048]{2,1,0:T(8,128)(2,1)} %copy-done.3) | copy-start | bytes 12582916

commit v4 on v3

--- a/solution.py
+++ b/solution.py
@@ -6,6 +6,7 @@
 COL = ("cz", "cx", "cc")
 CHIPS = ("cz", "cx")
 CORE = "cc"
+LEVELS = ("cz", "cx", "cc")
 
 
 def span_masks(
@@ -84,10 +85,9 @@
     cot_valid = jnp.where(valid_rows[:, None], cotangent, jnp.zeros_like(cotangent))
     contract_last = (((1,), (1,)), ((), ()))
     contract_first = (((0,), (0,)), ((), ()))
-    both = jnp.concatenate([masked, cot_valid], axis=1)
-    both_all = gather_by_exchange(
-        gather_by_exchange(both, CHIPS, lax.psum(1, CHIPS)), CORE, lax.psum(1, CORE)
-    )
+    both_all = jnp.concatenate([masked, cot_valid], axis=1)
+    for level in LEVELS:
+        both_all = gather_by_exchange(both_all, level, lax.psum(1, level))
     tokens_all = both_all[:, :feat_cols]
     cot_all = both_all[:, feat_cols:]
     sums = sum_by_exchange(
@@ -128,30 +128,26 @@
     grad_up = lax.dot_general(
         tokens_all, dup_all, contract_first, preferred_element_type=jnp.float32
     ).astype(jnp.bfloat16)
-    out_sums = sum_by_exchange(
-        sum_by_exchange(
-            jnp.concatenate(
-            [
-                jnp.dot(hidden_all, down_weight, preferred_element_type=jnp.float32).astype(
-                    jnp.bfloat16
-                ),
-                (
-                    lax.dot_general(
-                        dgate_all, gate_weight, contract_last, preferred_element_type=jnp.float32
-                    )
-                    + lax.dot_general(
-                        dup_all, up_weight, contract_last, preferred_element_type=jnp.float32
-                    )
-                ).astype(jnp.bfloat16),
-            ],
-            axis=1,
-        ),
-            CORE,
-            lax.psum(1, CORE),
-        ).astype(jnp.bfloat16),
-        CHIPS,
-        lax.psum(1, CHIPS),
+    out_sums = jnp.concatenate(
+        [
+            jnp.dot(hidden_all, down_weight, preferred_element_type=jnp.float32).astype(
+                jnp.bfloat16
+            ),
+            (
+                lax.dot_general(
+                    dgate_all, gate_weight, contract_last, preferred_element_type=jnp.float32
+                )
+                + lax.dot_general(
+                    dup_all, up_weight, contract_last, preferred_element_type=jnp.float32
+                )
+            ).astype(jnp.bfloat16),
+        ],
+        axis=1,
     )
+    for level in reversed(LEVELS):
+        if level != LEVELS[-1]:
+            out_sums = out_sums.astype(jnp.bfloat16)
+        out_sums = sum_by_exchange(out_sums, level, lax.psum(1, level))
     output = out_sums[:, :feat_cols].astype(jnp.bfloat16)
     grad_masked = out_sums[:, feat_cols:]
     grad_frames = jnp.where(keep_mask, grad_masked, jnp.zeros_like(grad_masked)).astype(

time: 233 us -> 244 us (1.047)
  blocking collectives: 154 us -> 186 us
  waiting for transfers between devices: 42.5 us -> 20.9 us
    all_to_all x2 -> x3, blocking collectives: 47.9 us -> 76.5 us  [sum_by_exchange(): got = lax.all_to_all(split, axis, 0, 0)]
    all_to_all x1, waiting for transfers between devices: 42.5 us -> 20.9 us  [sum_by_exchange(): got = lax.all_to_all(split, axis, 0, 0)]
    all_to_all x3 -> x4, blocking collectives: 107 us -> 109 us  [gather_by_exchange(): got = lax.all_to_all(spread, axis, 0, 0)]
    reduce_sum x3 -> x4, other arithmetic: 5.11 us -> 6.61 us  [sum_by_exchange(): return jnp.sum(got.astype(jnp.float32), axis=0)]
  transfers between devices with their start and end apart: 1 -> 1, of which waited for: 1 -> 1; matrix products, arithmetic and copies ran while one was open for 4% -> 3% of each run, Pallas kernels for 0% -> 0%
where the time goes in v4:
time: 244 us; the launch traced here: 243 us
  blocking collectives  186 us (76%)
  waiting for transfers between devices  20.9 us (9%)
  matrix products  15.6 us (6%)
  other arithmetic  10.9 us (4%)
  local copies, waits for them, and re-layouts  5.71 us (2%)
  starting transfers between devices  3.56 us (1%)
    all_to_all x4, blocking collectives, gather_by_exchange(): got = lax.all_to_all(spread, axis, 0, 0)  109 us
    all_to_all x3, blocking collectives, sum_by_exchange(): got = lax.all_to_all(split, axis, 0, 0)  76.5 us
    all_to_all x1, waiting for transfers between devices, sum_by_exchange(): got = lax.all_to_all(split, axis, 0, 0)  20.9 us
    reduce_sum x4, other arithmetic, sum_by_exchange(): return jnp.sum(got.astype(jnp.float32), axis=0)  6.61 us
  transfers between devices with their start and end apart: 1, of which 1 were waited for; matrix products, arithmetic and copies ran while one was open for 3% of the time, Pallas kernels for 0%

profile of v4, /device:TPU:1, one launch (start us, length us, event | category | flops | bytes accessed | tf_op | source)
XLA Modules:
  0.0 243.1 jit_solution(2114480188688606333)
XLA Ops:
  0.6 0.0 copy-start
  0.7 0.9 convert_reduce_fusion.2
  1.5 0.8 dynamic_slice.3
  2.3 0.8 select_reduce_fusion.2
  3.2 1.0 broadcast_select_fusion
  4.2 0.1 broadcast_in_dim.23
  4.3 36.2 %all_to_all.40 = bf16[8,32,2048]{2,1,0:T(8,128)(2,1)S(1)} all-to-all(bf16[8,32,2048]{2,1,0:T(8,128)(2,1)S(1)} %broadcast_in_dim.23), channel_id=1, replica_groups=mesh['row'=8,'cz'=8,'cx'=2,'cc'=2] {'cz'}, dimensions={0} | all-to-all | bytes 2097152 | tf_op jit(solution)/shard_map/all_to_all | solution.py:43
  40.5 0.3 broadcast_in_dim.25
  40.7 27.6 %all_to_all.41 = bf16[2,256,2048]{2,1,0:T(8,128)(2,1)S(1)} all-to-all(bf16[2,256,2048]{2,1,0:T(8,128)(2,1)S(1)} %broadcast_in_dim.25), channel_id=1, replica_groups=mesh['row'=8,'cz'=8,'cx'=2,'cc'=2] {'cx'}, dimensions={0} | all-to-all | bytes 4194304 | tf_op jit(solution)/shard_map/all_to_all | solution.py:43
  68.3 0.5 broadcast_in_dim.27
  68.9 0.0 copy-start.6
  68.9 10.3 %all_to_all.42 = bf16[2,512,2048]{2,1,0:T(8,128)(2,1)S(1)} all-to-all(bf16[2,512,2048]{2,1,0:T(8,128)(2,1)S(1)} %broadcast_in_dim.27), channel_id=1, replica_groups=mesh['row'=8,'cz'=8,'cx'=2,'cc'=2] {'cc'}, dimensions={0} | all-to-all | bytes 8388608 | tf_op jit(solution)/shard_map/all_to_all | solution.py:43
  79.2 0.0 copy-done.6
  79.2 1.1 fusion.17
  80.4 0.2 copy.79
  80.6 0.0 copy-done
  80.6 0.0 copy-start.7
  80.6 1.2 fusion.20
  81.8 0.2 copy.78
  81.9 0.0 copy-done.4
  82.0 0.0 copy-done.7
  82.0 1.2 fusion.14
  83.1 0.2 copy.80
  83.3 0.2 pad_maximum_fusion.1
  83.5 37.1 %all_to_all.43 = bf16[8,128,1344]{1,2,0:T(8,128)(2,1)S(1)} all-to-all(bf16[8,128,1344]{1,2,0:T(8,128)(2,1)S(1)} %pad_maximum_fusion.1), channel_id=1, replica_groups=mesh['row'=8,'cz'=8,'cx'=2,'cc'=2] {'row'}, dimensions={0} | all-to-all | bytes 5505024 | tf_op jit(solution)/shard_map/all_to_all | solution.py:49
  120.6 0.4 convert_reduce_fusion
  121.0 0.1 multiply_convert_fusion.2
  121.1 0.4 broadcast_in_dim.28
  121.5 34.9 %all_to_all.44 = bf16[8,128,1344]{1,2,0:T(8,128)(2,1)S(1)} all-to-all(bf16[8,128,1344]{1,2,0:T(8,128)(2,1)S(1)} %broadcast_in_dim.28), channel_id=1, replica_groups=mesh['row'=8,'cz'=8,'cx'=2,'cc'=2] {'row'}, dimensions={0} | all-to-all | bytes 5505024 | tf_op jit(solution)/shard_map/all_to_all | solution.py:43
  156.4 0.4 copy_bitcast_fusion.1
  156.9 1.3 convolution_convert_fusion
  158.2 1.3 fusion.26
  159.5 1.3 add_convert_fusion
  160.8 0.4 pad_maximum_fusion
  161.3 0.3 copy.76
  161.6 10.8 %all_to_all.45 = bf16[2,512,2048]{1,2,0:T(8,128)(2,1)} all-to-all(bf16[2,512,2048]{1,2,0:T(8,128)(2,1)S(1)} %bitcast.39), channel_id=1, replica_groups=mesh['row'=8,'cz'=8,'cx'=2,'cc'=2] {'cc'}, dimensions={0} | all-to-all | bytes 8388608 | tf_op jit(solution)/shard_map/all_to_all | solution.py:49
  172.4 4.4 %reduce_sum.113 = bf16[512,2048]{0,1:T(8,128)(2,1)S(1)} reduce(bf16[2,512,2048]{1,2,0:T(8,128)(2,1)} %all_to_all.45, bf16[]{:T(256)} %constant.38.clone.1), dimensions={0}, to_apply=%region_8.9 | reduce | flops 1048576 | bytes 6291458 | tf_op jit(solution)/shard_map/reduce_sum | solution.py:50
  176.8 0.1 copy.77
  176.9 28.7 %all_to_all.46 = bf16[2,256,2048]{1,2,0:T(8,128)(2,1)S(1)} all-to-all(bf16[2,256,2048]{1,2,0:T(8,128)(2,1)S(1)} %bitcast.42), channel_id=1, replica_groups=mesh['row'=8,'cz'=8,'cx'=2,'cc'=2] {'cx'}, dimensions={0} | all-to-all | bytes 4194304 | tf_op jit(solution)/shard_map/all_to_all | solution.py:49
  205.6 1.7 reduce_sum.114
  207.3 2.3 copy.57
  209.5 3.6 %all-to-all-start.7 = ((bf16[8,32,2048]{2,1,0:T(8,128)(2,1)}), bf16[8,32,2048]{2,1,0:T(8,128)(2,1)S(1)}, u32[]{:S(2)}, u32[]{:S(2)}) async-start(bf16[8,32,2048]{2,1,0:T(8,128)(2,1)} %bitcast.3), calls=%async_computation.7 | async-start | bytes 2097152 | tf_op jit(solution)/shard_map/all_to_all | solution.py:49
  213.1 4.1 %fusion.7 = bf16[448,1024]{1,0:T(8,128)(2,1)} fusion(bf16[1024,2048]{1,0:T(8,128)(2,1)} %bitcast.47, bf16[1024,1344]{0,1:T(8,128)(2,1)} %copy-done.2), kind=kOutput, calls=%fused_computation.14 | convolution fusion | flops 939982848 | bytes 3932160 | tf_op jit(solution)/shard_map/dot_general | solution.py:122
  217.2 2.1 convolution_convert_fusion.2
  219.2 2.0 convolution_convert_fusion.1
  221.3 20.9 %all-to-all-done.7 = bf16[8,32,2048]{2,1,0:T(8,128)(2,1)S(1)} async-done(((bf16[8,32,2048]{2,1,0:T(8,128)(2,1)}), bf16[8,32,2048]{2,1,0:T(8,128)(2,1)S(1)}, u32[]{:S(2)}, u32[]{:S(2)}) %all-to-all-start.7) | async-done | bytes 1048608 | tf_op jit(solution)/shard_map/all_to_all | solution.py:49
  242.2 0.1 convert_reduce_fusion.1
  242.4 0.7 fusion.30
  (14 shorter events, 0.1 us)
Async XLA Ops:
  0.6 79.9 %copy-start = (bf16[448,1024]{1,0:T(8,128)(2,1)S(1)}, bf16[448,1024]{1,0:T(8,128)(2,1)}, u32[]{:S(2)}) copy-start(bf16[448,1024]{1,0:T(8,128)(2,1)} %param.15) | copy-start | bytes 2752516
  68.9 10.4 %copy-start.6 = (bf16[1024,448]{0,1:T(8,128)(2,1)S(1)}, bf16[1024,448]{0,1:T(8,128)(2,1)}, u32[]{:S(2)}) copy-start(bf16[1024,448]{0,1:T(8,128)(2,1)} %param.14) | copy-start | bytes 2752516
  79.2 2.7 %copy-start.4 = (bf16[2,512,2048]{2,1,0:T(8,128)(2,1)}, bf16[2,512,2048]{2,1,0:T(8,128)(2,1)S(1)}, u32[]{:S(2)}) copy-start(bf16[2,512,2048]{2,1,0:T(8,128)(2,1)S(1)} %all_to_all.42) | copy-start | bytes 12582916
  80.6 1.4 copy-start.7
  156.8 2.6 %copy-start.2 = (bf16[1024,1344]{0,1:T(8,128)(2,1)}, bf16[1024,1344]{0,1:T(8,128)(2,1)S(1)}, u32[]{:S(2)}) copy-start(bf16[1024,1344]{0,1:T(8,128)(2,1)S(1)} %copy_bitcast_fusion.1) | copy-start | bytes 8257540
  209.5 32.7 %all-to-all-start.7 = ((bf16[8,32,2048]{2,1,0:T(8,128)(2,1)}), bf16[8,32,2048]{2,1,0:T(8,128)(2,1)S(1)}, u32[]{:S(2)}, u32[]{:S(2)}) async-start(bf16[8,32,2048]{2,1,0:T(8,128)(2,1)} %bitcast.3), calls=%async_computation.7 | async-start | bytes 2097152 | tf_op jit(solution)/shard_map/all_to_all | solution.py:49
  213.1 4.1 %copy-start.3 = (bf16[1024,1344]{0,1:T(8,128)(2,1)S(1)}, bf16[1024,1344]{0,1:T(8,128)(2,1)}, u32[]{:S(2)}) copy-start(bf16[1024,1344]{0,1:T(8,128)(2,1)} %copy-done.2) | copy-start | bytes 8257540
  213.1 4.1 %copy-start.5 = (bf16[2,512,2048]{2,1,0:T(8,128)(2,1)S(1)}, bf16[2,512,2048]{2,1,0:T(8,128)(2,1)}, u32[]{:S(2)}) copy-start(bf16[2,512,2048]{2,1,0:T(8,128)(2,1)} %copy-done.4) | copy-start | bytes 12582916
  219.2 23.9 %copy-start.1 = (bf16[448,1024]{1,0:T(8,128)(2,1)S(1)}, bf16[448,1024]{1,0:T(8,128)(2,1)}, u32[]{:S(2)}) copy-start(bf16[448,1024]{1,0:T(8,128)(2,1)} %param.15) | copy-start | bytes 2752516

commit v5 on v3

--- a/solution.py
+++ b/solution.py
@@ -45,8 +45,11 @@
 
 def sum_by_exchange(partial, axis, count):
     split = partial.reshape((count, partial.shape[0] // count) + partial.shape[1:])
-    got = lax.all_to_all(split, axis, 0, 0)
-    return jnp.sum(got.astype(jnp.float32), axis=0)
+    got = lax.all_to_all(split, axis, 0, 0).astype(jnp.float32)
+    total = got[0]
+    for index in range(1, count):
+        total = total + got[index]
+    return total
 
 
 def shards(

time: 233 us -> 238 us (1.021)
  local copies, waits for them, and re-layouts: 5.68 us -> 9.44 us
    all_to_all x0 -> x1, local copies, waits for them, and re-layouts: none -> 6.27 us  [sum_by_exchange(): got = lax.all_to_all(split, axis, 0, 0).astype(jnp.float32)]
    convert_element_type x0 -> x4, other arithmetic: none -> 6.08 us  [the longest x3 4.12 us: sum_by_exchange(): got = lax.all_to_all(split, axis, 0, 0).astype(jnp.float32)]
    reduce_sum x3 -> x0, other arithmetic: 5.11 us -> none  [sum_by_exchange(): return jnp.sum(got.astype(jnp.float32), axis=0)]
    reduce_sum x1 -> x0, local copies, waits for them, and re-layouts: 2.52 us -> none  [sum_by_exchange(): return jnp.sum(got.astype(jnp.float32), axis=0)]
  transfers between devices with their start and end apart: 1 -> 1, of which waited for: 1 -> 1; matrix products, arithmetic and copies ran while one was open for 4% -> 3% of each run, Pallas kernels for 0% -> 0%
where the time goes in v5:
time: 238 us
  blocking collectives  154 us (65%)
  waiting for transfers between devices  42.5 us (18%)
  matrix products  15.7 us (7%)
  other arithmetic  10.8 us (5%)
  local copies, waits for them, and re-layouts  9.44 us (4%)
  starting transfers between devices  3.72 us (2%)
    all_to_all x3, blocking collectives, gather_by_exchange(): got = lax.all_to_all(spread, axis, 0, 0)  107 us
    all_to_all x2, blocking collectives, sum_by_exchange(): got = lax.all_to_all(split, axis, 0, 0).astype(jnp.float32)  47.9 us
    all_to_all x1, waiting for transfers between devices, sum_by_exchange(): got = lax.all_to_all(split, axis, 0, 0).astype(jnp.float32)  42.5 us
    all_to_all x1, local copies, waits for them, and re-layouts, sum_by_exchange(): got = lax.all_to_all(split, axis, 0, 0).astype(jnp.float32)  6.27 us
  transfers between devices with their start and end apart: 1, of which 1 were waited for; matrix products, arithmetic and copies ran while one was open for 3% of the time, Pallas kernels for 0%

profile of v5, /device:TPU:1, one launch (start us, length us, event | category | flops | bytes accessed | tf_op | source)
XLA Modules:
  0.0 237.6 jit_solution(6082800037299667410)
XLA Ops:
  0.6 0.0 copy-start
  0.7 0.9 convert_reduce_fusion
  1.5 0.8 dynamic_slice.3
  2.3 0.8 select_reduce_fusion.2
  3.2 1.0 broadcast_select_fusion
  4.2 0.2 broadcast_in_dim.16
  4.4 62.3 %all_to_all.30 = bf16[16,32,2048]{2,1,0:T(8,128)(2,1)S(1)} all-to-all(bf16[16,32,2048]{2,1,0:T(8,128)(2,1)S(1)} %broadcast_in_dim.16), channel_id=1, replica_groups=mesh['row'=8,'cz'=8,'cx'=2,'cc'=2] {'cz','cx'}, dimensions={0} | all-to-all | bytes 4194304 | tf_op jit(solution)/shard_map/all_to_all | solution.py:42
  66.7 0.5 broadcast_in_dim.18
  67.2 0.0 copy-start.6
  67.2 9.5 %all_to_all.31 = bf16[2,512,2048]{2,1,0:T(8,128)(2,1)S(1)} all-to-all(bf16[2,512,2048]{2,1,0:T(8,128)(2,1)S(1)} %broadcast_in_dim.18), channel_id=1, replica_groups=mesh['row'=8,'cz'=8,'cx'=2,'cc'=2] {'cc'}, dimensions={0} | all-to-all | bytes 8388608 | tf_op jit(solution)/shard_map/all_to_all | solution.py:42
  76.7 0.0 copy-done.6
  76.7 1.2 fusion.18
  77.9 0.2 copy.47
  78.0 0.0 copy-done
  78.0 0.0 copy-start.7
  78.1 1.2 fusion.21
  79.2 0.2 copy.46
  79.4 0.0 copy-done.4
  79.4 0.0 copy-done.7
  79.4 1.1 fusion.15
  80.6 0.2 copy.48
  80.8 0.2 pad_maximum_fusion.1
  80.9 37.1 %all_to_all.32 = bf16[8,128,1344]{1,2,0:T(8,128)(2,1)S(1)} all-to-all(bf16[8,128,1344]{1,2,0:T(8,128)(2,1)S(1)} %pad_maximum_fusion.1), channel_id=1, replica_groups=mesh['row'=8,'cz'=8,'cx'=2,'cc'=2] {'row'}, dimensions={0} | all-to-all | bytes 5505024 | tf_op jit(solution)/shard_map/all_to_all | solution.py:48
  118.0 0.4 convert_element_type.51
  118.4 0.2 fusion.31
  118.6 0.1 multiply_convert_fusion.2
  118.8 0.4 broadcast_in_dim.19
  119.2 34.9 %all_to_all.33 = bf16[8,128,1344]{1,2,0:T(8,128)(2,1)S(1)} all-to-all(bf16[8,128,1344]{1,2,0:T(8,128)(2,1)S(1)} %broadcast_in_dim.19), channel_id=1, replica_groups=mesh['row'=8,'cz'=8,'cx'=2,'cc'=2] {'row'}, dimensions={0} | all-to-all | bytes 5505024 | tf_op jit(solution)/shard_map/all_to_all | solution.py:42
  154.1 0.4 copy_bitcast_fusion.1
  154.5 1.3 convolution_convert_fusion
  155.8 1.4 fusion.27
  157.2 1.4 add_convert_fusion
  158.6 0.4 pad_maximum_fusion
  159.1 0.3 copy.45
  159.4 10.8 %all_to_all.34 = bf16[2,512,2048]{1,2,0:T(8,128)(2,1)} all-to-all(bf16[2,512,2048]{1,2,0:T(8,128)(2,1)S(1)} %bitcast.38), channel_id=1, replica_groups=mesh['row'=8,'cz'=8,'cx'=2,'cc'=2] {'cc'}, dimensions={0} | all-to-all | bytes 8388608 | tf_op jit(solution)/shard_map/all_to_all | solution.py:48
  170.2 6.3 %copy.34 = bf16[2,512,2048]{2,1,0:T(8,128)(2,1)} copy(bf16[2,512,2048]{1,2,0:T(8,128)(2,1)} %all_to_all.34) | data formatting | bytes 8388608 | tf_op jit(solution)/shard_map/all_to_all | solution.py:48
  176.5 3.3 %convert_element_type.57 = f32[2,512,2048]{2,1,0:T(8,128)S(1)} convert(bf16[2,512,2048]{2,1,0:T(8,128)(2,1)} %copy.34) | non-fusion elementwise | flops 2097152 | bytes 12582912 | tf_op jit(solution)/shard_map/convert_element_type | solution.py:48
  179.7 2.0 fusion
  181.7 3.7 %all-to-all-start.5 = ((bf16[16,32,2048]{2,1,0:T(8,128)(2,1)}), bf16[16,32,2048]{2,1,0:T(8,128)(2,1)S(1)}, u32[]{:S(2)}, u32[]{:S(2)}) async-start(bf16[16,32,2048]{2,1,0:T(8,128)(2,1)} %bitcast.39), calls=%async_computation.5 | async-start | bytes 4194304 | tf_op jit(solution)/shard_map/all_to_all | solution.py:48
  185.4 4.1 %fusion.8 = bf16[448,1024]{1,0:T(8,128)(2,1)} fusion(bf16[1024,2048]{1,0:T(8,128)(2,1)} %bitcast.44, bf16[1024,1344]{0,1:T(8,128)(2,1)} %copy-done.2), kind=kOutput, calls=%fused_computation.13 | convolution fusion | flops 939982848 | bytes 3932160 | tf_op jit(solution)/shard_map/dot_general | solution.py:125
  189.5 0.0 copy-done.3
  189.5 2.1 convolution_convert_fusion.2
  191.6 2.0 convolution_convert_fusion.1
  193.6 42.5 %all-to-all-done.5 = bf16[16,32,2048]{2,1,0:T(8,128)(2,1)S(1)} async-done(((bf16[16,32,2048]{2,1,0:T(8,128)(2,1)}), bf16[16,32,2048]{2,1,0:T(8,128)(2,1)S(1)}, u32[]{:S(2)}, u32[]{:S(2)}) %all-to-all-start.5) | async-done | bytes 2097184 | tf_op jit(solution)/shard_map/all_to_all | solution.py:48
  236.1 0.5 convert_element_type.60
  236.6 0.2 fusion.32
  236.8 0.7 fusion.33
  237.6 0.0 copy-done.1
  (12 shorter events, 0.1 us)
Async XLA Ops:
  0.6 77.4 %copy-start = (bf16[448,1024]{1,0:T(8,128)(2,1)S(1)}, bf16[448,1024]{1,0:T(8,128)(2,1)}, u32[]{:S(2)}) copy-start(bf16[448,1024]{1,0:T(8,128)(2,1)} %param.15) | copy-start | bytes 2752516
  67.2 9.5 %copy-start.6 = (bf16[1024,448]{0,1:T(8,128)(2,1)S(1)}, bf16[1024,448]{0,1:T(8,128)(2,1)}, u32[]{:S(2)}) copy-start(bf16[1024,448]{0,1:T(8,128)(2,1)} %param.14) | copy-start | bytes 2752516
  76.7 2.7 %copy-start.4 = (bf16[2,512,2048]{2,1,0:T(8,128)(2,1)}, bf16[2,512,2048]{2,1,0:T(8,128)(2,1)S(1)}, u32[]{:S(2)}) copy-start(bf16[2,512,2048]{2,1,0:T(8,128)(2,1)S(1)} %all_to_all.31) | copy-start | bytes 12582916
  78.0 1.4 copy-start.7
  154.5 2.7 %copy-start.2 = (bf16[1024,1344]{0,1:T(8,128)(2,1)}, bf16[1024,1344]{0,1:T(8,128)(2,1)S(1)}, u32[]{:S(2)}) copy-start(bf16[1024,1344]{0,1:T(8,128)(2,1)S(1)} %copy_bitcast_fusion.1) | copy-start | bytes 8257540
  181.7 54.4 %all-to-all-start.5 = ((bf16[16,32,2048]{2,1,0:T(8,128)(2,1)}), bf16[16,32,2048]{2,1,0:T(8,128)(2,1)S(1)}, u32[]{:S(2)}, u32[]{:S(2)}) async-start(bf16[16,32,2048]{2,1,0:T(8,128)(2,1)} %bitcast.39), calls=%async_computation.5 | async-start | bytes 4194304 | tf_op jit(solution)/shard_map/all_to_all | solution.py:48
  185.4 4.1 %copy-start.3 = (bf16[1024,1344]{0,1:T(8,128)(2,1)S(1)}, bf16[1024,1344]{0,1:T(8,128)(2,1)}, u32[]{:S(2)}) copy-start(bf16[1024,1344]{0,1:T(8,128)(2,1)} %copy-done.2) | copy-start | bytes 8257540
  185.4 4.1 %copy-start.5 = (bf16[2,512,2048]{2,1,0:T(8,128)(2,1)S(1)}, bf16[2,512,2048]{2,1,0:T(8,128)(2,1)}, u32[]{:S(2)}) copy-start(bf16[2,512,2048]{2,1,0:T(8,128)(2,1)} %copy-done.4) | copy-start | bytes 12582916
  236.1 1.5 copy-start.1

commit v6 on v3

--- a/solution.py
+++ b/solution.py
@@ -80,13 +80,36 @@
         freq_start,
         freq_width,
     )
-    masked = jnp.where(keep_mask, frames, jnp.zeros_like(frames))
-    cot_valid = jnp.where(valid_rows[:, None], cotangent, jnp.zeros_like(cotangent))
     contract_last = (((1,), (1,)), ((), ()))
     contract_first = (((0,), (0,)), ((), ()))
-    both = jnp.concatenate([masked, cot_valid], axis=1)
-    both_all = gather_by_exchange(
-        gather_by_exchange(both, CHIPS, lax.psum(1, CHIPS)), CORE, lax.psum(1, CORE)
+    n_chips, n_core = lax.psum(1, CHIPS), lax.psum(1, CORE)
+    raw_all = gather_by_exchange(
+        gather_by_exchange(jnp.concatenate([frames, cotangent], axis=1), CHIPS, n_chips),
+        CORE,
+        n_core,
+    )
+    spot = jnp.arange(raw_all.shape[0], dtype=jnp.int32)
+    chunk = n_chips * tok_rows
+    all_index = ((spot % chunk) // tok_rows * n_core + spot // chunk) * tok_rows + spot % tok_rows
+    keep_all, valid_all = span_masks(
+        utt_ids,
+        jnp.take(utt_ids, all_index),
+        all_index,
+        feat_index,
+        valid_len,
+        time_start,
+        time_width,
+        freq_start,
+        freq_width,
+    )
+    both_all = jnp.concatenate(
+        [
+            jnp.where(keep_all, raw_all[:, :feat_cols], jnp.zeros_like(raw_all[:, :feat_cols])),
+            jnp.where(
+                valid_all[:, None], raw_all[:, feat_cols:], jnp.zeros_like(raw_all[:, feat_cols:])
+            ),
+        ],
+        axis=1,
     )
     tokens_all = both_all[:, :feat_cols]
     cot_all = both_all[:, feat_cols:]

time: 233 us -> 234 us (level)
  blocking collectives: 154 us -> 92.6 us
  waiting for transfers between devices: 42.5 us -> 86.2 us
  starting transfers between devices: 3.72 us -> 15.4 us
  local copies, waits for them, and re-layouts: 5.68 us -> 12.5 us
    all_to_all x3 -> x2, blocking collectives: 107 us -> 44.7 us  [gather_by_exchange(): got = lax.all_to_all(spread, axis, 0, 0)]
    all_to_all x0 -> x1, waiting for transfers between devices: none -> 44.9 us  [gather_by_exchange(): got = lax.all_to_all(spread, axis, 0, 0)]
    all_to_all x0 -> x1, starting transfers between devices: none -> 11.6 us  [gather_by_exchange(): got = lax.all_to_all(spread, axis, 0, 0)]
    gather x0 -> x1, local copies, waits for them, and re-layouts: none -> 4.53 us  [shards(): jnp.take(utt_ids, all_index)]
  transfers between devices with their start and end apart: 1 -> 2, of which waited for: 1 -> 2; matrix products, arithmetic and copies ran while one was open for 4% -> 6% of each run, Pallas kernels for 0% -> 0%
where the time goes in v6:
time: 234 us; the launch traced here: 233 us
  blocking collectives  92.6 us (40%)
  waiting for transfers between devices  86.2 us (37%)
  matrix products  15.9 us (7%)
  starting transfers between devices  15.4 us (7%)
  local copies, waits for them, and re-layouts  12.5 us (5%)
  other arithmetic  9.69 us (4%)
    all_to_all x2, blocking collectives, sum_by_exchange(): got = lax.all_to_all(split, axis, 0, 0)  48 us
    all_to_all x1, waiting for transfers between devices, gather_by_exchange(): got = lax.all_to_all(spread, axis, 0, 0)  44.9 us
    all_to_all x2, blocking collectives, gather_by_exchange(): got = lax.all_to_all(spread, axis, 0, 0)  44.7 us
    all_to_all x1, waiting for transfers between devices, sum_by_exchange(): got = lax.all_to_all(split, axis, 0, 0)  41.3 us
    all_to_all x1, starting transfers between devices, gather_by_exchange(): got = lax.all_to_all(spread, axis, 0, 0)  11.6 us
    reduce_sum x3, other arithmetic, sum_by_exchange(): return jnp.sum(got.astype(jnp.float32), axis=0)  5.11 us
  transfers between devices with their start and end apart: 2, of which 2 were waited for; matrix products, arithmetic and copies ran while one was open for 6% of the time, Pallas kernels for 0%

profile of v6, /device:TPU:1, one launch (start us, length us, event | category | flops | bytes accessed | tf_op | source)
XLA Modules:
  0.0 233.4 jit_solution(10666879614744614759)
XLA Ops:
  0.6 0.0 copy-start
  0.6 1.0 pad_maximum_fusion.3
  1.6 0.0 copy-start.2
  1.6 1.6 broadcast_in_dim.20
  3.2 11.6 %all-to-all-start = ((bf16[16,32,2048]{2,1,0:T(8,128)(2,1)}), bf16[16,32,2048]{2,1,0:T(8,128)(2,1)S(1)}, u32[]{:S(2)}, u32[]{:S(2)}) async-start(bf16[16,32,2048]{2,1,0:T(8,128)(2,1)} %broadcast_in_dim.20), calls=%async_computation | async-start | bytes 4194304 | tf_op jit(solution)/shard_map/all_to_all | solution.py:42
  14.8 0.0 copy-start.10
  14.8 0.0 copy-start.11
  14.8 0.0 copy-start.12
  14.9 4.5 %gather_fusion = s32[1024]{0:T(1024)S(1)} fusion(s32[1024]{0:T(1024)S(1)} %copy-done.2, s32[1024]{0:T(1024)S(1)} %broadcast_clamp_fusion), kind=kCustom, calls=%fused_computation | custom fusion | bytes 12288 | tf_op jit(solution)/shard_map/jit(_take)/gather | solution.py:96
  19.5 0.1 convert_reduce_fusion.2
  19.7 0.1 select_reduce_fusion.2
  19.8 44.9 %all-to-all-done = bf16[16,32,2048]{2,1,0:T(8,128)(2,1)S(1)} async-done(((bf16[16,32,2048]{2,1,0:T(8,128)(2,1)}), bf16[16,32,2048]{2,1,0:T(8,128)(2,1)S(1)}, u32[]{:S(2)}, u32[]{:S(2)}) %all-to-all-start) | async-done | bytes 2097184 | tf_op jit(solution)/shard_map/all_to_all | solution.py:42
  64.7 0.7 broadcast_in_dim.22
  65.5 9.8 %all_to_all.30 = bf16[2,512,2048]{2,1,0:T(8,128)(2,1)S(1)} all-to-all(bf16[2,512,2048]{2,1,0:T(8,128)(2,1)S(1)} %broadcast_in_dim.22), channel_id=1, replica_groups=mesh['row'=8,'cz'=8,'cx'=2,'cc'=2] {'cc'}, dimensions={0} | all-to-all | bytes 8388608 | tf_op jit(solution)/shard_map/all_to_all | solution.py:42
  75.2 1.6 and_select_fusion
  76.9 0.2 copy-done.9
  77.1 1.1 fusion.1
  78.2 0.2 copy-done.7
  78.4 0.4 copy-done.15
  78.9 1.2 fusion
  80.0 0.2 copy.54
  80.2 1.3 fusion.2
  81.5 0.4 copy_bitcast_fusion.2
  82.0 0.2 pad_maximum_fusion.1
  82.1 37.1 %all_to_all.31 = bf16[8,128,1344]{1,2,0:T(8,128)(2,1)S(1)} all-to-all(bf16[8,128,1344]{1,2,0:T(8,128)(2,1)S(1)} %pad_maximum_fusion.1), channel_id=1, replica_groups=mesh['row'=8,'cz'=8,'cx'=2,'cc'=2] {'row'}, dimensions={0} | all-to-all | bytes 5505024 | tf_op jit(solution)/shard_map/all_to_all | solution.py:48
  119.2 0.4 convert_reduce_fusion
  119.6 0.1 multiply_convert_fusion.2
  119.8 0.4 broadcast_in_dim.24
  120.2 34.9 %all_to_all.32 = bf16[8,128,1344]{1,2,0:T(8,128)(2,1)S(1)} all-to-all(bf16[8,128,1344]{1,2,0:T(8,128)(2,1)S(1)} %broadcast_in_dim.24), channel_id=1, replica_groups=mesh['row'=8,'cz'=8,'cx'=2,'cc'=2] {'row'}, dimensions={0} | all-to-all | bytes 5505024 | tf_op jit(solution)/shard_map/all_to_all | solution.py:42
  155.1 0.4 copy_bitcast_fusion.1
  155.5 1.3 convolution_convert_fusion
  156.8 1.4 fusion.6
  158.2 1.4 add_convert_fusion
  159.6 0.4 pad_maximum_fusion
  160.1 0.3 copy.53
  160.4 10.9 %all_to_all.33 = bf16[2,512,2048]{1,2,0:T(8,128)(2,1)} all-to-all(bf16[2,512,2048]{1,2,0:T(8,128)(2,1)S(1)} %bitcast.37), channel_id=1, replica_groups=mesh['row'=8,'cz'=8,'cx'=2,'cc'=2] {'cc'}, dimensions={0} | all-to-all | bytes 8388608 | tf_op jit(solution)/shard_map/all_to_all | solution.py:48
  171.3 4.4 %reduce_sum.159 = bf16[512,2048]{0,1:T(8,128)(2,1)S(1)} reduce(bf16[2,512,2048]{1,2,0:T(8,128)(2,1)} %all_to_all.33, bf16[]{:T(256)} %constant.111.clone.1), dimensions={0}, to_apply=%region_8.9 | reduce | flops 1048576 | bytes 6291458 | tf_op jit(solution)/shard_map/reduce_sum | solution.py:49
  175.7 2.5 %copy.37 = bf16[512,2048]{1,0:T(8,128)(2,1)} copy(bf16[512,2048]{0,1:T(8,128)(2,1)S(1)} %reduce_sum.159) | data formatting | bytes 4194304 | tf_op jit(solution)/shard_map/reduce_sum | solution.py:49
  178.2 3.8 %all-to-all-start.5 = ((bf16[16,32,2048]{2,1,0:T(8,128)(2,1)}), bf16[16,32,2048]{2,1,0:T(8,128)(2,1)S(1)}, u32[]{:S(2)}, u32[]{:S(2)}) async-start(bf16[16,32,2048]{2,1,0:T(8,128)(2,1)} %bitcast.42), calls=%async_computation.5 | async-start | bytes 4194304 | tf_op jit(solution)/shard_map/all_to_all | solution.py:48
  182.1 0.1 dynamic_slice.3
  182.2 0.1 select_reduce_fusion.11
  182.3 4.1 %convolution_convert_fusion.2 = bf16[1024,448]{0,1:T(8,128)(2,1)} fusion(bf16[1024,1024]{1,0:T(8,128)(2,1)} %copy-done.7, bf16[1024,1344]{0,1:T(8,128)(2,1)} %copy-done.5), kind=kOutput, calls=%fused_computation.12 | convolution fusion | flops 939982848 | bytes 3932160 | tf_op jit(solution)/shard_map/dot_general | solution.py:148
  186.4 2.1 convolution_convert_fusion.1
  188.4 0.4 copy-done.4
  188.8 2.1 convolution_convert_fusion.3
  191.0 41.3 %all-to-all-done.5 = bf16[16,32,2048]{2,1,0:T(8,128)(2,1)S(1)} async-done(((bf16[16,32,2048]{2,1,0:T(8,128)(2,1)}), bf16[16,32,2048]{2,1,0:T(8,128)(2,1)S(1)}, u32[]{:S(2)}, u32[]{:S(2)}) %all-to-all-start.5) | async-done | bytes 2097184 | tf_op jit(solution)/shard_map/all_to_all | solution.py:48
  232.3 0.3 convert_reduce_fusion.1
  232.6 0.7 fusion.10
  (32 shorter events, 0.2 us)
Async XLA Ops:
  0.6 79.6 %copy-start = (bf16[448,1024]{1,0:T(8,128)(2,1)S(1)}, bf16[448,1024]{1,0:T(8,128)(2,1)}, u32[]{:S(2)}) copy-start(bf16[448,1024]{1,0:T(8,128)(2,1)} %param.15) | copy-start | bytes 2752516
  1.6 13.3 %copy-start.2 = (s32[1024]{0:T(1024)S(1)}, s32[1024]{0:T(1024)}, u32[]{:S(2)}) copy-start(s32[1024]{0:T(1024)} %param.16) | copy-start | bytes 12292
  3.2 61.5 %all-to-all-start = ((bf16[16,32,2048]{2,1,0:T(8,128)(2,1)}), bf16[16,32,2048]{2,1,0:T(8,128)(2,1)S(1)}, u32[]{:S(2)}, u32[]{:S(2)}) async-start(bf16[16,32,2048]{2,1,0:T(8,128)(2,1)} %broadcast_in_dim.20), calls=%async_computation | async-start | bytes 4194304 | tf_op jit(solution)/shard_map/all_to_all | solution.py:42
  14.8 4.8 %copy-start.10 = (s32[16]{0:T(128)S(1)}, s32[16]{0:T(128)}, u32[]{:S(2)}) copy-start(s32[16]{0:T(128)} %param.19) | copy-start | bytes 196
  14.8 4.8 %copy-start.11 = (s32[16]{0:T(128)S(1)}, s32[16]{0:T(128)}, u32[]{:S(2)}) copy-start(s32[16]{0:T(128)} %param.21) | copy-start | bytes 196
  14.8 4.8 %copy-start.12 = (s32[16]{0:T(128)S(1)}, s32[16]{0:T(128)}, u32[]{:S(2)}) copy-start(s32[16]{0:T(128)} %param.20) | copy-start | bytes 196
  14.8 4.8 %copy-start.13 = (s32[16]{0:T(128)S(1)}, s32[16]{0:T(128)}, u32[]{:S(2)}) copy-start(s32[16]{0:T(128)} %param.18) | copy-start | bytes 196
  14.9 4.8 %copy-start.14 = (s32[16]{0:T(128)S(1)}, s32[16]{0:T(128)}, u32[]{:S(2)}) copy-start(s32[16]{0:T(128)} %param.17) | copy-start | bytes 196
  75.2 5.0 %copy-start.3 = (bf16[2,512,2048]{2,1,0:T(8,128)(2,1)}, bf16[2,512,2048]{2,1,0:T(8,128)(2,1)S(1)}, u32[]{:S(2)}) copy-start(bf16[2,512,2048]{2,1,0:T(8,128)(2,1)S(1)} %all_to_all.30) | copy-start | bytes 12582916
  75.2 1.8 copy-start.9
  77.1 1.4 copy-start.7
  77.1 1.8 copy-start.15
  155.5 2.7 %copy-start.5 = (bf16[1024,1344]{0,1:T(8,128)(2,1)}, bf16[1024,1344]{0,1:T(8,128)(2,1)S(1)}, u32[]{:S(2)}) copy-start(bf16[1024,1344]{0,1:T(8,128)(2,1)S(1)} %copy_bitcast_fusion.1) | copy-start | bytes 8257540
  178.2 54.0 %all-to-all-start.5 = ((bf16[16,32,2048]{2,1,0:T(8,128)(2,1)}), bf16[16,32,2048]{2,1,0:T(8,128)(2,1)S(1)}, u32[]{:S(2)}, u32[]{:S(2)}) async-start(bf16[16,32,2048]{2,1,0:T(8,128)(2,1)} %bitcast.42), calls=%async_computation.5 | async-start | bytes 4194304 | tf_op jit(solution)/shard_map/all_to_all | solution.py:48
  182.3 4.1 %copy-start.6 = (bf16[1024,1344]{0,1:T(8,128)(2,1)S(1)}, bf16[1024,1344]{0,1:T(8,128)(2,1)}, u32[]{:S(2)}) copy-start(bf16[1024,1344]{0,1:T(8,128)(2,1)} %copy-done.5) | copy-start | bytes 8257540
  182.3 4.1 %copy-start.8 = (bf16[1024,1024]{1,0:T(8,128)(2,1)S(1)}, bf16[1024,1024]{1,0:T(8,128)(2,1)}, u32[]{:S(2)}) copy-start(bf16[1024,1024]{1,0:T(8,128)(2,1)} %copy-done.7) | copy-start | bytes 6291460
  186.4 2.5 %copy-start.4 = (bf16[2,512,2048]{2,1,0:T(8,128)(2,1)S(1)}, bf16[2,512,2048]{2,1,0:T(8,128)(2,1)}, u32[]{:S(2)}) copy-start(bf16[2,512,2048]{2,1,0:T(8,128)(2,1)} %copy-done.3) | copy-start | bytes 12582916
  188.8 44.5 %copy-start.1 = (bf16[448,1024]{1,0:T(8,128)(2,1)S(1)}, bf16[448,1024]{1,0:T(8,128)(2,1)}, u32[]{:S(2)}) copy-start(bf16[448,1024]{1,0:T(8,128)(2,1)} %param.15) | copy-start | bytes 2752516

commit v7 on v3

--- a/solution.py
+++ b/solution.py
@@ -1,6 +1,7 @@
 import jax
 import jax.numpy as jnp
 from jax import lax
+from jax.experimental.layout import Layout, with_layout_constraint
 from jax.sharding import Mesh, PartitionSpec as P
 
 COL = ("cz", "cx", "cc")
@@ -35,6 +36,10 @@
     in_freq = (feat_index[None, :] >= freq_low) & (feat_index[None, :] < freq_high)
     keep_mask = (valid_rows & jnp.logical_not(in_time))[:, None] & jnp.logical_not(in_freq)
     return (keep_mask, valid_rows)
+
+
+def tokens_major(value):
+    return with_layout_constraint(value, Layout((0, 1)))
 
 
 def gather_by_exchange(part, axis, count):
@@ -130,7 +135,7 @@
     ).astype(jnp.bfloat16)
     out_sums = sum_by_exchange(
         sum_by_exchange(
-            jnp.concatenate(
+            tokens_major(jnp.concatenate(
             [
                 jnp.dot(hidden_all, down_weight, preferred_element_type=jnp.float32).astype(
                     jnp.bfloat16
@@ -145,7 +150,7 @@
                 ).astype(jnp.bfloat16),
             ],
             axis=1,
-        ),
+        )),
             CORE,
             lax.psum(1, CORE),
         ).astype(jnp.bfloat16),

time: 233 us -> 230 us (0.987)
  local copies, waits for them, and re-layouts: 5.68 us -> 2.83 us
    reduce_sum x1 -> x0, local copies, waits for them, and re-layouts: 2.52 us -> none  [sum_by_exchange(): return jnp.sum(got.astype(jnp.float32), axis=0)]
where the time goes in v7:
time: 230 us
  blocking collectives  154 us (67%)
  waiting for transfers between devices  42.3 us (18%)
  matrix products  15.5 us (7%)
  other arithmetic  10.1 us (4%)
  starting transfers between devices  3.9 us (2%)
  local copies, waits for them, and re-layouts  2.83 us (1%)
    all_to_all x3, blocking collectives, gather_by_exchange(): got = lax.all_to_all(spread, axis, 0, 0)  107 us
    all_to_all x2, blocking collectives, sum_by_exchange(): got = lax.all_to_all(split, axis, 0, 0)  47.8 us
    all_to_all x1, waiting for transfers between devices, sum_by_exchange(): got = lax.all_to_all(split, axis, 0, 0)  42.3 us
    reduce_sum x3, other arithmetic, sum_by_exchange(): return jnp.sum(got.astype(jnp.float32), axis=0)  5.84 us
  transfers between devices with their start and end apart: 1, of which 1 were waited for; matrix products, arithmetic and copies ran while one was open for 4% of the time, Pallas kernels for 0%

profile of v7, /device:TPU:1, one launch (start us, length us, event | category | flops | bytes accessed | tf_op | source)
XLA Modules:
  0.0 229.9 jit_solution(7348122992483060759)
XLA Ops:
  0.6 0.0 copy-start
  0.7 0.9 convert_reduce_fusion.2
  1.5 0.8 dynamic_slice.3
  2.3 0.8 select_reduce_fusion.2
  3.2 1.0 broadcast_select_fusion
  4.2 0.2 broadcast_in_dim.16
  4.4 62.3 %all_to_all.30 = bf16[16,32,2048]{2,1,0:T(8,128)(2,1)S(1)} all-to-all(bf16[16,32,2048]{2,1,0:T(8,128)(2,1)S(1)} %broadcast_in_dim.16), channel_id=1, replica_groups=mesh['row'=8,'cz'=8,'cx'=2,'cc'=2] {'cz','cx'}, dimensions={0} | all-to-all | bytes 4194304 | tf_op jit(solution)/shard_map/all_to_all | solution.py:47
  66.7 0.5 broadcast_in_dim.18
  67.2 0.0 copy-start.5
  67.2 9.5 %all_to_all.31 = bf16[2,512,2048]{2,1,0:T(8,128)(2,1)S(1)} all-to-all(bf16[2,512,2048]{2,1,0:T(8,128)(2,1)S(1)} %broadcast_in_dim.18), channel_id=1, replica_groups=mesh['row'=8,'cz'=8,'cx'=2,'cc'=2] {'cc'}, dimensions={0} | all-to-all | bytes 8388608 | tf_op jit(solution)/shard_map/all_to_all | solution.py:47
  76.7 0.0 copy-start.3
  76.7 0.0 copy-done.5
  76.7 1.1 fusion.17
  77.9 0.2 copy.58
  78.0 0.0 copy-done
  78.0 0.0 copy-start.6
  78.0 1.2 fusion.20
  79.2 0.2 copy.57
  79.4 0.0 copy-done.3
  79.4 0.0 copy-done.6
  79.4 1.2 fusion.14
  80.6 0.2 copy.59
  80.8 0.2 pad_maximum_fusion.1
  80.9 37.1 %all_to_all.32 = bf16[8,128,1344]{1,2,0:T(8,128)(2,1)S(1)} all-to-all(bf16[8,128,1344]{1,2,0:T(8,128)(2,1)S(1)} %pad_maximum_fusion.1), channel_id=1, replica_groups=mesh['row'=8,'cz'=8,'cx'=2,'cc'=2] {'row'}, dimensions={0} | all-to-all | bytes 5505024 | tf_op jit(solution)/shard_map/all_to_all | solution.py:53
  118.0 0.4 convert_reduce_fusion
  118.4 0.1 multiply_convert_fusion.2
  118.6 0.4 broadcast_in_dim.19
  119.0 34.9 %all_to_all.33 = bf16[8,128,1344]{1,2,0:T(8,128)(2,1)S(1)} all-to-all(bf16[8,128,1344]{1,2,0:T(8,128)(2,1)S(1)} %broadcast_in_dim.19), channel_id=1, replica_groups=mesh['row'=8,'cz'=8,'cx'=2,'cc'=2] {'row'}, dimensions={0} | all-to-all | bytes 5505024 | tf_op jit(solution)/shard_map/all_to_all | solution.py:47
  153.9 0.4 copy_bitcast_fusion
  154.3 0.0 copy-start.1
  154.3 1.3 convolution_convert_fusion
  155.6 1.3 fusion.26
  156.9 0.0 copy-done.1
  156.9 1.3 add_convert_fusion
  158.2 0.4 pad_maximum_fusion
  158.7 10.7 %all_to_all.34 = bf16[2,512,2048]{2,1,0:T(8,128)(2,1)} all-to-all(bf16[2,512,2048]{2,1,0:T(8,128)(2,1)S(1)} %bitcast.30), channel_id=1, replica_groups=mesh['row'=8,'cz'=8,'cx'=2,'cc'=2] {'cc'}, dimensions={0} | all-to-all | bytes 8388608 | tf_op jit(solution)/shard_map/all_to_all | solution.py:53
  169.4 5.1 %reduce_sum.101 = bf16[512,2048]{1,0:T(8,128)(2,1)} reduce(bf16[2,512,2048]{2,1,0:T(8,128)(2,1)} %all_to_all.34, bf16[]{:T(256)} %constant.37.clone.1), dimensions={0}, to_apply=%region_8.9 | reduce | flops 1048576 | bytes 6291458 | tf_op jit(solution)/shard_map/reduce_sum | solution.py:54
  174.5 3.9 %all-to-all-start.5 = ((bf16[16,32,2048]{2,1,0:T(8,128)(2,1)}), bf16[16,32,2048]{2,1,0:T(8,128)(2,1)S(1)}, u32[]{:S(2)}, u32[]{:S(2)}) async-start(bf16[16,32,2048]{2,1,0:T(8,128)(2,1)} %bitcast.3), calls=%async_computation.5 | async-start | bytes 4194304 | tf_op jit(solution)/shard_map/all_to_all | solution.py:53
  178.4 0.0 copy-start.2
  178.4 0.0 copy-start.4
  178.4 4.1 %fusion.7 = bf16[448,1024]{1,0:T(8,128)(2,1)} fusion(bf16[1024,2048]{1,0:T(8,128)(2,1)} %bitcast.35, bf16[1024,1344]{0,1:T(8,128)(2,1)} %copy-done.1), kind=kOutput, calls=%fused_computation.12 | convolution fusion | flops 939982848 | bytes 3932160 | tf_op jit(solution)/shard_map/dot_general | solution.py:127
  182.5 0.0 copy-done.2
  182.5 0.0 copy-done.4
  182.5 2.1 convolution_convert_fusion.2
  184.6 2.0 convolution_convert_fusion.1
  186.6 42.3 %all-to-all-done.5 = bf16[16,32,2048]{2,1,0:T(8,128)(2,1)S(1)} async-done(((bf16[16,32,2048]{2,1,0:T(8,128)(2,1)}), bf16[16,32,2048]{2,1,0:T(8,128)(2,1)S(1)}, u32[]{:S(2)}, u32[]{:S(2)}) %all-to-all-start.5) | async-done | bytes 2097184 | tf_op jit(solution)/shard_map/all_to_all | solution.py:53
  228.9 0.3 convert_reduce_fusion.1
  229.2 0.7 fusion.30
  (5 shorter events, 0.1 us)
Async XLA Ops:
  0.6 77.4 %copy-start = (bf16[448,1024]{1,0:T(8,128)(2,1)S(1)}, bf16[448,1024]{1,0:T(8,128)(2,1)}, u32[]{:S(2)}) copy-start(bf16[448,1024]{1,0:T(8,128)(2,1)} %param.15) | copy-start | bytes 2752516
  67.2 9.5 %copy-start.5 = (bf16[1024,448]{0,1:T(8,128)(2,1)S(1)}, bf16[1024,448]{0,1:T(8,128)(2,1)}, u32[]{:S(2)}) copy-start(bf16[1024,448]{0,1:T(8,128)(2,1)} %param.14) | copy-start | bytes 2752516
  76.7 2.7 %copy-start.3 = (bf16[2,512,2048]{2,1,0:T(8,128)(2,1)}, bf16[2,512,2048]{2,1,0:T(8,128)(2,1)S(1)}, u32[]{:S(2)}) copy-start(bf16[2,512,2048]{2,1,0:T(8,128)(2,1)S(1)} %all_to_all.31) | copy-start | bytes 12582916
  78.0 1.4 copy-start.6
  154.3 2.6 %copy-start.1 = (bf16[1024,1344]{0,1:T(8,128)(2,1)}, bf16[1024,1344]{0,1:T(8,128)(2,1)S(1)}, u32[]{:S(2)}) copy-start(bf16[1024,1344]{0,1:T(8,128)(2,1)S(1)} %copy_bitcast_fusion) | copy-start | bytes 8257540
  174.5 54.4 %all-to-all-start.5 = ((bf16[16,32,2048]{2,1,0:T(8,128)(2,1)}), bf16[16,32,2048]{2,1,0:T(8,128)(2,1)S(1)}, u32[]{:S(2)}, u32[]{:S(2)}) async-start(bf16[16,32,2048]{2,1,0:T(8,128)(2,1)} %bitcast.3), calls=%async_computation.5 | async-start | bytes 4194304 | tf_op jit(solution)/shard_map/all_to_all | solution.py:53
  178.4 4.1 %copy-start.2 = (bf16[1024,1344]{0,1:T(8,128)(2,1)S(1)}, bf16[1024,1344]{0,1:T(8,128)(2,1)}, u32[]{:S(2)}) copy-start(bf16[1024,1344]{0,1:T(8,128)(2,1)} %copy-done.1) | copy-start | bytes 8257540
  178.4 4.1 %copy-start.4 = (bf16[2,512,2048]{2,1,0:T(8,128)(2,1)S(1)}, bf16[2,512,2048]{2,1,0:T(8,128)(2,1)}, u32[]{:S(2)}) copy-start(bf16[2,512,2048]{2,1,0:T(8,128)(2,1)} %copy-done.3) | copy-start | bytes 12582916

commit v8 on v7

--- a/solution.py
+++ b/solution.py
@@ -51,7 +51,9 @@
 def sum_by_exchange(partial, axis, count):
     split = partial.reshape((count, partial.shape[0] // count) + partial.shape[1:])
     got = lax.all_to_all(split, axis, 0, 0)
-    return jnp.sum(got.astype(jnp.float32), axis=0)
+    if count > 2:
+        return jnp.sum(got.astype(jnp.float32), axis=0)
+    return got[0].astype(jnp.float32) + got[1].astype(jnp.float32)
 
 
 def shards(

time: 230 us -> 226 us (0.983)
  other arithmetic: 10.1 us -> 7.17 us
    reduce_sum x3 -> x2, other arithmetic: 5.84 us -> 0.72 us  [sum_by_exchange(): return jnp.sum(got.astype(jnp.float32), axis=0)]
where the time goes in v8:
time: 226 us
  blocking collectives  153 us (68%)
  waiting for transfers between devices  42.1 us (19%)
  matrix products  15.5 us (7%)
  other arithmetic  7.17 us (3%)
  starting transfers between devices  3.9 us (2%)
  local copies, waits for them, and re-layouts  2.83 us (1%)
    all_to_all x3, blocking collectives, gather_by_exchange(): got = lax.all_to_all(spread, axis, 0, 0)  107 us
    all_to_all x2, blocking collectives, sum_by_exchange(): got = lax.all_to_all(split, axis, 0, 0)  46.7 us
    all_to_all x1, waiting for transfers between devices, sum_by_exchange(): got = lax.all_to_all(split, axis, 0, 0)  42.1 us
  transfers between devices with their start and end apart: 1, of which 1 were waited for; matrix products, arithmetic and copies ran while one was open for 4% of the time, Pallas kernels for 0%

profile of v8, /device:TPU:1, one launch (start us, length us, event | category | flops | bytes accessed | tf_op | source)
XLA Modules:
  0.0 225.8 jit_solution(6418253357798554151)
XLA Ops:
  0.6 0.0 copy-start
  0.7 0.9 convert_reduce_fusion.2
  1.5 0.8 dynamic_slice.3
  2.3 0.8 select_reduce_fusion.2
  3.2 1.0 broadcast_select_fusion
  4.2 0.2 broadcast_in_dim.16
  4.4 62.3 %all_to_all.30 = bf16[16,32,2048]{2,1,0:T(8,128)(2,1)S(1)} all-to-all(bf16[16,32,2048]{2,1,0:T(8,128)(2,1)S(1)} %broadcast_in_dim.16), channel_id=1, replica_groups=mesh['row'=8,'cz'=8,'cx'=2,'cc'=2] {'cz','cx'}, dimensions={0} | all-to-all | bytes 4194304 | tf_op jit(solution)/shard_map/all_to_all | solution.py:47
  66.7 0.5 broadcast_in_dim.18
  67.2 0.0 copy-start.5
  67.2 9.5 %all_to_all.31 = bf16[2,512,2048]{2,1,0:T(8,128)(2,1)S(1)} all-to-all(bf16[2,512,2048]{2,1,0:T(8,128)(2,1)S(1)} %broadcast_in_dim.18), channel_id=1, replica_groups=mesh['row'=8,'cz'=8,'cx'=2,'cc'=2] {'cc'}, dimensions={0} | all-to-all | bytes 8388608 | tf_op jit(solution)/shard_map/all_to_all | solution.py:47
  76.7 0.0 copy-start.3
  76.7 0.0 copy-done.5
  76.7 1.1 fusion.17
  77.9 0.2 copy.58
  78.0 0.0 copy-done
  78.0 0.0 copy-start.6
  78.0 1.2 fusion.20
  79.2 0.2 copy.57
  79.4 0.0 copy-done.3
  79.4 0.0 copy-done.6
  79.4 1.2 fusion.14
  80.6 0.2 copy.59
  80.8 0.2 pad_maximum_fusion.1
  80.9 37.1 %all_to_all.32 = bf16[8,128,1344]{1,2,0:T(8,128)(2,1)S(1)} all-to-all(bf16[8,128,1344]{1,2,0:T(8,128)(2,1)S(1)} %pad_maximum_fusion.1), channel_id=1, replica_groups=mesh['row'=8,'cz'=8,'cx'=2,'cc'=2] {'row'}, dimensions={0} | all-to-all | bytes 5505024 | tf_op jit(solution)/shard_map/all_to_all | solution.py:53
  118.0 0.4 convert_reduce_fusion
  118.4 0.1 multiply_convert_fusion.2
  118.6 0.4 broadcast_in_dim.19
  119.0 34.9 %all_to_all.33 = bf16[8,128,1344]{1,2,0:T(8,128)(2,1)S(1)} all-to-all(bf16[8,128,1344]{1,2,0:T(8,128)(2,1)S(1)} %broadcast_in_dim.19), channel_id=1, replica_groups=mesh['row'=8,'cz'=8,'cx'=2,'cc'=2] {'row'}, dimensions={0} | all-to-all | bytes 5505024 | tf_op jit(solution)/shard_map/all_to_all | solution.py:47
  153.9 0.4 copy_bitcast_fusion
  154.3 0.0 copy-start.1
  154.3 1.3 convolution_convert_fusion
  155.6 1.3 fusion.26
  156.9 0.0 copy-done.1
  156.9 1.3 add_convert_fusion.1
  158.2 0.4 pad_maximum_fusion
  158.7 9.7 %all_to_all.34 = bf16[2,512,2048]{2,1,0:T(8,128)(2,1)S(1)} all-to-all(bf16[2,512,2048]{2,1,0:T(8,128)(2,1)S(1)} %bitcast.30), channel_id=1, replica_groups=mesh['row'=8,'cz'=8,'cx'=2,'cc'=2] {'cc'}, dimensions={0} | all-to-all | bytes 8388608 | tf_op jit(solution)/shard_map/all_to_all | solution.py:53
  168.3 2.2 add_convert_fusion
  170.5 3.9 %all-to-all-start.5 = ((bf16[16,32,2048]{2,1,0:T(8,128)(2,1)}), bf16[16,32,2048]{2,1,0:T(8,128)(2,1)S(1)}, u32[]{:S(2)}, u32[]{:S(2)}) async-start(bf16[16,32,2048]{2,1,0:T(8,128)(2,1)} %bitcast.3), calls=%async_computation.5 | async-start | bytes 4194304 | tf_op jit(solution)/shard_map/all_to_all | solution.py:53
  174.5 0.0 copy-start.2
  174.5 0.0 copy-start.4
  174.5 4.1 %fusion.7 = bf16[448,1024]{1,0:T(8,128)(2,1)} fusion(bf16[1024,2048]{1,0:T(8,128)(2,1)} %bitcast.35, bf16[1024,1344]{0,1:T(8,128)(2,1)} %copy-done.1), kind=kOutput, calls=%fused_computation.13 | convolution fusion | flops 939982848 | bytes 3932160 | tf_op jit(solution)/shard_map/dot_general | solution.py:129
  178.5 0.0 copy-done.2
  178.5 0.0 copy-done.4
  178.5 2.1 convolution_convert_fusion.2
  180.6 2.0 convolution_convert_fusion.1
  182.6 42.1 %all-to-all-done.5 = bf16[16,32,2048]{2,1,0:T(8,128)(2,1)S(1)} async-done(((bf16[16,32,2048]{2,1,0:T(8,128)(2,1)}), bf16[16,32,2048]{2,1,0:T(8,128)(2,1)S(1)}, u32[]{:S(2)}, u32[]{:S(2)}) %all-to-all-start.5) | async-done | bytes 2097184 | tf_op jit(solution)/shard_map/all_to_all | solution.py:53
  224.7 0.3 convert_reduce_fusion.1
  225.0 0.7 fusion.30
  (5 shorter events, 0.1 us)
Async XLA Ops:
  0.6 77.4 %copy-start = (bf16[448,1024]{1,0:T(8,128)(2,1)S(1)}, bf16[448,1024]{1,0:T(8,128)(2,1)}, u32[]{:S(2)}) copy-start(bf16[448,1024]{1,0:T(8,128)(2,1)} %param.15) | copy-start | bytes 2752516
  67.2 9.5 %copy-start.5 = (bf16[1024,448]{0,1:T(8,128)(2,1)S(1)}, bf16[1024,448]{0,1:T(8,128)(2,1)}, u32[]{:S(2)}) copy-start(bf16[1024,448]{0,1:T(8,128)(2,1)} %param.14) | copy-start | bytes 2752516
  76.7 2.7 %copy-start.3 = (bf16[2,512,2048]{2,1,0:T(8,128)(2,1)}, bf16[2,512,2048]{2,1,0:T(8,128)(2,1)S(1)}, u32[]{:S(2)}) copy-start(bf16[2,512,2048]{2,1,0:T(8,128)(2,1)S(1)} %all_to_all.31) | copy-start | bytes 12582916
  78.0 1.4 copy-start.6
  154.3 2.6 %copy-start.1 = (bf16[1024,1344]{0,1:T(8,128)(2,1)}, bf16[1024,1344]{0,1:T(8,128)(2,1)S(1)}, u32[]{:S(2)}) copy-start(bf16[1024,1344]{0,1:T(8,128)(2,1)S(1)} %copy_bitcast_fusion) | copy-start | bytes 8257540
  170.5 54.2 %all-to-all-start.5 = ((bf16[16,32,2048]{2,1,0:T(8,128)(2,1)}), bf16[16,32,2048]{2,1,0:T(8,128)(2,1)S(1)}, u32[]{:S(2)}, u32[]{:S(2)}) async-start(bf16[16,32,2048]{2,1,0:T(8,128)(2,1)} %bitcast.3), calls=%async_computation.5 | async-start | bytes 4194304 | tf_op jit(solution)/shard_map/all_to_all | solution.py:53
  174.5 4.1 %copy-start.2 = (bf16[1024,1344]{0,1:T(8,128)(2,1)S(1)}, bf16[1024,1344]{0,1:T(8,128)(2,1)}, u32[]{:S(2)}) copy-start(bf16[1024,1344]{0,1:T(8,128)(2,1)} %copy-done.1) | copy-start | bytes 8257540
  174.5 4.1 %copy-start.4 = (bf16[2,512,2048]{2,1,0:T(8,128)(2,1)S(1)}, bf16[2,512,2048]{2,1,0:T(8,128)(2,1)}, u32[]{:S(2)}) copy-start(bf16[2,512,2048]{2,1,0:T(8,128)(2,1)} %copy-done.3) | copy-start | bytes 12582916

commit v9 on v4

--- a/solution.py
+++ b/solution.py
@@ -1,12 +1,12 @@
 import jax
 import jax.numpy as jnp
 from jax import lax
+from jax.experimental.layout import Layout, with_layout_constraint
 from jax.sharding import Mesh, PartitionSpec as P
 
 COL = ("cz", "cx", "cc")
 CHIPS = ("cz", "cx")
 CORE = "cc"
-LEVELS = ("cz", "cx", "cc")
 
 
 def span_masks(
@@ -38,6 +38,10 @@
     return (keep_mask, valid_rows)
 
 
+def tokens_major(value):
+    return with_layout_constraint(value, Layout((0, 1)))
+
+
 def gather_by_exchange(part, axis, count):
     spread = jnp.broadcast_to(part[None], (count,) + part.shape)
     got = lax.all_to_all(spread, axis, 0, 0)
@@ -47,7 +51,9 @@
 def sum_by_exchange(partial, axis, count):
     split = partial.reshape((count, partial.shape[0] // count) + partial.shape[1:])
     got = lax.all_to_all(split, axis, 0, 0)
-    return jnp.sum(got.astype(jnp.float32), axis=0)
+    if count > 2:
+        return jnp.sum(got.astype(jnp.float32), axis=0)
+    return got[0].astype(jnp.float32) + got[1].astype(jnp.float32)
 
 
 def shards(
@@ -85,9 +91,10 @@
     cot_valid = jnp.where(valid_rows[:, None], cotangent, jnp.zeros_like(cotangent))
     contract_last = (((1,), (1,)), ((), ()))
     contract_first = (((0,), (0,)), ((), ()))
-    both_all = jnp.concatenate([masked, cot_valid], axis=1)
-    for level in LEVELS:
-        both_all = gather_by_exchange(both_all, level, lax.psum(1, level))
+    both = jnp.concatenate([masked, cot_valid], axis=1)
+    both_all = gather_by_exchange(
+        gather_by_exchange(both, CHIPS, lax.psum(1, CHIPS)), CORE, lax.psum(1, CORE)
+    )
     tokens_all = both_all[:, :feat_cols]
     cot_all = both_all[:, feat_cols:]
     sums = sum_by_exchange(
@@ -128,7 +135,7 @@
     grad_up = lax.dot_general(
         tokens_all, dup_all, contract_first, preferred_element_type=jnp.float32
     ).astype(jnp.bfloat16)
-    out_sums = jnp.concatenate(
+    out_partial = jnp.concatenate(
         [
             jnp.dot(hidden_all, down_weight, preferred_element_type=jnp.float32).astype(
                 jnp.bfloat16
@@ -144,10 +151,8 @@
         ],
         axis=1,
     )
-    for level in reversed(LEVELS):
-        if level != LEVELS[-1]:
-            out_sums = out_sums.astype(jnp.bfloat16)
-        out_sums = sum_by_exchange(out_sums, level, lax.psum(1, level))
+    chip_sums = sum_by_exchange(tokens_major(out_partial), CORE, lax.psum(1, CORE))
+    out_sums = sum_by_exchange(chip_sums.astype(jnp.bfloat16), CHIPS, lax.psum(1, CHIPS))
     output = out_sums[:, :feat_cols].astype(jnp.bfloat16)
     grad_masked = out_sums[:, feat_cols:]
     grad_frames = jnp.where(keep_mask, grad_masked, jnp.zeros_like(grad_masked)).astype(

time: 244 us -> 226 us (0.926)
  blocking collectives: 186 us -> 153 us
  waiting for transfers between devices: 20.9 us -> 42.1 us
  other arithmetic: 10.9 us -> 7.17 us
  local copies, waits for them, and re-layouts: 5.71 us -> 2.83 us
    all_to_all x3 -> x2, blocking collectives: 76.5 us -> 46.7 us  [sum_by_exchange(): got = lax.all_to_all(split, axis, 0, 0)]
    all_to_all x1, waiting for transfers between devices: 20.9 us -> 42.1 us  [sum_by_exchange(): got = lax.all_to_all(split, axis, 0, 0)]
    reduce_sum x4 -> x2, other arithmetic: 6.61 us -> 0.72 us  [sum_by_exchange(): return jnp.sum(got.astype(jnp.float32), axis=0)]
    all_to_all x4 -> x3, blocking collectives: 109 us -> 107 us  [gather_by_exchange(): got = lax.all_to_all(spread, axis, 0, 0)]
  transfers between devices with their start and end apart: 1 -> 1, of which waited for: 1 -> 1; matrix products, arithmetic and copies ran while one was open for 3% -> 4% of each run, Pallas kernels for 0% -> 0%
where the time goes in v9:
time: 226 us
  blocking collectives  153 us (68%)
  waiting for transfers between devices  42.1 us (19%)
  matrix products  15.5 us (7%)
  other arithmetic  7.17 us (3%)
  starting transfers between devices  3.9 us (2%)
  local copies, waits for them, and re-layouts  2.83 us (1%)
    all_to_all x3, blocking collectives, gather_by_exchange(): got = lax.all_to_all(spread, axis, 0, 0)  107 us
    all_to_all x2, blocking collectives, sum_by_exchange(): got = lax.all_to_all(split, axis, 0, 0)  46.7 us
    all_to_all x1, waiting for transfers between devices, sum_by_exchange(): got = lax.all_to_all(split, axis, 0, 0)  42.1 us
  transfers between devices with their start and end apart: 1, of which 1 were waited for; matrix products, arithmetic and copies ran while one was open for 4% of the time, Pallas kernels for 0%

profile of v9, /device:TPU:1, one launch (start us, length us, event | category | flops | bytes accessed | tf_op | source)
XLA Modules:
  0.0 225.8 jit_solution(6418253357798554151)
XLA Ops:
  0.6 0.0 copy-start
  0.7 0.9 convert_reduce_fusion.2
  1.5 0.8 dynamic_slice.3
  2.3 0.8 select_reduce_fusion.2
  3.2 1.0 broadcast_select_fusion
  4.2 0.2 broadcast_in_dim.16
  4.4 62.3 %all_to_all.30 = bf16[16,32,2048]{2,1,0:T(8,128)(2,1)S(1)} all-to-all(bf16[16,32,2048]{2,1,0:T(8,128)(2,1)S(1)} %broadcast_in_dim.16), channel_id=1, replica_groups=mesh['row'=8,'cz'=8,'cx'=2,'cc'=2] {'cz','cx'}, dimensions={0} | all-to-all | bytes 4194304 | tf_op jit(solution)/shard_map/all_to_all | solution.py:47
  66.7 0.5 broadcast_in_dim.18
  67.2 0.0 copy-start.5
  67.2 9.5 %all_to_all.31 = bf16[2,512,2048]{2,1,0:T(8,128)(2,1)S(1)} all-to-all(bf16[2,512,2048]{2,1,0:T(8,128)(2,1)S(1)} %broadcast_in_dim.18), channel_id=1, replica_groups=mesh['row'=8,'cz'=8,'cx'=2,'cc'=2] {'cc'}, dimensions={0} | all-to-all | bytes 8388608 | tf_op jit(solution)/shard_map/all_to_all | solution.py:47
  76.7 0.0 copy-start.3
  76.7 0.0 copy-done.5
  76.7 1.1 fusion.17
  77.9 0.2 copy.58
  78.0 0.0 copy-done
  78.0 0.0 copy-start.6
  78.0 1.2 fusion.20
  79.2 0.2 copy.57
  79.4 0.0 copy-done.3
  79.4 0.0 copy-done.6
  79.4 1.2 fusion.14
  80.6 0.2 copy.59
  80.8 0.2 pad_maximum_fusion.1
  80.9 37.1 %all_to_all.32 = bf16[8,128,1344]{1,2,0:T(8,128)(2,1)S(1)} all-to-all(bf16[8,128,1344]{1,2,0:T(8,128)(2,1)S(1)} %pad_maximum_fusion.1), channel_id=1, replica_groups=mesh['row'=8,'cz'=8,'cx'=2,'cc'=2] {'row'}, dimensions={0} | all-to-all | bytes 5505024 | tf_op jit(solution)/shard_map/all_to_all | solution.py:53
  118.0 0.4 convert_reduce_fusion
  118.4 0.1 multiply_convert_fusion.2
  118.6 0.4 broadcast_in_dim.19
  119.0 34.9 %all_to_all.33 = bf16[8,128,1344]{1,2,0:T(8,128)(2,1)S(1)} all-to-all(bf16[8,128,1344]{1,2,0:T(8,128)(2,1)S(1)} %broadcast_in_dim.19), channel_id=1, replica_groups=mesh['row'=8,'cz'=8,'cx'=2,'cc'=2] {'row'}, dimensions={0} | all-to-all | bytes 5505024 | tf_op jit(solution)/shard_map/all_to_all | solution.py:47
  153.9 0.4 copy_bitcast_fusion
  154.3 0.0 copy-start.1
  154.3 1.3 convolution_convert_fusion
  155.6 1.3 fusion.26
  156.9 0.0 copy-done.1
  156.9 1.3 add_convert_fusion.1
  158.2 0.4 pad_maximum_fusion
  158.7 9.7 %all_to_all.34 = bf16[2,512,2048]{2,1,0:T(8,128)(2,1)S(1)} all-to-all(bf16[2,512,2048]{2,1,0:T(8,128)(2,1)S(1)} %bitcast.30), channel_id=1, replica_groups=mesh['row'=8,'cz'=8,'cx'=2,'cc'=2] {'cc'}, dimensions={0} | all-to-all | bytes 8388608 | tf_op jit(solution)/shard_map/all_to_all | solution.py:53
  168.3 2.2 add_convert_fusion
  170.5 3.9 %all-to-all-start.5 = ((bf16[16,32,2048]{2,1,0:T(8,128)(2,1)}), bf16[16,32,2048]{2,1,0:T(8,128)(2,1)S(1)}, u32[]{:S(2)}, u32[]{:S(2)}) async-start(bf16[16,32,2048]{2,1,0:T(8,128)(2,1)} %bitcast.3), calls=%async_computation.5 | async-start | bytes 4194304 | tf_op jit(solution)/shard_map/all_to_all | solution.py:53
  174.5 0.0 copy-start.2
  174.5 0.0 copy-start.4
  174.5 4.1 %fusion.7 = bf16[448,1024]{1,0:T(8,128)(2,1)} fusion(bf16[1024,2048]{1,0:T(8,128)(2,1)} %bitcast.35, bf16[1024,1344]{0,1:T(8,128)(2,1)} %copy-done.1), kind=kOutput, calls=%fused_computation.13 | convolution fusion | flops 939982848 | bytes 3932160 | tf_op jit(solution)/shard_map/dot_general | solution.py:129
  178.5 0.0 copy-done.2
  178.5 0.0 copy-done.4
  178.5 2.1 convolution_convert_fusion.2
  180.6 2.0 convolution_convert_fusion.1
  182.6 42.1 %all-to-all-done.5 = bf16[16,32,2048]{2,1,0:T(8,128)(2,1)S(1)} async-done(((bf16[16,32,2048]{2,1,0:T(8,128)(2,1)}), bf16[16,32,2048]{2,1,0:T(8,128)(2,1)S(1)}, u32[]{:S(2)}, u32[]{:S(2)}) %all-to-all-start.5) | async-done | bytes 2097184 | tf_op jit(solution)/shard_map/all_to_all | solution.py:53
  224.7 0.3 convert_reduce_fusion.1
  225.0 0.7 fusion.30
  (5 shorter events, 0.1 us)
Async XLA Ops:
  0.6 77.4 %copy-start = (bf16[448,1024]{1,0:T(8,128)(2,1)S(1)}, bf16[448,1024]{1,0:T(8,128)(2,1)}, u32[]{:S(2)}) copy-start(bf16[448,1024]{1,0:T(8,128)(2,1)} %param.15) | copy-start | bytes 2752516
  67.2 9.5 %copy-start.5 = (bf16[1024,448]{0,1:T(8,128)(2,1)S(1)}, bf16[1024,448]{0,1:T(8,128)(2,1)}, u32[]{:S(2)}) copy-start(bf16[1024,448]{0,1:T(8,128)(2,1)} %param.14) | copy-start | bytes 2752516
  76.7 2.7 %copy-start.3 = (bf16[2,512,2048]{2,1,0:T(8,128)(2,1)}, bf16[2,512,2048]{2,1,0:T(8,128)(2,1)S(1)}, u32[]{:S(2)}) copy-start(bf16[2,512,2048]{2,1,0:T(8,128)(2,1)S(1)} %all_to_all.31) | copy-start | bytes 12582916
  78.0 1.4 copy-start.6
  154.3 2.6 %copy-start.1 = (bf16[1024,1344]{0,1:T(8,128)(2,1)}, bf16[1024,1344]{0,1:T(8,128)(2,1)S(1)}, u32[]{:S(2)}) copy-start(bf16[1024,1344]{0,1:T(8,128)(2,1)S(1)} %copy_bitcast_fusion) | copy-start | bytes 8257540
  170.5 54.2 %all-to-all-start.5 = ((bf16[16,32,2048]{2,1,0:T(8,128)(2,1)}), bf16[16,32,2048]{2,1,0:T(8,128)(2,1)S(1)}, u32[]{:S(2)}, u32[]{:S(2)}) async-start(bf16[16,32,2048]{2,1,0:T(8,128)(2,1)} %bitcast.3), calls=%async_computation.5 | async-start | bytes 4194304 | tf_op jit(solution)/shard_map/all_to_all | solution.py:53
  174.5 4.1 %copy-start.2 = (bf16[1024,1344]{0,1:T(8,128)(2,1)S(1)}, bf16[1024,1344]{0,1:T(8,128)(2,1)}, u32[]{:S(2)}) copy-start(bf16[1024,1344]{0,1:T(8,128)(2,1)} %copy-done.1) | copy-start | bytes 8257540
  174.5 4.1 %copy-start.4 = (bf16[2,512,2048]{2,1,0:T(8,128)(2,1)S(1)}, bf16[2,512,2048]{2,1,0:T(8,128)(2,1)}, u32[]{:S(2)}) copy-start(bf16[2,512,2048]{2,1,0:T(8,128)(2,1)} %copy-done.3) | copy-start | bytes 12582916

commit v10 on v9

--- a/solution.py
+++ b/solution.py
@@ -11,7 +11,6 @@
 
 def span_masks(
     utt_ids,
-    local_ids,
     tok_index,
     feat_index,
     valid_len,
@@ -22,7 +21,10 @@
 ):
     utt_index = jnp.arange(valid_len.shape[0], dtype=jnp.int32)
     starts = jnp.sum((utt_ids[None, :] < utt_index[:, None]).astype(jnp.int32), axis=1)
-    member = (local_ids[:, None] == utt_index[None, :]).astype(jnp.int32)
+    ends = jnp.sum((utt_ids[None, :] <= utt_index[:, None]).astype(jnp.int32), axis=1)
+    member = (
+        (tok_index[:, None] >= starts[None, :]) & (tok_index[:, None] < ends[None, :])
+    ).astype(jnp.int32)
 
     def lookup(table):
         return jnp.sum(member * table[None, :], axis=1)
@@ -75,10 +77,8 @@
     first_feat = lax.axis_index("row") * feat_cols
     tok_index = first_tok + jnp.arange(tok_rows, dtype=jnp.int32)
     feat_index = first_feat + jnp.arange(feat_cols, dtype=jnp.int32)
-    local_ids = lax.dynamic_slice_in_dim(utt_ids, first_tok, tok_rows)
     keep_mask, valid_rows = span_masks(
         utt_ids,
-        local_ids,
         tok_index,
         feat_index,
         valid_len,

time: 226 us -> 225 us (level)
  no operation moved by 1% of the time
where the time goes in v10:
time: 225 us
  blocking collectives  153 us (68%)
  waiting for transfers between devices  42.1 us (19%)
  matrix products  15.5 us (7%)
  other arithmetic  7.18 us (3%)
  starting transfers between devices  3.9 us (2%)
    all_to_all x3, blocking collectives, gather_by_exchange(): got = lax.all_to_all(spread, axis, 0, 0)  107 us
    all_to_all x2, blocking collectives, sum_by_exchange(): got = lax.all_to_all(split, axis, 0, 0)  46.7 us
    all_to_all x1, waiting for transfers between devices, sum_by_exchange(): got = lax.all_to_all(split, axis, 0, 0)  42.1 us
  transfers between devices with their start and end apart: 1, of which 1 were waited for; matrix products, arithmetic and copies ran while one was open for 4% of the time, Pallas kernels for 0%

profile of v10, /device:TPU:1, one launch (start us, length us, event | category | flops | bytes accessed | tf_op | source)
XLA Modules:
  0.0 225.1 jit_solution(4600141931290606210)
XLA Ops:
  0.6 0.0 copy-start
  0.7 0.9 convert_reduce_fusion.3
  1.6 0.8 select_reduce_fusion.2
  2.4 1.0 broadcast_select_fusion
  3.4 0.2 broadcast_in_dim.16
  3.7 62.3 %all_to_all.30 = bf16[16,32,2048]{2,1,0:T(8,128)(2,1)S(1)} all-to-all(bf16[16,32,2048]{2,1,0:T(8,128)(2,1)S(1)} %broadcast_in_dim.16), channel_id=1, replica_groups=mesh['row'=8,'cz'=8,'cx'=2,'cc'=2] {'cz','cx'}, dimensions={0} | all-to-all | bytes 4194304 | tf_op jit(solution)/shard_map/all_to_all | solution.py:49
  65.9 0.5 broadcast_in_dim.18
  66.5 0.0 copy-start.5
  66.5 9.5 %all_to_all.31 = bf16[2,512,2048]{2,1,0:T(8,128)(2,1)S(1)} all-to-all(bf16[2,512,2048]{2,1,0:T(8,128)(2,1)S(1)} %broadcast_in_dim.18), channel_id=1, replica_groups=mesh['row'=8,'cz'=8,'cx'=2,'cc'=2] {'cc'}, dimensions={0} | all-to-all | bytes 8388608 | tf_op jit(solution)/shard_map/all_to_all | solution.py:49
  76.0 0.0 copy-start.3
  76.0 0.0 copy-done.5
  76.0 1.2 fusion.17
  77.1 0.2 copy.58
  77.3 0.0 copy-done
  77.3 0.0 copy-start.6
  77.3 1.2 fusion.20
  78.5 0.2 copy.57
  78.7 0.0 copy-done.3
  78.7 0.0 copy-done.6
  78.7 1.2 fusion.14
  79.8 0.2 copy.59
  80.0 0.2 pad_maximum_fusion.1
  80.2 37.1 %all_to_all.32 = bf16[8,128,1344]{1,2,0:T(8,128)(2,1)S(1)} all-to-all(bf16[8,128,1344]{1,2,0:T(8,128)(2,1)S(1)} %pad_maximum_fusion.1), channel_id=1, replica_groups=mesh['row'=8,'cz'=8,'cx'=2,'cc'=2] {'row'}, dimensions={0} | all-to-all | bytes 5505024 | tf_op jit(solution)/shard_map/all_to_all | solution.py:55
  117.3 0.4 convert_reduce_fusion
  117.7 0.1 multiply_convert_fusion.2
  117.9 0.4 broadcast_in_dim.19
  118.2 34.9 %all_to_all.33 = bf16[8,128,1344]{1,2,0:T(8,128)(2,1)S(1)} all-to-all(bf16[8,128,1344]{1,2,0:T(8,128)(2,1)S(1)} %broadcast_in_dim.19), channel_id=1, replica_groups=mesh['row'=8,'cz'=8,'cx'=2,'cc'=2] {'row'}, dimensions={0} | all-to-all | bytes 5505024 | tf_op jit(solution)/shard_map/all_to_all | solution.py:49
  153.2 0.4 copy_bitcast_fusion
  153.6 0.0 copy-start.1
  153.6 1.3 convolution_convert_fusion
  154.9 1.3 fusion.26
  156.2 0.0 copy-done.1
  156.2 1.3 add_convert_fusion.1
  157.5 0.4 pad_maximum_fusion
  157.9 9.7 %all_to_all.34 = bf16[2,512,2048]{2,1,0:T(8,128)(2,1)S(1)} all-to-all(bf16[2,512,2048]{2,1,0:T(8,128)(2,1)S(1)} %bitcast.30), channel_id=1, replica_groups=mesh['row'=8,'cz'=8,'cx'=2,'cc'=2] {'cc'}, dimensions={0} | all-to-all | bytes 8388608 | tf_op jit(solution)/shard_map/all_to_all | solution.py:55
  167.6 2.2 add_convert_fusion
  169.8 3.9 %all-to-all-start.5 = ((bf16[16,32,2048]{2,1,0:T(8,128)(2,1)}), bf16[16,32,2048]{2,1,0:T(8,128)(2,1)S(1)}, u32[]{:S(2)}, u32[]{:S(2)}) async-start(bf16[16,32,2048]{2,1,0:T(8,128)(2,1)} %bitcast.3), calls=%async_computation.5 | async-start | bytes 4194304 | tf_op jit(solution)/shard_map/all_to_all | solution.py:55
  173.7 0.0 copy-start.2
  173.7 0.0 copy-start.4
  173.7 4.1 %fusion.7 = bf16[448,1024]{1,0:T(8,128)(2,1)} fusion(bf16[1024,2048]{1,0:T(8,128)(2,1)} %bitcast.35, bf16[1024,1344]{0,1:T(8,128)(2,1)} %copy-done.1), kind=kOutput, calls=%fused_computation.13 | convolution fusion | flops 939982848 | bytes 3932160 | tf_op jit(solution)/shard_map/dot_general | solution.py:129
  177.8 0.0 copy-done.2
  177.8 0.0 copy-done.4
  177.8 2.1 convolution_convert_fusion.2
  179.9 2.0 convolution_convert_fusion.1
  181.9 42.1 %all-to-all-done.5 = bf16[16,32,2048]{2,1,0:T(8,128)(2,1)S(1)} async-done(((bf16[16,32,2048]{2,1,0:T(8,128)(2,1)}), bf16[16,32,2048]{2,1,0:T(8,128)(2,1)S(1)}, u32[]{:S(2)}, u32[]{:S(2)}) %all-to-all-start.5) | async-done | bytes 2097184 | tf_op jit(solution)/shard_map/all_to_all | solution.py:55
  224.0 0.3 convert_reduce_fusion.1
  224.3 0.7 fusion.30
  (6 shorter events, 0.1 us)
Async XLA Ops:
  0.6 76.7 %copy-start = (bf16[448,1024]{1,0:T(8,128)(2,1)S(1)}, bf16[448,1024]{1,0:T(8,128)(2,1)}, u32[]{:S(2)}) copy-start(bf16[448,1024]{1,0:T(8,128)(2,1)} %param.15) | copy-start | bytes 2752516
  66.5 9.5 %copy-start.5 = (bf16[1024,448]{0,1:T(8,128)(2,1)S(1)}, bf16[1024,448]{0,1:T(8,128)(2,1)}, u32[]{:S(2)}) copy-start(bf16[1024,448]{0,1:T(8,128)(2,1)} %param.14) | copy-start | bytes 2752516
  76.0 2.7 %copy-start.3 = (bf16[2,512,2048]{2,1,0:T(8,128)(2,1)}, bf16[2,512,2048]{2,1,0:T(8,128)(2,1)S(1)}, u32[]{:S(2)}) copy-start(bf16[2,512,2048]{2,1,0:T(8,128)(2,1)S(1)} %all_to_all.31) | copy-start | bytes 12582916
  77.3 1.4 copy-start.6
  153.6 2.6 %copy-start.1 = (bf16[1024,1344]{0,1:T(8,128)(2,1)}, bf16[1024,1344]{0,1:T(8,128)(2,1)S(1)}, u32[]{:S(2)}) copy-start(bf16[1024,1344]{0,1:T(8,128)(2,1)S(1)} %copy_bitcast_fusion) | copy-start | bytes 8257540
  169.8 54.2 %all-to-all-start.5 = ((bf16[16,32,2048]{2,1,0:T(8,128)(2,1)}), bf16[16,32,2048]{2,1,0:T(8,128)(2,1)S(1)}, u32[]{:S(2)}, u32[]{:S(2)}) async-start(bf16[16,32,2048]{2,1,0:T(8,128)(2,1)} %bitcast.3), calls=%async_computation.5 | async-start | bytes 4194304 | tf_op jit(solution)/shard_map/all_to_all | solution.py:55
  173.7 4.1 %copy-start.2 = (bf16[1024,1344]{0,1:T(8,128)(2,1)S(1)}, bf16[1024,1344]{0,1:T(8,128)(2,1)}, u32[]{:S(2)}) copy-start(bf16[1024,1344]{0,1:T(8,128)(2,1)} %copy-done.1) | copy-start | bytes 8257540
  173.7 4.1 %copy-start.4 = (bf16[2,512,2048]{2,1,0:T(8,128)(2,1)S(1)}, bf16[2,512,2048]{2,1,0:T(8,128)(2,1)}, u32[]{:S(2)}) copy-start(bf16[2,512,2048]{2,1,0:T(8,128)(2,1)} %copy-done.3) | copy-start | bytes 12582916

commit v11 on v10

--- a/solution.py
+++ b/solution.py
@@ -42,6 +42,10 @@
 
 def tokens_major(value):
     return with_layout_constraint(value, Layout((0, 1)))
+
+
+def swap_cores(value):
+    return lax.ppermute(value, CORE, [(0, 1), (1, 0)])
 
 
 def gather_by_exchange(part, axis, count):
@@ -92,9 +96,8 @@
     contract_last = (((1,), (1,)), ((), ()))
     contract_first = (((0,), (0,)), ((), ()))
     both = jnp.concatenate([masked, cot_valid], axis=1)
-    both_all = gather_by_exchange(
-        gather_by_exchange(both, CHIPS, lax.psum(1, CHIPS)), CORE, lax.psum(1, CORE)
-    )
+    both_own = gather_by_exchange(both, CHIPS, lax.psum(1, CHIPS))
+    both_all = jnp.concatenate([both_own, swap_cores(both_own)], axis=0)
     tokens_all = both_all[:, :feat_cols]
     cot_all = both_all[:, feat_cols:]
     sums = sum_by_exchange(
@@ -151,7 +154,11 @@
         ],
         axis=1,
     )
-    chip_sums = sum_by_exchange(tokens_major(out_partial), CORE, lax.psum(1, CORE))
+    out_partial = tokens_major(out_partial)
+    half = out_partial.shape[0] // 2
+    chip_sums = out_partial[:half].astype(jnp.float32) + swap_cores(out_partial[half:]).astype(
+        jnp.float32
+    )
     out_sums = sum_by_exchange(chip_sums.astype(jnp.bfloat16), CHIPS, lax.psum(1, CHIPS))
     output = out_sums[:, :feat_cols].astype(jnp.bfloat16)
     grad_masked = out_sums[:, feat_cols:]

time: 225 us -> 223 us (level)
  blocking collectives: 153 us -> 134 us
  waiting for transfers between devices: 42.1 us -> 50.1 us
  starting transfers between devices: 3.9 us -> 10.2 us
    all_to_all x2 -> x1, blocking collectives: 46.7 us -> 37.1 us  [sum_by_exchange(): got = lax.all_to_all(split, axis, 0, 0)]
    all_to_all x3 -> x2, blocking collectives: 107 us -> 97.2 us  [gather_by_exchange(): got = lax.all_to_all(spread, axis, 0, 0)]
    ppermute x0 -> x2, waiting for transfers between devices: none -> 7.57 us  [swap_cores(): return lax.ppermute(value, CORE, [(0, 1), (1, 0)])]
    ppermute x0 -> x2, starting transfers between devices: none -> 5.62 us  [swap_cores(): return lax.ppermute(value, CORE, [(0, 1), (1, 0)])]
  transfers between devices with their start and end apart: 1 -> 3, of which waited for: 1 -> 3; matrix products, arithmetic and copies ran while one was open for 4% -> 3% of each run, Pallas kernels for 0% -> 0%
where the time goes in v11:
time: 223 us; the launch traced here: 222 us
  blocking collectives  134 us (60%)
  waiting for transfers between devices  50.1 us (22%)
  matrix products  15.2 us (7%)
  starting transfers between devices  10.2 us (5%)
  other arithmetic  8.82 us (4%)
  local copies, waits for them, and re-layouts  2.96 us (1%)
    all_to_all x2, blocking collectives, gather_by_exchange(): got = lax.all_to_all(spread, axis, 0, 0)  97.2 us
    all_to_all x1, waiting for transfers between devices, sum_by_exchange(): got = lax.all_to_all(split, axis, 0, 0)  42.5 us
    all_to_all x1, blocking collectives, sum_by_exchange(): got = lax.all_to_all(split, axis, 0, 0)  37.1 us
    ppermute x2, waiting for transfers between devices, swap_cores(): return lax.ppermute(value, CORE, [(0, 1), (1, 0)])  7.57 us
    ppermute x2, starting transfers between devices, swap_cores(): return lax.ppermute(value, CORE, [(0, 1), (1, 0)])  5.62 us
    all_to_all x1, starting transfers between devices, sum_by_exchange(): got = lax.all_to_all(split, axis, 0, 0)  4.62 us
  transfers between devices with their start and end apart: 3, of which 3 were waited for; matrix products, arithmetic and copies ran while one was open for 3% of the time, Pallas kernels for 0%

profile of v11, /device:TPU:1, one launch (start us, length us, event | category | flops | bytes accessed | tf_op | source)
XLA Modules:
  0.0 222.5 jit_solution(4157218757246814632)
XLA Ops:
  0.6 0.0 copy-start
  0.7 0.9 convert_reduce_fusion.3
  1.6 0.8 select_reduce_fusion.2
  2.4 1.0 broadcast_select_fusion
  3.4 0.2 broadcast_in_dim.12
  3.7 62.3 %all_to_all.20 = bf16[16,32,2048]{2,1,0:T(8,128)(2,1)S(1)} all-to-all(bf16[16,32,2048]{2,1,0:T(8,128)(2,1)S(1)} %broadcast_in_dim.12), channel_id=1, replica_groups=mesh['row'=8,'cz'=8,'cx'=2,'cc'=2] {'cz','cx'}, dimensions={0} | all-to-all | bytes 4194304 | tf_op jit(solution)/shard_map/all_to_all | solution.py:53
  65.9 2.6 %collective-permute-start = (bf16[512,2048]{1,0:T(8,128)(2,1)S(1)}, bf16[512,2048]{1,0:T(8,128)(2,1)S(1)}, u32[]{:S(2)}, u32[]{:S(2)}) collective-permute-start(bf16[512,2048]{1,0:T(8,128)(2,1)S(1)} %bitcast.32), channel_id=1, source_target_pairs={{0,1},{1,0},{2,3},{3,2},{4,5},{5,4},{6,7},{7,6},{8,9},{9,8},{10,11... | collective-permute-start | bytes 6291464 | tf_op jit(solution)/shard_map/ppermute | solution.py:48
  68.5 3.8 %collective-permute-done = bf16[512,2048]{1,0:T(8,128)(2,1)S(1)} collective-permute-done((bf16[512,2048]{1,0:T(8,128)(2,1)S(1)}, bf16[512,2048]{1,0:T(8,128)(2,1)S(1)}, u32[]{:S(2)}, u32[]{:S(2)}) %collective-permute-start) | collective-permute-done | bytes 2097184 | tf_op jit(solution)/shard_map/ppermute | solution.py:48
  72.3 0.0 copy-done
  72.3 0.0 copy-start.3
  72.3 1.2 fusion.4
  73.5 0.2 copy.57
  73.7 0.0 copy-done.3
  73.7 0.3 fusion.1
  74.0 0.9 copy-done.6
  74.9 1.2 fusion.3
  76.0 0.2 copy.58
  76.2 0.0 copy-done.4
  76.2 0.5 copy-done.7
  76.7 1.2 fusion.2
  77.9 0.2 copy.59
  78.1 0.2 pad_maximum_fusion
  78.2 37.1 %all_to_all.21 = bf16[8,128,1344]{1,2,0:T(8,128)(2,1)S(1)} all-to-all(bf16[8,128,1344]{1,2,0:T(8,128)(2,1)S(1)} %pad_maximum_fusion), channel_id=1, replica_groups=mesh['row'=8,'cz'=8,'cx'=2,'cc'=2] {'row'}, dimensions={0} | all-to-all | bytes 5505024 | tf_op jit(solution)/shard_map/all_to_all | solution.py:59
  115.3 0.4 convert_reduce_fusion
  115.7 0.1 multiply_convert_fusion.2
  115.9 0.4 broadcast_in_dim.13
  116.3 34.9 %all_to_all.22 = bf16[8,128,1344]{1,2,0:T(8,128)(2,1)S(1)} all-to-all(bf16[8,128,1344]{1,2,0:T(8,128)(2,1)S(1)} %broadcast_in_dim.13), channel_id=1, replica_groups=mesh['row'=8,'cz'=8,'cx'=2,'cc'=2] {'row'}, dimensions={0} | all-to-all | bytes 5505024 | tf_op jit(solution)/shard_map/all_to_all | solution.py:53
  151.2 0.4 copy_bitcast_fusion
  151.6 0.0 copy-start.1
  151.6 1.3 convolution_convert_fusion
  152.9 1.3 fusion.8
  154.2 0.0 copy-done.1
  154.2 1.4 add_convert_fusion.1
  155.6 0.2 pad_maximum_fusion.1
  155.8 3.0 %collective-permute-start.1 = (bf16[512,2048]{1,0:T(8,128)(2,1)S(1)}, bf16[512,2048]{1,0:T(8,128)(2,1)S(1)}, u32[]{:S(2)}, u32[]{:S(2)}) collective-permute-start(bf16[512,2048]{1,0:T(8,128)(2,1)S(1)} %pad_maximum_fusion.1), channel_id=1, source_target_pairs={{0,1},{1,0},{2,3},{3,2},{4,5},{5,4},{6,7},{7,6},{8,9},{9,8},{10,11... | collective-permute-start | bytes 6291464 | tf_op jit(solution)/shard_map/ppermute | solution.py:48
  158.9 3.8 %collective-permute-done.1 = bf16[512,2048]{1,0:T(8,128)(2,1)S(1)} collective-permute-done((bf16[512,2048]{1,0:T(8,128)(2,1)S(1)}, bf16[512,2048]{1,0:T(8,128)(2,1)S(1)}, u32[]{:S(2)}, u32[]{:S(2)}) %collective-permute-start.1) | collective-permute-done | bytes 2097184 | tf_op jit(solution)/shard_map/ppermute | solution.py:48
  162.6 2.2 %add_convert_fusion = bf16[512,2048]{1,0:T(8,128)(2,1)} fusion(bf16[512,2048]{1,0:T(8,128)(2,1)S(1)} %collective-permute-done.1, bf16[1024,1024]{1,0:T(8,128)(2,1)S(1)} %convolution_convert_fusion, bf16[1024,1024]{1,0:T(8,128)(2,1)S(1)} %add_convert_fusion.1), kind=kLoop, calls=%fused_computation.6 | loop fusion | flops 7340032 | bytes 8388608 | tf_op jit(solution)/shard_map/convert_element_type | solution.py:162
  164.9 4.6 %all-to-all-start.3 = ((bf16[16,32,2048]{2,1,0:T(8,128)(2,1)}), bf16[16,32,2048]{2,1,0:T(8,128)(2,1)}, u32[]{:S(2)}, u32[]{:S(2)}) async-start(bf16[16,32,2048]{2,1,0:T(8,128)(2,1)} %bitcast.36), calls=%async_computation.3 | async-start | bytes 4194304 | tf_op jit(solution)/shard_map/all_to_all | solution.py:59
  169.5 0.0 copy-start.2
  169.5 0.0 copy-start.5
  169.5 3.7 %convolution_convert_fusion.3 = bf16[448,1024]{1,0:T(8,128)(2,1)} fusion(bf16[1024,1344]{0,1:T(8,128)(2,1)} %copy-done.1, bf16[512,2048]{1,0:T(8,128)(2,1)} %copy-done.3, bf16[512,2048]{1,0:T(8,128)(2,1)S(1)} %bitcast.35), kind=kOutput, calls=%fused_computation.17 | convolution fusion | flops 944177152 | bytes 6029312 | tf_op jit(solution)/shard_map/dot_general | solution.py:132
  173.2 0.0 copy-done.2
  173.2 0.0 copy-done.5
  173.2 2.0 convolution_convert_fusion.2
  175.3 2.0 convolution_convert_fusion.1
  177.3 42.5 %all-to-all-done.3 = bf16[16,32,2048]{2,1,0:T(8,128)(2,1)} async-done(((bf16[16,32,2048]{2,1,0:T(8,128)(2,1)}), bf16[16,32,2048]{2,1,0:T(8,128)(2,1)}, u32[]{:S(2)}, u32[]{:S(2)}) %all-to-all-start.3) | async-done | bytes 2097184 | tf_op jit(solution)/shard_map/all_to_all | solution.py:59
  219.8 1.9 convert_reduce_fusion.1
  221.7 0.7 fusion.12
  (9 shorter events, 0.1 us)
Async XLA Ops:
  0.6 71.7 %copy-start = (bf16[448,1024]{1,0:T(8,128)(2,1)S(1)}, bf16[448,1024]{1,0:T(8,128)(2,1)}, u32[]{:S(2)}) copy-start(bf16[448,1024]{1,0:T(8,128)(2,1)} %param.15) | copy-start | bytes 2752516
  65.9 6.4 %collective-permute-start = (bf16[512,2048]{1,0:T(8,128)(2,1)S(1)}, bf16[512,2048]{1,0:T(8,128)(2,1)S(1)}, u32[]{:S(2)}, u32[]{:S(2)}) collective-permute-start(bf16[512,2048]{1,0:T(8,128)(2,1)S(1)} %bitcast.32), channel_id=1, source_target_pairs={{0,1},{1,0},{2,3},{3,2},{4,5},{5,4},{6,7},{7,6},{8,9},{9,8},{10,11... | collective-permute-start | bytes 6291464 | tf_op jit(solution)/shard_map/ppermute | solution.py:48
  72.3 1.4 copy-start.3
  73.7 1.2 copy-start.6
  74.9 1.3 copy-start.4
  74.9 1.8 copy-start.7
  151.6 2.6 %copy-start.1 = (bf16[1024,1344]{0,1:T(8,128)(2,1)}, bf16[1024,1344]{0,1:T(8,128)(2,1)S(1)}, u32[]{:S(2)}) copy-start(bf16[1024,1344]{0,1:T(8,128)(2,1)S(1)} %copy_bitcast_fusion) | copy-start | bytes 8257540
  155.8 6.8 %collective-permute-start.1 = (bf16[512,2048]{1,0:T(8,128)(2,1)S(1)}, bf16[512,2048]{1,0:T(8,128)(2,1)S(1)}, u32[]{:S(2)}, u32[]{:S(2)}) collective-permute-start(bf16[512,2048]{1,0:T(8,128)(2,1)S(1)} %pad_maximum_fusion.1), channel_id=1, source_target_pairs={{0,1},{1,0},{2,3},{3,2},{4,5},{5,4},{6,7},{7,6},{8,9},{9,8},{10,11... | collective-permute-start | bytes 6291464 | tf_op jit(solution)/shard_map/ppermute | solution.py:48
  164.9 54.9 %all-to-all-start.3 = ((bf16[16,32,2048]{2,1,0:T(8,128)(2,1)}), bf16[16,32,2048]{2,1,0:T(8,128)(2,1)}, u32[]{:S(2)}, u32[]{:S(2)}) async-start(bf16[16,32,2048]{2,1,0:T(8,128)(2,1)} %bitcast.36), calls=%async_computation.3 | async-start | bytes 4194304 | tf_op jit(solution)/shard_map/all_to_all | solution.py:59
  169.5 3.7 %copy-start.2 = (bf16[1024,1344]{0,1:T(8,128)(2,1)S(1)}, bf16[1024,1344]{0,1:T(8,128)(2,1)}, u32[]{:S(2)}) copy-start(bf16[1024,1344]{0,1:T(8,128)(2,1)} %copy-done.1) | copy-start | bytes 8257540
  169.5 3.7 %copy-start.5 = (bf16[1024,1024]{1,0:T(8,128)(2,1)S(1)}, bf16[1024,1024]{1,0:T(8,128)(2,1)}, u32[]{:S(2)}) copy-start(bf16[1024,1024]{1,0:T(8,128)(2,1)} %copy-done.4) | copy-start | bytes 6291460

commit v12 on v11

--- a/solution.py
+++ b/solution.py
@@ -97,20 +97,25 @@
     contract_first = (((0,), (0,)), ((), ()))
     both = jnp.concatenate([masked, cot_valid], axis=1)
     both_own = gather_by_exchange(both, CHIPS, lax.psum(1, CHIPS))
-    both_all = jnp.concatenate([both_own, swap_cores(both_own)], axis=0)
+    both_other = swap_cores(both_own)
+    both_all = jnp.concatenate([both_own, both_other], axis=0)
     tokens_all = both_all[:, :feat_cols]
     cot_all = both_all[:, feat_cols:]
-    sums = sum_by_exchange(
-        jnp.concatenate(
+
+    def row_partial(rows):
+        return jnp.concatenate(
             [
-                jnp.dot(tokens_all, gate_weight, preferred_element_type=jnp.float32),
-                jnp.dot(tokens_all, up_weight, preferred_element_type=jnp.float32),
+                jnp.dot(rows[:, :feat_cols], gate_weight, preferred_element_type=jnp.float32),
+                jnp.dot(rows[:, :feat_cols], up_weight, preferred_element_type=jnp.float32),
                 lax.dot_general(
-                    cot_all, down_weight, contract_last, preferred_element_type=jnp.float32
+                    rows[:, feat_cols:], down_weight, contract_last, preferred_element_type=jnp.float32
                 ),
             ],
             axis=1,
-        ).astype(jnp.bfloat16),
+        ).astype(jnp.bfloat16)
+
+    sums = sum_by_exchange(
+        jnp.concatenate([row_partial(both_own), row_partial(both_other)], axis=0),
         "row",
         lax.psum(1, "row"),
     )
@@ -138,27 +143,35 @@
     grad_up = lax.dot_general(
         tokens_all, dup_all, contract_first, preferred_element_type=jnp.float32
     ).astype(jnp.bfloat16)
-    out_partial = jnp.concatenate(
-        [
-            jnp.dot(hidden_all, down_weight, preferred_element_type=jnp.float32).astype(
-                jnp.bfloat16
-            ),
-            (
-                lax.dot_general(
-                    dgate_all, gate_weight, contract_last, preferred_element_type=jnp.float32
-                )
-                + lax.dot_general(
-                    dup_all, up_weight, contract_last, preferred_element_type=jnp.float32
-                )
-            ).astype(jnp.bfloat16),
-        ],
-        axis=1,
-    )
-    out_partial = tokens_major(out_partial)
-    half = out_partial.shape[0] // 2
-    chip_sums = out_partial[:half].astype(jnp.float32) + swap_cores(out_partial[half:]).astype(
-        jnp.float32
-    )
+    def col_partial(rows):
+        return tokens_major(
+            jnp.concatenate(
+                [
+                    jnp.dot(
+                        acts_all[rows, :hidden_cols], down_weight, preferred_element_type=jnp.float32
+                    ).astype(jnp.bfloat16),
+                    (
+                        lax.dot_general(
+                            acts_all[rows, hidden_cols : 2 * hidden_cols],
+                            gate_weight,
+                            contract_last,
+                            preferred_element_type=jnp.float32,
+                        )
+                        + lax.dot_general(
+                            acts_all[rows, 2 * hidden_cols :],
+                            up_weight,
+                            contract_last,
+                            preferred_element_type=jnp.float32,
+                        )
+                    ).astype(jnp.bfloat16),
+                ],
+                axis=1,
+            )
+        )
+
+    half = acts_all.shape[0] // 2
+    sent = swap_cores(col_partial(slice(half, None)))
+    chip_sums = col_partial(slice(0, half)).astype(jnp.float32) + sent.astype(jnp.float32)
     out_sums = sum_by_exchange(chip_sums.astype(jnp.bfloat16), CHIPS, lax.psum(1, CHIPS))
     output = out_sums[:, :feat_cols].astype(jnp.bfloat16)
     grad_masked = out_sums[:, feat_cols:]

time: 223 us -> 225 us (level)
  other arithmetic: 8.82 us -> 16.9 us
  waiting for transfers between devices: 50.1 us -> 45.6 us
    reshape x0 -> x1, other arithmetic: none -> 10.2 us  [sum_by_exchange(): partial.reshape((count, partial.shape[0] // count) + partial.shape[1:])]
    ppermute x2, waiting for transfers between devices: 7.57 us -> 3.27 us  [swap_cores(): return lax.ppermute(value, CORE, [(0, 1), (1, 0)])]
    dot_general x6 -> x12, matrix products: 7.46 us -> 8.45 us  [the longest x2 1.48 us: col_partial(): lax.dot_general(acts_all[rows, 2 * hidden_cols:], up_weight, contract_las...]
  transfers between devices with their start and end apart: 3 -> 3, of which waited for: 3 -> 3; matrix products, arithmetic and copies ran while one was open for 3% -> 5% of each run, Pallas kernels for 0% -> 0%
where the time goes in v12:
time: 225 us
  blocking collectives  134 us (60%)
  waiting for transfers between devices  45.6 us (20%)
  other arithmetic  16.9 us (8%)
  matrix products  16.6 us (7%)
  starting transfers between devices  9.33 us (4%)
    all_to_all x2, blocking collectives, gather_by_exchange(): got = lax.all_to_all(spread, axis, 0, 0)  97.3 us
    all_to_all x1, waiting for transfers between devices, sum_by_exchange(): got = lax.all_to_all(split, axis, 0, 0)  42.3 us
    all_to_all x1, blocking collectives, sum_by_exchange(): got = lax.all_to_all(split, axis, 0, 0)  37.1 us
    reshape x1, other arithmetic, sum_by_exchange(): partial.reshape((count, partial.shape[0] // count) + partial.shape[1:])  10.2 us
    ppermute x2, starting transfers between devices, swap_cores(): return lax.ppermute(value, CORE, [(0, 1), (1, 0)])  5.61 us
  transfers between devices with their start and end apart: 3, of which 3 were waited for; matrix products, arithmetic and copies ran while one was open for 5% of the time, Pallas kernels for 0%

profile of v12, /device:TPU:1, one launch (start us, length us, event | category | flops | bytes accessed | tf_op | source)
XLA Modules:
  0.0 224.7 jit_solution(16217627318641338450)
XLA Ops:
  0.6 0.0 copy-start
  0.7 0.9 convert_reduce_fusion.3
  1.6 0.8 select_reduce_fusion.2
  2.4 1.0 broadcast_select_fusion
  3.4 0.0 copy-start.4
  3.5 0.2 broadcast_in_dim.12
  3.7 62.4 %all_to_all.20 = bf16[16,32,2048]{2,1,0:T(8,128)(2,1)S(1)} all-to-all(bf16[16,32,2048]{2,1,0:T(8,128)(2,1)S(1)} %broadcast_in_dim.12), channel_id=1, replica_groups=mesh['row'=8,'cz'=8,'cx'=2,'cc'=2] {'cz','cx'}, dimensions={0} | all-to-all | bytes 4194304 | tf_op jit(solution)/shard_map/all_to_all | solution.py:53
  66.1 2.6 %collective-permute-start = (bf16[512,2048]{1,0:T(8,128)(2,1)S(1)}, bf16[512,2048]{1,0:T(8,128)(2,1)S(1)}, u32[]{:S(2)}, u32[]{:S(2)}) collective-permute-start(bf16[512,2048]{1,0:T(8,128)(2,1)S(1)} %bitcast.24), channel_id=1, source_target_pairs={{0,1},{1,0},{2,3},{3,2},{4,5},{5,4},{6,7},{7,6},{8,9},{9,8},{10,11... | collective-permute-start | bytes 6291464 | tf_op jit(solution)/shard_map/ppermute | solution.py:48
  68.7 0.0 copy-done.4
  68.7 0.7 convolution_convert_fusion.8
  69.4 0.0 copy-done
  69.4 0.7 convolution_convert_fusion.7
  70.1 0.0 copy-done.5
  70.1 0.0 copy-done.3
  70.1 0.7 convolution_convert_fusion.9
  70.8 1.7 collective-permute-done
  72.5 0.7 convolution_convert_fusion.5
  73.2 0.7 convolution_convert_fusion.4
  73.8 0.0 copy-done.7
  73.9 0.7 convolution_convert_fusion.6
  74.5 10.2 %copy_bitcast_fusion.1 = bf16[8,128,1344]{1,2,0:T(8,128)(2,1)S(1)} fusion(bf16[512,448]{0,1:T(8,128)(2,1)S(1)} %convolution_convert_fusion.4, bf16[512,448]{0,1:T(8,128)(2,1)S(1)} %convolution_convert_fusion.5, bf16[512,448]{0,1:T(8,128)(2,1)S(1)} %convolution_convert_fusion.6, bf16[512,448]{0,1:T(8,128)(2,1)S(1)} %convolution_convert_fusion.7, ...), kind=kLoop, calls=%fused_computation.6 | loop fusion | flops 16515072 | bytes 5505024 | tf_op jit(solution)/shard_map/reshape | solution.py:58
  84.7 37.1 %all_to_all.21 = bf16[8,128,1344]{1,2,0:T(8,128)(2,1)S(1)} all-to-all(bf16[8,128,1344]{1,2,0:T(8,128)(2,1)S(1)} %copy_bitcast_fusion.1), channel_id=1, replica_groups=mesh['row'=8,'cz'=8,'cx'=2,'cc'=2] {'row'}, dimensions={0} | all-to-all | bytes 5505024 | tf_op jit(solution)/shard_map/all_to_all | solution.py:59
  121.8 0.4 convert_reduce_fusion
  122.2 0.1 multiply_convert_fusion.2
  122.4 0.4 broadcast_in_dim.13
  122.7 34.9 %all_to_all.22 = bf16[8,128,1344]{1,2,0:T(8,128)(2,1)S(1)} all-to-all(bf16[8,128,1344]{1,2,0:T(8,128)(2,1)S(1)} %broadcast_in_dim.13), channel_id=1, replica_groups=mesh['row'=8,'cz'=8,'cx'=2,'cc'=2] {'row'}, dimensions={0} | all-to-all | bytes 5505024 | tf_op jit(solution)/shard_map/all_to_all | solution.py:53
  157.7 0.4 copy_bitcast_fusion
  158.1 0.0 copy-start.1
  158.1 0.7 convolution_convert_fusion
  158.8 0.7 fusion.14
  159.6 0.7 add_convert_fusion.1
  160.3 0.2 pad_maximum_fusion.2
  160.5 3.0 %collective-permute-start.1 = (bf16[512,2048]{1,0:T(8,128)(2,1)S(1)}, bf16[512,2048]{1,0:T(8,128)(2,1)S(1)}, u32[]{:S(2)}, u32[]{:S(2)}) collective-permute-start(bf16[512,2048]{1,0:T(8,128)(2,1)S(1)} %pad_maximum_fusion.2), channel_id=1, source_target_pairs={{0,1},{1,0},{2,3},{3,2},{4,5},{5,4},{6,7},{7,6},{8,9},{9,8},{10,11... | collective-permute-start | bytes 6291464 | tf_op jit(solution)/shard_map/ppermute | solution.py:48
  163.5 0.7 convolution_convert_fusion.1
  164.2 0.7 fusion.18
  165.0 0.0 copy-done.1
  165.0 0.7 add_convert_fusion.2
  165.7 1.5 collective-permute-done.1
  167.3 2.2 add_convert_fusion
  169.5 3.7 %all-to-all-start.3 = ((bf16[16,32,2048]{2,1,0:T(8,128)(2,1)}), bf16[16,32,2048]{2,1,0:T(8,128)(2,1)S(1)}, u32[]{:S(2)}, u32[]{:S(2)}) async-start(bf16[16,32,2048]{2,1,0:T(8,128)(2,1)} %bitcast.1), calls=%async_computation.3 | async-start | bytes 4194304 | tf_op jit(solution)/shard_map/all_to_all | solution.py:59
  173.2 0.0 copy-start.2
  173.2 4.0 %fusion.3 = bf16[448,1024]{1,0:T(8,128)(2,1)} fusion(bf16[512,2048]{1,0:T(8,128)(2,1)} %copy-done.7, bf16[512,2048]{1,0:T(8,128)(2,1)} %bitcast.28, bf16[1024,1344]{0,1:T(8,128)(2,1)} %copy-done.1), kind=kOutput, calls=%fused_computation.17 | convolution fusion | flops 944177152 | bytes 6029312 | tf_op jit(solution)/shard_map/dot_general | solution.py:137
  177.2 0.0 copy-done.6
  177.3 2.0 convolution_convert_fusion.2
  179.3 2.0 convolution_convert_fusion.3
  181.3 42.3 %all-to-all-done.3 = bf16[16,32,2048]{2,1,0:T(8,128)(2,1)S(1)} async-done(((bf16[16,32,2048]{2,1,0:T(8,128)(2,1)}), bf16[16,32,2048]{2,1,0:T(8,128)(2,1)S(1)}, u32[]{:S(2)}, u32[]{:S(2)}) %all-to-all-start.3) | async-done | bytes 2097184 | tf_op jit(solution)/shard_map/all_to_all | solution.py:59
  223.7 0.3 convert_reduce_fusion.1
  224.0 0.7 fusion.21
  (13 shorter events, 0.1 us)
Async XLA Ops:
  0.6 68.7 %copy-start = (bf16[448,1024]{1,0:T(8,128)(2,1)S(1)}, bf16[448,1024]{1,0:T(8,128)(2,1)}, u32[]{:S(2)}) copy-start(bf16[448,1024]{1,0:T(8,128)(2,1)} %param.15) | copy-start | bytes 2752516
  3.4 65.2 %copy-start.4 = (bf16[1024,448]{0,1:T(8,128)(2,1)S(1)}, bf16[1024,448]{0,1:T(8,128)(2,1)}, u32[]{:S(2)}) copy-start(bf16[1024,448]{0,1:T(8,128)(2,1)} %param.14) | copy-start | bytes 2752516
  66.1 4.0 %copy-start.5 = (bf16[16,32,2048]{2,1,0:T(8,128)(2,1)}, bf16[16,32,2048]{2,1,0:T(8,128)(2,1)S(1)}, u32[]{:S(2)}) copy-start(bf16[16,32,2048]{2,1,0:T(8,128)(2,1)S(1)} %all_to_all.20) | copy-start | bytes 6291460
  66.1 4.0 %copy-start.3 = (bf16[1024,448]{0,1:T(8,128)(2,1)S(1)}, bf16[1024,448]{0,1:T(8,128)(2,1)}, u32[]{:S(2)}) copy-start(bf16[1024,448]{0,1:T(8,128)(2,1)} %param.13) | copy-start | bytes 2752516
  66.1 6.4 %collective-permute-start = (bf16[512,2048]{1,0:T(8,128)(2,1)S(1)}, bf16[512,2048]{1,0:T(8,128)(2,1)S(1)}, u32[]{:S(2)}, u32[]{:S(2)}) collective-permute-start(bf16[512,2048]{1,0:T(8,128)(2,1)S(1)} %bitcast.24), channel_id=1, source_target_pairs={{0,1},{1,0},{2,3},{3,2},{4,5},{5,4},{6,7},{7,6},{8,9},{9,8},{10,11... | collective-permute-start | bytes 6291464 | tf_op jit(solution)/shard_map/ppermute | solution.py:48
  72.5 1.4 copy-start.7
  158.1 6.9 %copy-start.1 = (bf16[1024,1344]{0,1:T(8,128)(2,1)}, bf16[1024,1344]{0,1:T(8,128)(2,1)S(1)}, u32[]{:S(2)}) copy-start(bf16[1024,1344]{0,1:T(8,128)(2,1)S(1)} %copy_bitcast_fusion) | copy-start | bytes 8257540
  160.5 6.8 %collective-permute-start.1 = (bf16[512,2048]{1,0:T(8,128)(2,1)S(1)}, bf16[512,2048]{1,0:T(8,128)(2,1)S(1)}, u32[]{:S(2)}, u32[]{:S(2)}) collective-permute-start(bf16[512,2048]{1,0:T(8,128)(2,1)S(1)} %pad_maximum_fusion.2), channel_id=1, source_target_pairs={{0,1},{1,0},{2,3},{3,2},{4,5},{5,4},{6,7},{7,6},{8,9},{9,8},{10,11... | collective-permute-start | bytes 6291464 | tf_op jit(solution)/shard_map/ppermute | solution.py:48
  169.5 54.2 %all-to-all-start.3 = ((bf16[16,32,2048]{2,1,0:T(8,128)(2,1)}), bf16[16,32,2048]{2,1,0:T(8,128)(2,1)S(1)}, u32[]{:S(2)}, u32[]{:S(2)}) async-start(bf16[16,32,2048]{2,1,0:T(8,128)(2,1)} %bitcast.1), calls=%async_computation.3 | async-start | bytes 4194304 | tf_op jit(solution)/shard_map/all_to_all | solution.py:59
  173.2 4.0 %copy-start.2 = (bf16[1024,1344]{0,1:T(8,128)(2,1)S(1)}, bf16[1024,1344]{0,1:T(8,128)(2,1)}, u32[]{:S(2)}) copy-start(bf16[1024,1344]{0,1:T(8,128)(2,1)} %copy-done.1) | copy-start | bytes 8257540
  173.2 4.0 %copy-start.6 = (bf16[16,32,2048]{2,1,0:T(8,128)(2,1)S(1)}, bf16[16,32,2048]{2,1,0:T(8,128)(2,1)}, u32[]{:S(2)}) copy-start(bf16[16,32,2048]{2,1,0:T(8,128)(2,1)} %copy-done.5) | copy-start | bytes 6291460
  173.2 4.0 %copy-start.8 = (bf16[512,2048]{1,0:T(8,128)(2,1)S(1)}, bf16[512,2048]{1,0:T(8,128)(2,1)}, u32[]{:S(2)}) copy-start(bf16[512,2048]{1,0:T(8,128)(2,1)} %copy-done.7) | copy-start | bytes 6291460

commit v13 on v11

--- a/solution.py
+++ b/solution.py
@@ -57,6 +57,9 @@
 def sum_by_exchange(partial, axis, count):
     split = partial.reshape((count, partial.shape[0] // count) + partial.shape[1:])
     got = lax.all_to_all(split, axis, 0, 0)
+    if count == 16:
+        grouped = got.astype(jnp.float32).reshape((4, 4) + got.shape[1:])
+        return jnp.sum(lax.optimization_barrier(jnp.sum(grouped, axis=1)), axis=0)
     if count > 2:
         return jnp.sum(got.astype(jnp.float32), axis=0)
     return got[0].astype(jnp.float32) + got[1].astype(jnp.float32)

time: 223 us -> 223 us (level)
  no operation moved by 1% of the time
where the time goes in v13:
time: 223 us
  blocking collectives  134 us (60%)
  waiting for transfers between devices  50.1 us (22%)
  matrix products  15.2 us (7%)
  starting transfers between devices  10.2 us (5%)
  other arithmetic  9.08 us (4%)
  local copies, waits for them, and re-layouts  2.96 us (1%)
    all_to_all x2, blocking collectives, gather_by_exchange(): got = lax.all_to_all(spread, axis, 0, 0)  97.2 us
    all_to_all x1, waiting for transfers between devices, sum_by_exchange(): got = lax.all_to_all(split, axis, 0, 0)  42.5 us
    all_to_all x1, blocking collectives, sum_by_exchange(): got = lax.all_to_all(split, axis, 0, 0)  37.1 us
    ppermute x2, waiting for transfers between devices, swap_cores(): return lax.ppermute(value, CORE, [(0, 1), (1, 0)])  7.57 us
    ppermute x2, starting transfers between devices, swap_cores(): return lax.ppermute(value, CORE, [(0, 1), (1, 0)])  5.62 us
    all_to_all x1, starting transfers between devices, sum_by_exchange(): got = lax.all_to_all(split, axis, 0, 0)  4.62 us
  transfers between devices with their start and end apart: 3, of which 3 were waited for; matrix products, arithmetic and copies ran while one was open for 3% of the time, Pallas kernels for 0%

profile of v13, /device:TPU:1, one launch (start us, length us, event | category | flops | bytes accessed | tf_op | source)
XLA Modules:
  0.0 222.7 jit_solution(4109265765243444948)
XLA Ops:
  0.6 0.0 copy-start
  0.7 0.9 convert_reduce_fusion.3
  1.6 0.8 select_reduce_fusion.2
  2.4 1.0 broadcast_select_fusion
  3.4 0.2 broadcast_in_dim.12
  3.7 62.3 %all_to_all.20 = bf16[16,32,2048]{2,1,0:T(8,128)(2,1)S(1)} all-to-all(bf16[16,32,2048]{2,1,0:T(8,128)(2,1)S(1)} %broadcast_in_dim.12), channel_id=1, replica_groups=mesh['row'=8,'cz'=8,'cx'=2,'cc'=2] {'cz','cx'}, dimensions={0} | all-to-all | bytes 4194304 | tf_op jit(solution)/shard_map/all_to_all | solution.py:53
  65.9 2.6 %collective-permute-start = (bf16[512,2048]{1,0:T(8,128)(2,1)S(1)}, bf16[512,2048]{1,0:T(8,128)(2,1)S(1)}, u32[]{:S(2)}, u32[]{:S(2)}) collective-permute-start(bf16[512,2048]{1,0:T(8,128)(2,1)S(1)} %bitcast.35), channel_id=1, source_target_pairs={{0,1},{1,0},{2,3},{3,2},{4,5},{5,4},{6,7},{7,6},{8,9},{9,8},{10,11... | collective-permute-start | bytes 6291464 | tf_op jit(solution)/shard_map/ppermute | solution.py:48
  68.5 3.8 %collective-permute-done = bf16[512,2048]{1,0:T(8,128)(2,1)S(1)} collective-permute-done((bf16[512,2048]{1,0:T(8,128)(2,1)S(1)}, bf16[512,2048]{1,0:T(8,128)(2,1)S(1)}, u32[]{:S(2)}, u32[]{:S(2)}) %collective-permute-start) | collective-permute-done | bytes 2097184 | tf_op jit(solution)/shard_map/ppermute | solution.py:48
  72.3 0.0 copy-done
  72.3 1.2 fusion.4
  73.5 0.2 copy.57
  73.7 0.0 copy-done.3
  73.7 0.3 fusion.1
  74.0 0.9 copy-done.6
  74.9 1.2 fusion.3
  76.0 0.2 copy.58
  76.2 0.0 copy-done.4
  76.2 0.5 copy-done.7
  76.7 1.2 fusion.2
  77.9 0.2 copy.59
  78.1 0.2 pad_maximum_fusion
  78.2 37.1 %all_to_all.21 = bf16[8,128,1344]{1,2,0:T(8,128)(2,1)S(1)} all-to-all(bf16[8,128,1344]{1,2,0:T(8,128)(2,1)S(1)} %pad_maximum_fusion), channel_id=1, replica_groups=mesh['row'=8,'cz'=8,'cx'=2,'cc'=2] {'row'}, dimensions={0} | all-to-all | bytes 5505024 | tf_op jit(solution)/shard_map/all_to_all | solution.py:59
  115.3 0.4 convert_reduce_fusion
  115.7 0.1 multiply_convert_fusion.2
  115.9 0.4 broadcast_in_dim.13
  116.3 34.9 %all_to_all.22 = bf16[8,128,1344]{1,2,0:T(8,128)(2,1)S(1)} all-to-all(bf16[8,128,1344]{1,2,0:T(8,128)(2,1)S(1)} %broadcast_in_dim.13), channel_id=1, replica_groups=mesh['row'=8,'cz'=8,'cx'=2,'cc'=2] {'row'}, dimensions={0} | all-to-all | bytes 5505024 | tf_op jit(solution)/shard_map/all_to_all | solution.py:53
  151.2 0.4 copy_bitcast_fusion
  151.6 0.0 copy-start.1
  151.6 1.3 convolution_convert_fusion
  152.9 1.3 fusion.8
  154.2 0.0 copy-done.1
  154.2 1.4 add_convert_fusion.1
  155.6 0.2 pad_maximum_fusion.1
  155.8 3.0 %collective-permute-start.1 = (bf16[512,2048]{1,0:T(8,128)(2,1)S(1)}, bf16[512,2048]{1,0:T(8,128)(2,1)S(1)}, u32[]{:S(2)}, u32[]{:S(2)}) collective-permute-start(bf16[512,2048]{1,0:T(8,128)(2,1)S(1)} %pad_maximum_fusion.1), channel_id=1, source_target_pairs={{0,1},{1,0},{2,3},{3,2},{4,5},{5,4},{6,7},{7,6},{8,9},{9,8},{10,11... | collective-permute-start | bytes 6291464 | tf_op jit(solution)/shard_map/ppermute | solution.py:48
  158.9 3.8 %collective-permute-done.1 = bf16[512,2048]{1,0:T(8,128)(2,1)S(1)} collective-permute-done((bf16[512,2048]{1,0:T(8,128)(2,1)S(1)}, bf16[512,2048]{1,0:T(8,128)(2,1)S(1)}, u32[]{:S(2)}, u32[]{:S(2)}) %collective-permute-start.1) | collective-permute-done | bytes 2097184 | tf_op jit(solution)/shard_map/ppermute | solution.py:48
  162.6 2.2 %add_convert_fusion = bf16[512,2048]{1,0:T(8,128)(2,1)} fusion(bf16[512,2048]{1,0:T(8,128)(2,1)S(1)} %collective-permute-done.1, bf16[1024,1024]{1,0:T(8,128)(2,1)S(1)} %convolution_convert_fusion, bf16[1024,1024]{1,0:T(8,128)(2,1)S(1)} %add_convert_fusion.1), kind=kLoop, calls=%fused_computation.6 | loop fusion | flops 7340032 | bytes 8388608 | tf_op jit(solution)/shard_map/convert_element_type | solution.py:165
  164.9 4.6 %all-to-all-start.3 = ((bf16[16,32,2048]{2,1,0:T(8,128)(2,1)}), bf16[16,32,2048]{2,1,0:T(8,128)(2,1)}, u32[]{:S(2)}, u32[]{:S(2)}) async-start(bf16[16,32,2048]{2,1,0:T(8,128)(2,1)} %bitcast.39), calls=%async_computation.3 | async-start | bytes 4194304 | tf_op jit(solution)/shard_map/all_to_all | solution.py:59
  169.5 0.0 copy-start.2
  169.5 0.0 copy-start.5
  169.5 3.7 %convolution_convert_fusion.3 = bf16[448,1024]{1,0:T(8,128)(2,1)} fusion(bf16[1024,1344]{0,1:T(8,128)(2,1)} %copy-done.1, bf16[512,2048]{1,0:T(8,128)(2,1)} %copy-done.3, bf16[512,2048]{1,0:T(8,128)(2,1)S(1)} %bitcast.38), kind=kOutput, calls=%fused_computation.17 | convolution fusion | flops 944177152 | bytes 6029312 | tf_op jit(solution)/shard_map/dot_general | solution.py:135
  173.2 0.0 copy-done.2
  173.2 0.0 copy-done.5
  173.2 2.0 convolution_convert_fusion.2
  175.3 2.0 convolution_convert_fusion.1
  177.3 42.5 %all-to-all-done.3 = bf16[16,32,2048]{2,1,0:T(8,128)(2,1)} async-done(((bf16[16,32,2048]{2,1,0:T(8,128)(2,1)}), bf16[16,32,2048]{2,1,0:T(8,128)(2,1)}, u32[]{:S(2)}, u32[]{:S(2)}) %all-to-all-start.3) | async-done | bytes 2097184 | tf_op jit(solution)/shard_map/all_to_all | solution.py:59
  219.8 2.1 convert_reduce_fusion.1
  221.9 0.1 reduce_sum.109
  222.0 0.7 fusion.12
  (10 shorter events, 0.1 us)
Async XLA Ops:
  0.6 71.7 %copy-start = (bf16[448,1024]{1,0:T(8,128)(2,1)S(1)}, bf16[448,1024]{1,0:T(8,128)(2,1)}, u32[]{:S(2)}) copy-start(bf16[448,1024]{1,0:T(8,128)(2,1)} %param.15) | copy-start | bytes 2752516
  65.9 6.4 %collective-permute-start = (bf16[512,2048]{1,0:T(8,128)(2,1)S(1)}, bf16[512,2048]{1,0:T(8,128)(2,1)S(1)}, u32[]{:S(2)}, u32[]{:S(2)}) collective-permute-start(bf16[512,2048]{1,0:T(8,128)(2,1)S(1)} %bitcast.35), channel_id=1, source_target_pairs={{0,1},{1,0},{2,3},{3,2},{4,5},{5,4},{6,7},{7,6},{8,9},{9,8},{10,11... | collective-permute-start | bytes 6291464 | tf_op jit(solution)/shard_map/ppermute | solution.py:48
  72.3 1.4 copy-start.3
  73.7 1.2 copy-start.6
  74.9 1.3 copy-start.4
  74.9 1.8 copy-start.7
  151.6 2.6 %copy-start.1 = (bf16[1024,1344]{0,1:T(8,128)(2,1)}, bf16[1024,1344]{0,1:T(8,128)(2,1)S(1)}, u32[]{:S(2)}) copy-start(bf16[1024,1344]{0,1:T(8,128)(2,1)S(1)} %copy_bitcast_fusion) | copy-start | bytes 8257540
  155.8 6.8 %collective-permute-start.1 = (bf16[512,2048]{1,0:T(8,128)(2,1)S(1)}, bf16[512,2048]{1,0:T(8,128)(2,1)S(1)}, u32[]{:S(2)}, u32[]{:S(2)}) collective-permute-start(bf16[512,2048]{1,0:T(8,128)(2,1)S(1)} %pad_maximum_fusion.1), channel_id=1, source_target_pairs={{0,1},{1,0},{2,3},{3,2},{4,5},{5,4},{6,7},{7,6},{8,9},{9,8},{10,11... | collective-permute-start | bytes 6291464 | tf_op jit(solution)/shard_map/ppermute | solution.py:48
  164.9 54.9 %all-to-all-start.3 = ((bf16[16,32,2048]{2,1,0:T(8,128)(2,1)}), bf16[16,32,2048]{2,1,0:T(8,128)(2,1)}, u32[]{:S(2)}, u32[]{:S(2)}) async-start(bf16[16,32,2048]{2,1,0:T(8,128)(2,1)} %bitcast.39), calls=%async_computation.3 | async-start | bytes 4194304 | tf_op jit(solution)/shard_map/all_to_all | solution.py:59
  169.5 3.7 %copy-start.2 = (bf16[1024,1344]{0,1:T(8,128)(2,1)S(1)}, bf16[1024,1344]{0,1:T(8,128)(2,1)}, u32[]{:S(2)}) copy-start(bf16[1024,1344]{0,1:T(8,128)(2,1)} %copy-done.1) | copy-start | bytes 8257540
  169.5 3.7 %copy-start.5 = (bf16[1024,1024]{1,0:T(8,128)(2,1)S(1)}, bf16[1024,1024]{1,0:T(8,128)(2,1)}, u32[]{:S(2)}) copy-start(bf16[1024,1024]{1,0:T(8,128)(2,1)} %copy-done.4) | copy-start | bytes 6291460

commit v14 on v12

--- a/solution.py
+++ b/solution.py
@@ -97,25 +97,20 @@
     contract_first = (((0,), (0,)), ((), ()))
     both = jnp.concatenate([masked, cot_valid], axis=1)
     both_own = gather_by_exchange(both, CHIPS, lax.psum(1, CHIPS))
-    both_other = swap_cores(both_own)
-    both_all = jnp.concatenate([both_own, both_other], axis=0)
+    both_all = jnp.concatenate([both_own, swap_cores(both_own)], axis=0)
     tokens_all = both_all[:, :feat_cols]
     cot_all = both_all[:, feat_cols:]
-
-    def row_partial(rows):
-        return jnp.concatenate(
+    sums = sum_by_exchange(
+        jnp.concatenate(
             [
-                jnp.dot(rows[:, :feat_cols], gate_weight, preferred_element_type=jnp.float32),
-                jnp.dot(rows[:, :feat_cols], up_weight, preferred_element_type=jnp.float32),
+                jnp.dot(tokens_all, gate_weight, preferred_element_type=jnp.float32),
+                jnp.dot(tokens_all, up_weight, preferred_element_type=jnp.float32),
                 lax.dot_general(
-                    rows[:, feat_cols:], down_weight, contract_last, preferred_element_type=jnp.float32
+                    cot_all, down_weight, contract_last, preferred_element_type=jnp.float32
                 ),
             ],
             axis=1,
-        ).astype(jnp.bfloat16)
-
-    sums = sum_by_exchange(
-        jnp.concatenate([row_partial(both_own), row_partial(both_other)], axis=0),
+        ).astype(jnp.bfloat16),
         "row",
         lax.psum(1, "row"),
     )

time: 225 us -> 221 us (0.982)
  other arithmetic: 16.9 us -> 8.79 us
    reshape x1 -> x0, other arithmetic: 10.2 us -> none  [sum_by_exchange(): partial.reshape((count, partial.shape[0] // count) + partial.shape[1:])]
where the time goes in v14:
time: 221 us
  blocking collectives  134 us (61%)
  waiting for transfers between devices  47.8 us (22%)
  matrix products  15.7 us (7%)
  starting transfers between devices  10.2 us (5%)
  other arithmetic  8.79 us (4%)
  local copies, waits for them, and re-layouts  2.96 us (1%)
    all_to_all x2, blocking collectives, gather_by_exchange(): got = lax.all_to_all(spread, axis, 0, 0)  97.2 us
    all_to_all x1, waiting for transfers between devices, sum_by_exchange(): got = lax.all_to_all(split, axis, 0, 0)  42.5 us
    all_to_all x1, blocking collectives, sum_by_exchange(): got = lax.all_to_all(split, axis, 0, 0)  37.1 us
    ppermute x2, starting transfers between devices, swap_cores(): return lax.ppermute(value, CORE, [(0, 1), (1, 0)])  5.62 us
    ppermute x2, waiting for transfers between devices, swap_cores(): return lax.ppermute(value, CORE, [(0, 1), (1, 0)])  5.27 us
    all_to_all x1, starting transfers between devices, sum_by_exchange(): got = lax.all_to_all(split, axis, 0, 0)  4.62 us
  transfers between devices with their start and end apart: 3, of which 3 were waited for; matrix products, arithmetic and copies ran while one was open for 5% of the time, Pallas kernels for 0%

profile of v14, /device:TPU:1, one launch (start us, length us, event | category | flops | bytes accessed | tf_op | source)
XLA Modules:
  0.0 220.6 jit_solution(4012357633672349552)
XLA Ops:
  0.6 0.0 copy-start
  0.7 0.9 convert_reduce_fusion.3
  1.6 0.8 select_reduce_fusion.2
  2.4 1.0 broadcast_select_fusion
  3.4 0.2 broadcast_in_dim.12
  3.7 62.3 %all_to_all.20 = bf16[16,32,2048]{2,1,0:T(8,128)(2,1)S(1)} all-to-all(bf16[16,32,2048]{2,1,0:T(8,128)(2,1)S(1)} %broadcast_in_dim.12), channel_id=1, replica_groups=mesh['row'=8,'cz'=8,'cx'=2,'cc'=2] {'cz','cx'}, dimensions={0} | all-to-all | bytes 4194304 | tf_op jit(solution)/shard_map/all_to_all | solution.py:53
  65.9 2.6 %collective-permute-start = (bf16[512,2048]{1,0:T(8,128)(2,1)S(1)}, bf16[512,2048]{1,0:T(8,128)(2,1)S(1)}, u32[]{:S(2)}, u32[]{:S(2)}) collective-permute-start(bf16[512,2048]{1,0:T(8,128)(2,1)S(1)} %bitcast.35), channel_id=1, source_target_pairs={{0,1},{1,0},{2,3},{3,2},{4,5},{5,4},{6,7},{7,6},{8,9},{9,8},{10,11... | collective-permute-start | bytes 6291464 | tf_op jit(solution)/shard_map/ppermute | solution.py:48
  68.5 3.8 %collective-permute-done = bf16[512,2048]{1,0:T(8,128)(2,1)S(1)} collective-permute-done((bf16[512,2048]{1,0:T(8,128)(2,1)S(1)}, bf16[512,2048]{1,0:T(8,128)(2,1)S(1)}, u32[]{:S(2)}, u32[]{:S(2)}) %collective-permute-start) | collective-permute-done | bytes 2097184 | tf_op jit(solution)/shard_map/ppermute | solution.py:48
  72.3 0.0 copy-done
  72.3 1.2 fusion.3
  73.5 0.2 copy.42
  73.7 0.0 copy-done.5
  73.7 0.3 fusion
  74.0 0.9 copy-done.4
  74.9 1.2 fusion.2
  76.0 0.2 copy.43
  76.2 0.0 copy-done.6
  76.2 0.5 copy-done.3
  76.7 1.2 fusion.1
  77.9 0.2 copy.44
  78.1 0.2 pad_maximum_fusion
  78.2 37.1 %all_to_all.21 = bf16[8,128,1344]{1,2,0:T(8,128)(2,1)S(1)} all-to-all(bf16[8,128,1344]{1,2,0:T(8,128)(2,1)S(1)} %pad_maximum_fusion), channel_id=1, replica_groups=mesh['row'=8,'cz'=8,'cx'=2,'cc'=2] {'row'}, dimensions={0} | all-to-all | bytes 5505024 | tf_op jit(solution)/shard_map/all_to_all | solution.py:59
  115.3 0.4 convert_reduce_fusion
  115.7 0.1 multiply_convert_fusion.2
  115.9 0.4 broadcast_in_dim.13
  116.3 34.9 %all_to_all.22 = bf16[8,128,1344]{1,2,0:T(8,128)(2,1)S(1)} all-to-all(bf16[8,128,1344]{1,2,0:T(8,128)(2,1)S(1)} %broadcast_in_dim.13), channel_id=1, replica_groups=mesh['row'=8,'cz'=8,'cx'=2,'cc'=2] {'row'}, dimensions={0} | all-to-all | bytes 5505024 | tf_op jit(solution)/shard_map/all_to_all | solution.py:53
  151.2 0.4 copy_bitcast_fusion
  151.6 0.0 copy-start.1
  151.6 0.7 convolution_convert_fusion
  152.3 0.7 fusion.8
  153.1 0.7 add_convert_fusion.1
  153.8 0.2 pad_maximum_fusion.2
  154.0 3.0 %collective-permute-start.1 = (bf16[512,2048]{1,0:T(8,128)(2,1)S(1)}, bf16[512,2048]{1,0:T(8,128)(2,1)S(1)}, u32[]{:S(2)}, u32[]{:S(2)}) collective-permute-start(bf16[512,2048]{1,0:T(8,128)(2,1)S(1)} %pad_maximum_fusion.2), channel_id=1, source_target_pairs={{0,1},{1,0},{2,3},{3,2},{4,5},{5,4},{6,7},{7,6},{8,9},{9,8},{10,11... | collective-permute-start | bytes 6291464 | tf_op jit(solution)/shard_map/ppermute | solution.py:48
  157.0 0.7 convolution_convert_fusion.1
  157.8 0.8 fusion.12
  158.5 0.0 copy-done.1
  158.5 0.8 add_convert_fusion.2
  159.3 1.5 collective-permute-done.1
  160.8 2.2 %add_convert_fusion = bf16[512,2048]{1,0:T(8,128)(2,1)} fusion(bf16[512,2048]{1,0:T(8,128)(2,1)S(1)} %collective-permute-done.1, bf16[512,1024]{1,0:T(8,128)(2,1)S(1)} %add_convert_fusion.2, bf16[512,1024]{1,0:T(8,128)(2,1)S(1)} %convolution_convert_fusion.1), kind=kLoop, calls=%fused_computation.4 | loop fusion | flops 7340032 | bytes 6291456 | tf_op jit(solution)/shard_map/convert_element_type | solution.py:170
  163.0 4.6 %all-to-all-start.3 = ((bf16[16,32,2048]{2,1,0:T(8,128)(2,1)}), bf16[16,32,2048]{2,1,0:T(8,128)(2,1)}, u32[]{:S(2)}, u32[]{:S(2)}) async-start(bf16[16,32,2048]{2,1,0:T(8,128)(2,1)} %bitcast.39), calls=%async_computation.3 | async-start | bytes 4194304 | tf_op jit(solution)/shard_map/all_to_all | solution.py:59
  167.7 0.0 copy-start.2
  167.7 0.0 copy-start.7
  167.7 3.7 %convolution_convert_fusion.4 = bf16[448,1024]{1,0:T(8,128)(2,1)} fusion(bf16[1024,1344]{0,1:T(8,128)(2,1)} %copy-done.1, bf16[512,2048]{1,0:T(8,128)(2,1)} %copy-done.5, bf16[512,2048]{1,0:T(8,128)(2,1)S(1)} %bitcast.38), kind=kOutput, calls=%fused_computation.16 | convolution fusion | flops 944177152 | bytes 6029312 | tf_op jit(solution)/shard_map/dot_general | solution.py:132
  171.4 2.0 convolution_convert_fusion.2
  173.4 2.0 convolution_convert_fusion.3
  175.5 42.5 %all-to-all-done.3 = bf16[16,32,2048]{2,1,0:T(8,128)(2,1)} async-done(((bf16[16,32,2048]{2,1,0:T(8,128)(2,1)}), bf16[16,32,2048]{2,1,0:T(8,128)(2,1)}, u32[]{:S(2)}, u32[]{:S(2)}) %all-to-all-start.3) | async-done | bytes 2097184 | tf_op jit(solution)/shard_map/all_to_all | solution.py:59
  218.0 1.9 convert_reduce_fusion.1
  219.9 0.7 fusion.15
  (12 shorter events, 0.1 us)
Async XLA Ops:
  0.6 71.7 %copy-start = (bf16[448,1024]{1,0:T(8,128)(2,1)S(1)}, bf16[448,1024]{1,0:T(8,128)(2,1)}, u32[]{:S(2)}) copy-start(bf16[448,1024]{1,0:T(8,128)(2,1)} %param.15) | copy-start | bytes 2752516
  65.9 6.4 %collective-permute-start = (bf16[512,2048]{1,0:T(8,128)(2,1)S(1)}, bf16[512,2048]{1,0:T(8,128)(2,1)S(1)}, u32[]{:S(2)}, u32[]{:S(2)}) collective-permute-start(bf16[512,2048]{1,0:T(8,128)(2,1)S(1)} %bitcast.35), channel_id=1, source_target_pairs={{0,1},{1,0},{2,3},{3,2},{4,5},{5,4},{6,7},{7,6},{8,9},{9,8},{10,11... | collective-permute-start | bytes 6291464 | tf_op jit(solution)/shard_map/ppermute | solution.py:48
  72.3 1.4 copy-start.5
  73.7 1.2 copy-start.4
  74.9 1.3 copy-start.6
  74.9 1.8 copy-start.3
  151.6 6.9 %copy-start.1 = (bf16[1024,1344]{0,1:T(8,128)(2,1)}, bf16[1024,1344]{0,1:T(8,128)(2,1)S(1)}, u32[]{:S(2)}) copy-start(bf16[1024,1344]{0,1:T(8,128)(2,1)S(1)} %copy_bitcast_fusion) | copy-start | bytes 8257540
  154.0 6.8 %collective-permute-start.1 = (bf16[512,2048]{1,0:T(8,128)(2,1)S(1)}, bf16[512,2048]{1,0:T(8,128)(2,1)S(1)}, u32[]{:S(2)}, u32[]{:S(2)}) collective-permute-start(bf16[512,2048]{1,0:T(8,128)(2,1)S(1)} %pad_maximum_fusion.2), channel_id=1, source_target_pairs={{0,1},{1,0},{2,3},{3,2},{4,5},{5,4},{6,7},{7,6},{8,9},{9,8},{10,11... | collective-permute-start | bytes 6291464 | tf_op jit(solution)/shard_map/ppermute | solution.py:48
  163.0 54.9 %all-to-all-start.3 = ((bf16[16,32,2048]{2,1,0:T(8,128)(2,1)}), bf16[16,32,2048]{2,1,0:T(8,128)(2,1)}, u32[]{:S(2)}, u32[]{:S(2)}) async-start(bf16[16,32,2048]{2,1,0:T(8,128)(2,1)} %bitcast.39), calls=%async_computation.3 | async-start | bytes 4194304 | tf_op jit(solution)/shard_map/all_to_all | solution.py:59
  167.7 3.7 %copy-start.2 = (bf16[1024,1344]{0,1:T(8,128)(2,1)S(1)}, bf16[1024,1344]{0,1:T(8,128)(2,1)}, u32[]{:S(2)}) copy-start(bf16[1024,1344]{0,1:T(8,128)(2,1)} %copy-done.1) | copy-start | bytes 8257540
  167.7 3.7 %copy-start.7 = (bf16[1024,1024]{1,0:T(8,128)(2,1)S(1)}, bf16[1024,1024]{1,0:T(8,128)(2,1)}, u32[]{:S(2)}) copy-start(bf16[1024,1024]{1,0:T(8,128)(2,1)} %copy-done.6) | copy-start | bytes 6291460
